TPU v7x, 1024 devices: a whole 4x8x16 slice. The times are simulated.
1024 devices in a mesh: tm: 32 (over x, y), ulysses: 32 (over z, core).
Axes of the slice: x: 4, y: 8, z: 16, core: 2. Of those that a mesh axis runs over, the one named last changes fastest.
Arguments:
- queries: bfloat16 [64, 64, 32, 1536], P('tm', None, 'ulysses'), may hold values from -24 to 24
- key_vectors: bfloat16 [64, 64, 32, 1536], P('tm', None, 'ulysses'), may hold values from -24 to 24
- value_vectors: bfloat16 [64, 64, 32, 1536], P('tm', None, 'ulysses'), may hold values from -6 to 6
- out_cotangent: bfloat16 [64, 64, 32, 1536], P('tm', None, 'ulysses'), may hold values from -6 to 6
- reach_time: int32 [12], replicated, may hold values from 0 to 1
- reach_height: int32 [12], replicated, may hold values from 0 to 1
- reach_width: int32 [12], replicated, may hold values from 0 to 3
Outputs:
- attention_out: bfloat16 [64, 64, 32, 1536], P('tm', None, 'ulysses')
- grad_queries: bfloat16 [64, 64, 32, 1536], P('tm', None, 'ulysses')
- grad_keys: bfloat16 [64, 64, 32, 1536], P('tm', None, 'ulysses')
- grad_values: bfloat16 [64, 64, 32, 1536], P('tm', None, 'ulysses')
All inputs are finite; a program needn't handle non-finite values.
Results may differ from a plain program's by a relative error of at most 0.012.
The roundings to bfloat16 on the way count: a program that leaves them out, or rounds other values in their place, can miss the bound.
Values may be sent and summed in bfloat16 or wider, within the bound.
No kernel may reach another device: no remote copies, remote signals or barrier semaphores. Data moves between devices by JAX's collectives and lax.ppermute only.
A program may use at most 64 MiB of HBM per device.

v0:
```python
import math

import jax
import jax.numpy as jnp
from jax import lax
from jax.experimental import pallas as pl
from jax.experimental.pallas import tpu as pltpu
from jax.sharding import PartitionSpec as P

DH = 128
HEADS = 12
TW = 8


def with_halo(array, sides, width):
    for axis, dim in sides:
        count, length = (lax.axis_size(axis), array.shape[dim])
        up = [(i, (i + 1) % count) for i in range(count - 1)]
        down = [(j, i) for i, j in up]
        last = lax.slice_in_dim(array, length - width, length, axis=dim)
        initial = lax.slice_in_dim(array, 0, width, axis=dim)
        before = lax.ppermute(last, axis, up)
        after = lax.ppermute(initial, axis, down)
        array = jnp.concatenate([before, array, after], axis=dim)
    return array


def window_mask(h, reach_ref, live_ref, own_frames, own_rows, cols, rim_frames, rim_rows):
    own_n = own_frames * own_rows * cols
    rim_n = rim_frames * rim_rows * cols
    own_i = lax.broadcasted_iota(jnp.int32, (own_n, rim_n), 0)
    rim_j = lax.broadcasted_iota(jnp.int32, (own_n, rim_n), 1)
    own_t = own_i // (own_rows * cols)
    own_r = (own_i // cols) % own_rows
    own_c = own_i % cols
    rim_t = rim_j // (rim_rows * cols) - 1
    rim_r = (rim_j // cols) % rim_rows - 1
    rim_c = rim_j % cols
    gap_t = jnp.abs(own_t - rim_t)
    gap_r = jnp.abs(own_r - rim_r)
    gap_w = jnp.abs(own_c // TW - rim_c // TW)
    inside = (
        (gap_t <= reach_ref[0, h])
        & (gap_r <= reach_ref[1, h])
        & (gap_w <= reach_ref[2, h])
    )
    return inside & (live_ref[...] > 0)


def make_query_kernel(dims):
    score_scale = 1.0 / math.sqrt(DH)

    def kernel(reach_ref, q_ref, do_ref, k_ref, v_ref, live_ref, og_ref, lse_ref, dot_ref):
        h = pl.program_id(0)
        window = window_mask(h, reach_ref, live_ref, *dims)
        q_now = q_ref[...]
        do_now = do_ref[...]
        k_rim = k_ref[...]
        v_rim = v_ref[...]
        nt = (((1,), (1,)), ((), ()))
        scores = lax.dot_general(q_now, k_rim, nt, preferred_element_type=jnp.float32) * score_scale
        scores = jnp.where(window, scores, -jnp.inf)
        row_peak = jnp.max(scores, axis=1, keepdims=True)
        log_total = row_peak + jnp.log(jnp.sum(jnp.exp(scores - row_peak), axis=1, keepdims=True))
        weights = jnp.exp(scores - log_total)
        weights_b = weights.astype(jnp.bfloat16)
        out_now = jnp.dot(weights_b, v_rim, preferred_element_type=jnp.float32).astype(jnp.bfloat16)
        row_dot = jnp.sum(
            do_now.astype(jnp.float32) * out_now.astype(jnp.float32), axis=1, keepdims=True
        )
        grad_weights = lax.dot_general(do_now, v_rim, nt, preferred_element_type=jnp.float32)
        grad_scores = (weights * (grad_weights - row_dot)).astype(jnp.bfloat16)
        grad_q = jnp.dot(grad_scores, k_rim, preferred_element_type=jnp.float32) * score_scale
        og_ref[0] = out_now
        og_ref[1] = grad_q.astype(jnp.bfloat16)
        lse_ref[...] = log_total
        dot_ref[...] = row_dot

    return kernel


def make_key_kernel(dims):
    score_scale = 1.0 / math.sqrt(DH)

    def kernel(reach_ref, k_ref, v_ref, q_ref, do_ref, lse_ref, dot_ref, live_ref, gkv_ref):
        h = pl.program_id(0)
        window = window_mask(h, reach_ref, live_ref, *dims)
        k_now = k_ref[...]
        v_now = v_ref[...]
        q_rim = q_ref[...]
        do_rim = do_ref[...]
        nt = (((1,), (1,)), ((), ()))
        scores = lax.dot_general(k_now, q_rim, nt, preferred_element_type=jnp.float32) * score_scale
        scores = jnp.where(window, scores, -jnp.inf)
        weights = jnp.exp(scores - lse_ref[...])
        weights_b = weights.astype(jnp.bfloat16)
        grad_weights = lax.dot_general(v_now, do_rim, nt, preferred_element_type=jnp.float32)
        grad_scores = (weights * (grad_weights - dot_ref[...])).astype(jnp.bfloat16)
        grad_k = jnp.dot(grad_scores, q_rim, preferred_element_type=jnp.float32) * score_scale
        grad_v = jnp.dot(weights_b, do_rim, preferred_element_type=jnp.float32)
        gkv_ref[0] = grad_k.astype(jnp.bfloat16)
        gkv_ref[1] = grad_v.astype(jnp.bfloat16)

    return kernel


def body(queries, key_vectors, value_vectors, out_cotangent, reach_time, reach_height, reach_width):
    lane_count = lax.axis_size("ulysses")
    band_index = lax.axis_index("ulysses")
    time_index = lax.axis_index("tm")
    time_count = lax.axis_size("tm")
    frames_dev, height = queries.shape[0], queries.shape[1]
    rows_dev = height // lane_count
    features = queries.shape[3]
    heads = features // DH
    stacked = jnp.stack([queries, key_vectors, value_vectors, out_cotangent])
    own = lax.all_to_all(stacked, "ulysses", split_axis=2, concat_axis=3, tiled=True)
    col_count = own.shape[3]
    rim = with_halo(own, (("tm", 1), ("ulysses", 2)), 1)
    rim_frames, rim_rows = frames_dev + 2, rows_dev + 2
    own_n = frames_dev * rows_dev * col_count
    rim_n = rim_frames * rim_rows * col_count
    own_flat = own.reshape(4, own_n, features)
    rim_flat = rim.reshape(4, rim_n, features)
    dims = (frames_dev, rows_dev, col_count, rim_frames, rim_rows)

    rim_pos = jnp.arange(rim_n, dtype=jnp.int32)
    frame_of = time_index * frames_dev + rim_pos // (rim_rows * col_count) - 1
    row_of = band_index * rows_dev + (rim_pos // col_count) % rim_rows - 1
    live = (
        (frame_of >= 0)
        & (frame_of < time_count * frames_dev)
        & (row_of >= 0)
        & (row_of < height)
    ).astype(jnp.int32).reshape(1, rim_n)
    reach = jnp.stack([reach_time, reach_height, reach_width]).astype(jnp.int32)

    def own_spec(which):
        return pl.BlockSpec((None, own_n, DH), lambda h, r: (which, 0, h))

    def rim_spec(which):
        return pl.BlockSpec((None, rim_n, DH), lambda h, r: (which, 0, h))

    live_spec = pl.BlockSpec((1, rim_n), lambda h, r: (0, 0))
    pair_spec = pl.BlockSpec((2, own_n, DH), lambda h, r: (0, 0, h))
    stat_spec = pl.BlockSpec((None, own_n, 1), lambda h, r: (h, 0, 0))

    og, lse, dots = pl.pallas_call(
        make_query_kernel(dims),
        grid_spec=pltpu.PrefetchScalarGridSpec(
            num_scalar_prefetch=1,
            grid=(heads,),
            in_specs=[own_spec(0), own_spec(3), rim_spec(1), rim_spec(2), live_spec],
            out_specs=[pair_spec, stat_spec, stat_spec],
        ),
        out_shape=[
            jax.ShapeDtypeStruct((2, own_n, features), jnp.bfloat16),
            jax.ShapeDtypeStruct((heads, own_n, 1), jnp.float32),
            jax.ShapeDtypeStruct((heads, own_n, 1), jnp.float32),
        ],
    )(reach, own_flat, own_flat, rim_flat, rim_flat, live)

    def back_to_columns(pair):
        shaped = pair.reshape(2, frames_dev, rows_dev, col_count, features)
        return lax.all_to_all(shaped, "ulysses", split_axis=3, concat_axis=2, tiled=True)

    og_back = back_to_columns(og)

    statistics = jnp.stack([lse, dots]).reshape(2, heads, frames_dev, rows_dev, col_count)
    stat_rim = with_halo(statistics, (("tm", 2), ("ulysses", 3)), 1).reshape(2, heads, 1, rim_n)
    stat_rim_spec = [
        pl.BlockSpec((None, None, 1, rim_n), lambda h, r, w=w: (w, h, 0, 0)) for w in range(2)
    ]
    gkv = pl.pallas_call(
        make_key_kernel(dims),
        grid_spec=pltpu.PrefetchScalarGridSpec(
            num_scalar_prefetch=1,
            grid=(heads,),
            in_specs=[own_spec(1), own_spec(2), rim_spec(0), rim_spec(3)]
            + stat_rim_spec
            + [live_spec],
            out_specs=pair_spec,
        ),
        out_shape=jax.ShapeDtypeStruct((2, own_n, features), jnp.bfloat16),
    )(reach, own_flat, own_flat, rim_flat, rim_flat, stat_rim, stat_rim, live)
    gkv_back = back_to_columns(gkv)
    return (og_back[0], og_back[1], gkv_back[0], gkv_back[1])


def solution(mesh):
    in_specs = (
        P("tm", None, "ulysses", None),
        P("tm", None, "ulysses", None),
        P("tm", None, "ulysses", None),
        P("tm", None, "ulysses", None),
        P(),
        P(),
        P(),
    )
    out_specs = (
        P("tm", None, "ulysses", None),
        P("tm", None, "ulysses", None),
        P("tm", None, "ulysses", None),
        P("tm", None, "ulysses", None),
    )
    return jax.shard_map(body, mesh=mesh, in_specs=in_specs, out_specs=out_specs, check_vma=False)
```

profile of v0, /device:TPU:1, one launch (start us, length us, event | category | flops | bytes accessed | tf_op | source)
XLA Modules:
  0.0 294.6 jit_solution(6452703388237077433)
XLA Ops:
  0.6 0.0 copy-start.4
  0.6 0.0 copy-start.3
  0.7 2.0 copy_bitcast_fusion
  2.6 0.0 copy-done.4
  2.7 0.0 copy-done.3
  2.7 0.8 copy_bitcast_fusion.2
  3.5 2.4 pad_maximum_fusion.2
  5.9 98.8 %all_to_all.48 = bf16[4,2,64,1,1536]{4,1,3,0,2:T(2,128)(2,1)S(1)} all-to-all(bf16[4,2,64,1,1536]{4,1,3,0,2:T(2,128)(2,1)S(1)} %pad_maximum_fusion.2), channel_id=1, replica_groups=mesh['tm'=32,'ulysses'=32] {'ulysses'}, dimensions={2} | all-to-all | bytes 3145728 | tf_op jit(solution)/shard_map/all_to_all | solution.py:117
  104.6 0.9 copy.53
  105.5 0.0 copy-start
  105.5 0.1 fusion.6
  105.6 3.2 %collective-permute-start = (bf16[4,1,2,32,1536]{4,3,2,1,0:T(8,128)(2,1)S(1)}, bf16[4,1,2,32,1536]{4,3,2,1,0:T(8,128)(2,1)S(1)}, u32[]{:S(2)}, u32[]{:S(2)}) collective-permute-start(bf16[4,1,2,32,1536]{4,3,2,1,0:T(8,128)(2,1)S(1)} %get-tuple-element.16), channel_id=1, source_target_pairs={{0,32},{32,64},{64,96},{96,128},{128,160},{160,192},{192,224},{224... | collective-permute-start | bytes 2359304 | tf_op jit(solution)/shard_map/ppermute | solution.py:22
  108.9 1.3 collective-permute-start.1
  110.2 15.0 %collective-permute-done = bf16[4,1,2,32,1536]{4,3,2,1,0:T(8,128)(2,1)S(1)} collective-permute-done((bf16[4,1,2,32,1536]{4,3,2,1,0:T(8,128)(2,1)S(1)}, bf16[4,1,2,32,1536]{4,3,2,1,0:T(8,128)(2,1)S(1)}, u32[]{:S(2)}, u32[]{:S(2)}) %collective-permute-start) | collective-permute-done | bytes 786464 | tf_op jit(solution)/shard_map/ppermute | solution.py:22
  125.2 3.8 %collective-permute-done.1 = bf16[4,1,2,32,1536]{4,3,2,1,0:T(8,128)(2,1)S(1)} collective-permute-done((bf16[4,1,2,32,1536]{4,3,2,1,0:T(8,128)(2,1)S(1)}, bf16[4,1,2,32,1536]{4,3,2,1,0:T(8,128)(2,1)S(1)}, u32[]{:S(2)}, u32[]{:S(2)}) %collective-permute-start.1) | collective-permute-done | bytes 786464 | tf_op jit(solution)/shard_map/ppermute | solution.py:23
  129.1 0.4 pad_maximum_fusion.1
  129.4 0.0 copy-start.5
  129.4 0.0 copy-start.6
  129.4 0.0 copy-start.7
  129.5 1.8 fusion.5
  131.3 2.1 collective-permute-start.2
  133.4 3.9 %collective-permute-start.3 = (bf16[4,4,1,32,1536]{4,3,2,1,0:T(8,128)(2,1)}, bf16[4,4,1,32,1536]{4,3,2,1,0:T(8,128)(2,1)}, u32[]{:S(2)}, u32[]{:S(2)}) collective-permute-start(bf16[4,4,1,32,1536]{4,3,2,1,0:T(8,128)(2,1)} %get-tuple-element.15), channel_id=1, source_target_pairs={{1,0},{2,1},{3,2},{4,3},{5,4},{6,5},{7,6},{8,7},{9,8},{10,9},{11,1... | collective-permute-start | bytes 4718600 | tf_op jit(solution)/shard_map/ppermute | solution.py:23
  137.3 0.6 and_convert_fusion.live_ref
  137.9 0.0 copy-done.6
  137.9 0.6 pad_add_fusion.reach_ref
  138.5 12.6 %collective-permute-done.2 = bf16[4,4,1,32,1536]{4,3,2,1,0:T(8,128)(2,1)} collective-permute-done((bf16[4,4,1,32,1536]{4,3,2,1,0:T(8,128)(2,1)}, bf16[4,4,1,32,1536]{4,3,2,1,0:T(8,128)(2,1)}, u32[]{:S(2)}, u32[]{:S(2)}) %collective-permute-start.2) | collective-permute-done | bytes 1572896 | tf_op jit(solution)/shard_map/ppermute | solution.py:22
  151.1 4.4 %collective-permute-done.3 = bf16[4,4,1,32,1536]{4,3,2,1,0:T(8,128)(2,1)} collective-permute-done((bf16[4,4,1,32,1536]{4,3,2,1,0:T(8,128)(2,1)}, bf16[4,4,1,32,1536]{4,3,2,1,0:T(8,128)(2,1)}, u32[]{:S(2)}, u32[]{:S(2)}) %collective-permute-start.3) | collective-permute-done | bytes 1572896 | tf_op jit(solution)/shard_map/ppermute | solution.py:23
  155.5 5.2 %pad_maximum_fusion = bf16[4,4,4,32,1536]{4,3,2,1,0:T(8,128)(2,1)} fusion(bf16[4,4,1,32,1536]{4,3,2,1,0:T(8,128)(2,1)} %collective-permute-done.3, bf16[4,1,2,32,1536]{4,3,2,1,0:T(8,128)(2,1)S(1)} %collective-permute-done.1, bf16[4,2,2,32,1536]{4,3,2,1,0:T(8,128)(2,1)S(1)} %bitcast.40, bf16[4,1,2,32,1536]{4,3,2,1,0:T(8,128)(2,1)S(1)} %collective-permute-done, ...), kind=kLoop, calls=%fused_computation | loop fusion | flops 12582912 | bytes 12582912 | tf_op jit(solution)/shard_map/concatenate | solution.py:24
  160.7 13.4 %shard_map.102 = (bf16[2,128,1536]{2,1,0:T(8,128)(2,1)}, f32[12,128,1]{2,1,0:T(8,128)}, f32[12,128,1]{2,1,0:T(8,128)}) custom-call(s32[3,12]{1,0:T(4,128)} %pad_add_fusion.reach_ref, bf16[4,128,1536]{2,1,0:T(8,128)(2,1)} %bitcast.41, bf16[4,128,1536]{2,1,0:T(8,128)(2,1)} %bitcast.42, bf16[4,512,1536]{2,1,0:T(8,128)(2,1)} %bitcast.34, ...), custom_call_target="tpu_custom_call" | custom-call | tf_op jit(solution)/shard_map/pallas_call | solution.py:148
  174.0 3.0 %copy.35 = bf16[2,2,2,32,1536]{4,2,1,0,3:T(2,128)(2,1)} copy(bf16[2,2,2,32,1536]{4,3,2,1,0:T(8,128)(2,1)} %bitcast.53) | data formatting | bytes 1572864 | tf_op jit(solution)/shard_map/reshape | solution.py:164
  177.0 6.8 %all-to-all-start.1 = ((bf16[2,2,2,32,1536]{4,2,1,0,3:T(2,128)(2,1)}), bf16[2,2,2,32,1536]{4,2,1,0,3:T(2,128)(2,1)S(1)}, u32[]{:S(2)}, u32[]{:S(2)}) async-start(bf16[2,2,2,32,1536]{4,2,1,0,3:T(2,128)(2,1)} %copy.35), calls=%async_computation.1 | async-start | bytes 1572864 | tf_op jit(solution)/shard_map/all_to_all | solution.py:165
  183.8 0.3 reduce
  184.1 0.1 stack.45
  184.2 0.0 copy-done.1
  184.2 0.3 reduce.1
  184.5 0.1 stack.46
  184.6 3.2 %collective-permute-start.4 = (f32[2,12,1,2,32]{4,3,2,0,1:T(2,128)S(1)}, f32[2,12,1,2,32]{4,3,2,0,1:T(2,128)S(1)}, u32[]{:S(2)}, u32[]{:S(2)}) collective-permute-start(f32[2,12,1,2,32]{4,3,2,0,1:T(2,128)S(1)} %get-tuple-element.26), channel_id=1, source_target_pairs={{0,32},{32,64},{64,96},{96,128},{128,160},{160,192},{192,224},{224... | collective-permute-start | bytes 18440 | tf_op jit(solution)/shard_map/ppermute | solution.py:22
  187.8 1.3 collective-permute-start.5
  189.1 0.0 collective-permute-done.4
  189.1 4.5 %collective-permute-done.5 = f32[2,12,1,2,32]{4,3,2,0,1:T(2,128)S(1)} collective-permute-done((f32[2,12,1,2,32]{4,3,2,0,1:T(2,128)S(1)}, f32[2,12,1,2,32]{4,3,2,0,1:T(2,128)S(1)}, u32[]{:S(2)}, u32[]{:S(2)}) %collective-permute-start.5) | collective-permute-done | bytes 6176 | tf_op jit(solution)/shard_map/ppermute | solution.py:23
  193.5 0.1 pad_maximum_fusion.4
  193.6 0.1 fusion.9
  193.7 4.4 %collective-permute-start.6 = (f32[2,12,4,1,32]{4,3,2,0,1:T(1,128)S(1)}, f32[2,12,4,1,32]{4,3,2,0,1:T(1,128)S(1)}, u32[]{:S(2)}, u32[]{:S(2)}) collective-permute-start(f32[2,12,4,1,32]{4,3,2,0,1:T(1,128)S(1)} %get-tuple-element.24), channel_id=1, source_target_pairs={{0,1},{1,2},{2,3},{3,4},{4,5},{5,6},{6,7},{7,8},{8,9},{9,10},{10,1... | collective-permute-start | bytes 36872 | tf_op jit(solution)/shard_map/ppermute | solution.py:22
  198.1 1.9 collective-permute-start.7
  200.0 13.8 %collective-permute-done.6 = f32[2,12,4,1,32]{4,3,2,0,1:T(1,128)S(1)} collective-permute-done((f32[2,12,4,1,32]{4,3,2,0,1:T(1,128)S(1)}, f32[2,12,4,1,32]{4,3,2,0,1:T(1,128)S(1)}, u32[]{:S(2)}, u32[]{:S(2)}) %collective-permute-start.6) | collective-permute-done | bytes 12320 | tf_op jit(solution)/shard_map/ppermute | solution.py:22
  213.8 5.4 %collective-permute-done.7 = f32[2,12,4,1,32]{4,3,2,0,1:T(1,128)S(1)} collective-permute-done((f32[2,12,4,1,32]{4,3,2,0,1:T(1,128)S(1)}, f32[2,12,4,1,32]{4,3,2,0,1:T(1,128)S(1)}, u32[]{:S(2)}, u32[]{:S(2)}) %collective-permute-start.7) | collective-permute-done | bytes 12320 | tf_op jit(solution)/shard_map/ppermute | solution.py:23
  219.2 0.2 pad_maximum_fusion.3
  219.4 0.2 reshape.170
  219.5 0.7 copy.46.lse_ref.dot_ref
  220.2 11.5 %shard_map.103 = bf16[2,128,1536]{2,1,0:T(8,128)(2,1)} custom-call(s32[3,12]{1,0:T(4,128)} %pad_add_fusion.reach_ref, bf16[4,128,1536]{2,1,0:T(8,128)(2,1)} %bitcast.43, bf16[4,128,1536]{2,1,0:T(8,128)(2,1)} %bitcast.44, bf16[4,512,1536]{2,1,0:T(8,128)(2,1)} %bitcast.36, bf16[4,512,1536]{2,1,0:T(8,128)(2,1)} %bitcast.37, ...), custom_call_target="tpu_custom_call" | custom-call | tf_op jit(solution)/shard_map/pallas_call | solution.py:174
  231.7 2.8 copy.39
  234.5 0.0 all-to-all-done.1
  234.5 12.7 %all-to-all-start.2 = ((bf16[2,2,2,32,1536]{4,2,1,0,3:T(2,128)(2,1)}), bf16[2,2,2,32,1536]{4,2,1,0,3:T(2,128)(2,1)S(1)}, u32[]{:S(2)}, u32[]{:S(2)}) async-start(bf16[2,2,2,32,1536]{4,2,1,0,3:T(2,128)(2,1)} %copy.39), calls=%async_computation.2 | async-start | bytes 1572864 | tf_op jit(solution)/shard_map/all_to_all | solution.py:165
  247.2 0.5 fusion.8
  247.8 0.3 copy.36
  248.1 0.8 copy.42
  248.9 0.3 copy.37
  249.2 0.8 copy.43
  249.9 41.9 %all-to-all-done.2 = bf16[2,2,2,32,1536]{4,2,1,0,3:T(2,128)(2,1)S(1)} async-done(((bf16[2,2,2,32,1536]{4,2,1,0,3:T(2,128)(2,1)}), bf16[2,2,2,32,1536]{4,2,1,0,3:T(2,128)(2,1)S(1)}, u32[]{:S(2)}, u32[]{:S(2)}) %all-to-all-start.2) | async-done | bytes 786464 | tf_op jit(solution)/shard_map/all_to_all | solution.py:165
  291.9 0.5 fusion.7
  292.4 0.3 copy.40
  292.7 0.8 copy.44
  293.5 0.3 copy.41
  293.8 0.8 copy.45
  (9 shorter events, 0.0 us)
Async XLA Ops:
  0.6 2.0 copy-start.4
  0.6 2.0 copy-start.3
  105.5 50.0 %copy-start = (bf16[4,2,32,2,1,1536]{5,2,3,1,0,4:T(8,128)(2,1)}, bf16[4,2,32,2,1,1536]{5,2,3,1,0,4:T(8,128)(2,1)S(1)}, u32[]{:S(2)}) copy-start(bf16[4,2,32,2,1,1536]{5,2,3,1,0,4:T(8,128)(2,1)S(1)} %copy.53) | copy-start | bytes 4718596
  105.6 19.6 %collective-permute-start = (bf16[4,1,2,32,1536]{4,3,2,1,0:T(8,128)(2,1)S(1)}, bf16[4,1,2,32,1536]{4,3,2,1,0:T(8,128)(2,1)S(1)}, u32[]{:S(2)}, u32[]{:S(2)}) collective-permute-start(bf16[4,1,2,32,1536]{4,3,2,1,0:T(8,128)(2,1)S(1)} %get-tuple-element.16), channel_id=1, source_target_pairs={{0,32},{32,64},{64,96},{96,128},{128,160},{160,192},{192,224},{224... | collective-permute-start | bytes 2359304 | tf_op jit(solution)/shard_map/ppermute | solution.py:22
  108.9 20.2 %collective-permute-start.1 = (bf16[4,1,2,32,1536]{4,3,2,1,0:T(8,128)(2,1)S(1)}, bf16[4,1,2,32,1536]{4,3,2,1,0:T(8,128)(2,1)S(1)}, u32[]{:S(2)}, u32[]{:S(2)}) collective-permute-start(bf16[4,1,2,32,1536]{4,3,2,1,0:T(8,128)(2,1)S(1)} %get-tuple-element.17), channel_id=1, source_target_pairs={{32,0},{64,32},{96,64},{128,96},{160,128},{192,160},{224,192},{256... | collective-permute-start | bytes 2359304 | tf_op jit(solution)/shard_map/ppermute | solution.py:23
  129.4 8.5 %copy-start.5 = (s32[12]{0:T(128)S(1)}, s32[12]{0:T(128)}, u32[]{:S(2)}) copy-start(s32[12]{0:T(128)} %param.13) | copy-start | bytes 148
  129.4 8.5 %copy-start.6 = (s32[12]{0:T(128)S(1)}, s32[12]{0:T(128)}, u32[]{:S(2)}) copy-start(s32[12]{0:T(128)} %param.12) | copy-start | bytes 148
  129.4 8.5 %copy-start.7 = (s32[12]{0:T(128)S(1)}, s32[12]{0:T(128)}, u32[]{:S(2)}) copy-start(s32[12]{0:T(128)} %param.11) | copy-start | bytes 148
  131.3 19.8 %collective-permute-start.2 = (bf16[4,4,1,32,1536]{4,3,2,1,0:T(8,128)(2,1)}, bf16[4,4,1,32,1536]{4,3,2,1,0:T(8,128)(2,1)}, u32[]{:S(2)}, u32[]{:S(2)}) collective-permute-start(bf16[4,4,1,32,1536]{4,3,2,1,0:T(8,128)(2,1)} %get-tuple-element.14), channel_id=1, source_target_pairs={{0,1},{1,2},{2,3},{3,4},{4,5},{5,6},{6,7},{7,8},{8,9},{9,10},{10,1... | collective-permute-start | bytes 4718600 | tf_op jit(solution)/shard_map/ppermute | solution.py:22
  133.4 22.1 %collective-permute-start.3 = (bf16[4,4,1,32,1536]{4,3,2,1,0:T(8,128)(2,1)}, bf16[4,4,1,32,1536]{4,3,2,1,0:T(8,128)(2,1)}, u32[]{:S(2)}, u32[]{:S(2)}) collective-permute-start(bf16[4,4,1,32,1536]{4,3,2,1,0:T(8,128)(2,1)} %get-tuple-element.15), channel_id=1, source_target_pairs={{1,0},{2,1},{3,2},{4,3},{5,4},{6,5},{7,6},{8,7},{9,8},{10,9},{11,1... | collective-permute-start | bytes 4718600 | tf_op jit(solution)/shard_map/ppermute | solution.py:23
  174.0 9.8 %copy-start.2 = (f32[12,128,1]{2,1,0:T(8,128)S(1)}, f32[12,128,1]{2,1,0:T(8,128)}, u32[]{:S(2)}) copy-start(f32[12,128,1]{2,1,0:T(8,128)} %get-tuple-element.8) | copy-start | bytes 18436
  177.0 7.2 %copy-start.1 = (f32[12,128,1]{2,1,0:T(8,128)S(1)}, f32[12,128,1]{2,1,0:T(8,128)}, u32[]{:S(2)}) copy-start(f32[12,128,1]{2,1,0:T(8,128)} %get-tuple-element.9) | copy-start | bytes 18436
  177.0 57.5 %all-to-all-start.1 = ((bf16[2,2,2,32,1536]{4,2,1,0,3:T(2,128)(2,1)}), bf16[2,2,2,32,1536]{4,2,1,0,3:T(2,128)(2,1)S(1)}, u32[]{:S(2)}, u32[]{:S(2)}) async-start(bf16[2,2,2,32,1536]{4,2,1,0,3:T(2,128)(2,1)} %copy.35), calls=%async_computation.1 | async-start | bytes 1572864 | tf_op jit(solution)/shard_map/all_to_all | solution.py:165
  184.6 4.5 %collective-permute-start.4 = (f32[2,12,1,2,32]{4,3,2,0,1:T(2,128)S(1)}, f32[2,12,1,2,32]{4,3,2,0,1:T(2,128)S(1)}, u32[]{:S(2)}, u32[]{:S(2)}) collective-permute-start(f32[2,12,1,2,32]{4,3,2,0,1:T(2,128)S(1)} %get-tuple-element.26), channel_id=1, source_target_pairs={{0,32},{32,64},{64,96},{96,128},{128,160},{160,192},{192,224},{224... | collective-permute-start | bytes 18440 | tf_op jit(solution)/shard_map/ppermute | solution.py:22
  187.8 5.8 %collective-permute-start.5 = (f32[2,12,1,2,32]{4,3,2,0,1:T(2,128)S(1)}, f32[2,12,1,2,32]{4,3,2,0,1:T(2,128)S(1)}, u32[]{:S(2)}, u32[]{:S(2)}) collective-permute-start(f32[2,12,1,2,32]{4,3,2,0,1:T(2,128)S(1)} %get-tuple-element.27), channel_id=1, source_target_pairs={{32,0},{64,32},{96,64},{128,96},{160,128},{192,160},{224,192},{256... | collective-permute-start | bytes 18440 | tf_op jit(solution)/shard_map/ppermute | solution.py:23
  193.7 20.1 %collective-permute-start.6 = (f32[2,12,4,1,32]{4,3,2,0,1:T(1,128)S(1)}, f32[2,12,4,1,32]{4,3,2,0,1:T(1,128)S(1)}, u32[]{:S(2)}, u32[]{:S(2)}) collective-permute-start(f32[2,12,4,1,32]{4,3,2,0,1:T(1,128)S(1)} %get-tuple-element.24), channel_id=1, source_target_pairs={{0,1},{1,2},{2,3},{3,4},{4,5},{5,6},{6,7},{7,8},{8,9},{9,10},{10,1... | collective-permute-start | bytes 36872 | tf_op jit(solution)/shard_map/ppermute | solution.py:22
  198.1 21.1 %collective-permute-start.7 = (f32[2,12,4,1,32]{4,3,2,0,1:T(1,128)S(1)}, f32[2,12,4,1,32]{4,3,2,0,1:T(1,128)S(1)}, u32[]{:S(2)}, u32[]{:S(2)}) collective-permute-start(f32[2,12,4,1,32]{4,3,2,0,1:T(1,128)S(1)} %get-tuple-element.25), channel_id=1, source_target_pairs={{1,0},{2,1},{3,2},{4,3},{5,4},{6,5},{7,6},{8,7},{9,8},{10,9},{11,1... | collective-permute-start | bytes 36872 | tf_op jit(solution)/shard_map/ppermute | solution.py:23
  234.5 57.3 %all-to-all-start.2 = ((bf16[2,2,2,32,1536]{4,2,1,0,3:T(2,128)(2,1)}), bf16[2,2,2,32,1536]{4,2,1,0,3:T(2,128)(2,1)S(1)}, u32[]{:S(2)}, u32[]{:S(2)}) async-start(bf16[2,2,2,32,1536]{4,2,1,0,3:T(2,128)(2,1)} %copy.39), calls=%async_computation.2 | async-start | bytes 1572864 | tf_op jit(solution)/shard_map/all_to_all | solution.py:165
where the time goes:
time: 297 us; the launch traced here: 295 us
  waiting for transfers between devices  101 us (34%)
  blocking collectives  98.8 us (33%)
  starting transfers between devices  40.7 us (14%)
  Pallas kernels  24.9 us (8%)
  local copies, waits for them, and re-layouts  18 us (6%)
  other arithmetic  9.85 us (3%)
    all_to_all x1, blocking collectives, body(): lax.all_to_all(stacked, 'ulysses', split_axis=2, concat_axis=3, tiled=True)  98.8 us
    all_to_all x2, waiting for transfers between devices, back_to_columns(): lax.all_to_all(shaped, 'ulysses', split_axis=3, concat_axis=2, tiled=True)  41.9 us
    ppermute x4, waiting for transfers between devices, with_halo(): before = lax.ppermute(last, axis, up)  41.4 us
    all_to_all x2, starting transfers between devices, back_to_columns(): lax.all_to_all(shaped, 'ulysses', split_axis=3, concat_axis=2, tiled=True)  19.4 us
    ppermute x4, waiting for transfers between devices, with_halo(): after = lax.ppermute(initial, axis, down)  18.1 us
    pallas_call x1, Pallas kernels, body(): pl.pallas_call(make_query_kernel(dims), grid_spec=pltpu.PrefetchScalarGri...  13.4 us
    ppermute x4, starting transfers between devices, with_halo(): before = lax.ppermute(last, axis, up)  12.9 us
    pallas_call x1, Pallas kernels, body(): pl.pallas_call(make_key_kernel(dims), grid_spec=pltpu.PrefetchScalarGridS...  11.5 us
  transfers between devices with their start and end apart: 10, of which 8 were waited for; matrix products, arithmetic and copies ran while one was open for 3% of the time, Pallas kernels for 4%

commit v1 on v0

--- a/solution.py
+++ b/solution.py
@@ -12,17 +12,44 @@
 TW = 8
 
 
-def with_halo(array, sides, width):
-    for axis, dim in sides:
-        count, length = (lax.axis_size(axis), array.shape[dim])
-        up = [(i, (i + 1) % count) for i in range(count - 1)]
-        down = [(j, i) for i, j in up]
-        last = lax.slice_in_dim(array, length - width, length, axis=dim)
-        initial = lax.slice_in_dim(array, 0, width, axis=dim)
-        before = lax.ppermute(last, axis, up)
-        after = lax.ppermute(initial, axis, down)
-        array = jnp.concatenate([before, array, after], axis=dim)
-    return array
+def neighbour(array, shift_t, shift_u):
+    time_count = lax.axis_size("tm")
+    lane_count = lax.axis_size("ulysses")
+    pairs = []
+    for t in range(time_count):
+        for u in range(lane_count):
+            t_to, u_to = t + shift_t, u + shift_u
+            if 0 <= t_to < time_count and 0 <= u_to < lane_count:
+                pairs.append((t * lane_count + u, t_to * lane_count + u_to))
+    return lax.ppermute(array, ("tm", "ulysses"), pairs)
+
+
+def with_rim(array, frame_dim):
+    row_dim = frame_dim + 1
+    frames, rows = array.shape[frame_dim], array.shape[row_dim]
+
+    def part(tensor, dim, lo, hi):
+        return lax.slice_in_dim(tensor, lo, hi, axis=dim)
+
+    first_f, last_f = part(array, frame_dim, 0, 1), part(array, frame_dim, frames - 1, frames)
+    slabs = []
+    for shift_t, edge in ((1, last_f), (-1, first_f)):
+        first_r, last_r = part(edge, row_dim, 0, 1), part(edge, row_dim, rows - 1, rows)
+        slabs.append(
+            jnp.concatenate(
+                [
+                    neighbour(last_r, shift_t, 1),
+                    neighbour(edge, shift_t, 0),
+                    neighbour(first_r, shift_t, -1),
+                ],
+                axis=row_dim,
+            )
+        )
+    first_r, last_r = part(array, row_dim, 0, 1), part(array, row_dim, rows - 1, rows)
+    middle = jnp.concatenate(
+        [neighbour(last_r, 0, 1), array, neighbour(first_r, 0, -1)], axis=row_dim
+    )
+    return jnp.concatenate([slabs[0], middle, slabs[1]], axis=frame_dim)
 
 
 def window_mask(h, reach_ref, live_ref, own_frames, own_rows, cols, rim_frames, rim_rows):
@@ -82,7 +109,7 @@
 def make_key_kernel(dims):
     score_scale = 1.0 / math.sqrt(DH)
 
-    def kernel(reach_ref, k_ref, v_ref, q_ref, do_ref, lse_ref, dot_ref, live_ref, gkv_ref):
+    def kernel(reach_ref, k_ref, v_ref, q_ref, do_ref, lse_ref, dot_ref, live_ref, buf_ref, gkv_ref):
         h = pl.program_id(0)
         window = window_mask(h, reach_ref, live_ref, *dims)
         k_now = k_ref[...]
@@ -113,15 +140,15 @@
     rows_dev = height // lane_count
     features = queries.shape[3]
     heads = features // DH
-    stacked = jnp.stack([queries, key_vectors, value_vectors, out_cotangent])
+    stacked = jnp.stack([key_vectors, value_vectors, queries, out_cotangent])
     own = lax.all_to_all(stacked, "ulysses", split_axis=2, concat_axis=3, tiled=True)
     col_count = own.shape[3]
-    rim = with_halo(own, (("tm", 1), ("ulysses", 2)), 1)
     rim_frames, rim_rows = frames_dev + 2, rows_dev + 2
     own_n = frames_dev * rows_dev * col_count
     rim_n = rim_frames * rim_rows * col_count
+    kv_rim = with_rim(own[0:2], 1).reshape(2, rim_n, features)
+    qd_rim = with_rim(own[2:4], 1).reshape(2, rim_n, features)
     own_flat = own.reshape(4, own_n, features)
-    rim_flat = rim.reshape(4, rim_n, features)
     dims = (frames_dev, rows_dev, col_count, rim_frames, rim_rows)
 
     rim_pos = jnp.arange(rim_n, dtype=jnp.int32)
@@ -141,50 +168,48 @@
     def rim_spec(which):
         return pl.BlockSpec((None, rim_n, DH), lambda h, r: (which, 0, h))
 
+    def pair_spec(which):
+        return pl.BlockSpec((2, own_n, DH), lambda h, r: (which, 0, h))
+
     live_spec = pl.BlockSpec((1, rim_n), lambda h, r: (0, 0))
-    pair_spec = pl.BlockSpec((2, own_n, DH), lambda h, r: (0, 0, h))
     stat_spec = pl.BlockSpec((None, own_n, 1), lambda h, r: (h, 0, 0))
 
-    og, lse, dots = pl.pallas_call(
+    results, lse, dots = pl.pallas_call(
         make_query_kernel(dims),
         grid_spec=pltpu.PrefetchScalarGridSpec(
             num_scalar_prefetch=1,
             grid=(heads,),
-            in_specs=[own_spec(0), own_spec(3), rim_spec(1), rim_spec(2), live_spec],
-            out_specs=[pair_spec, stat_spec, stat_spec],
+            in_specs=[own_spec(2), own_spec(3), rim_spec(0), rim_spec(1), live_spec],
+            out_specs=[pair_spec(0), stat_spec, stat_spec],
         ),
         out_shape=[
-            jax.ShapeDtypeStruct((2, own_n, features), jnp.bfloat16),
+            jax.ShapeDtypeStruct((4, own_n, features), jnp.bfloat16),
             jax.ShapeDtypeStruct((heads, own_n, 1), jnp.float32),
             jax.ShapeDtypeStruct((heads, own_n, 1), jnp.float32),
         ],
-    )(reach, own_flat, own_flat, rim_flat, rim_flat, live)
-
-    def back_to_columns(pair):
-        shaped = pair.reshape(2, frames_dev, rows_dev, col_count, features)
-        return lax.all_to_all(shaped, "ulysses", split_axis=3, concat_axis=2, tiled=True)
-
-    og_back = back_to_columns(og)
+    )(reach, own_flat, own_flat, kv_rim, kv_rim, live)
 
     statistics = jnp.stack([lse, dots]).reshape(2, heads, frames_dev, rows_dev, col_count)
-    stat_rim = with_halo(statistics, (("tm", 2), ("ulysses", 3)), 1).reshape(2, heads, 1, rim_n)
+    stat_rim = with_rim(statistics, 2).reshape(2, heads, 1, rim_n)
     stat_rim_spec = [
         pl.BlockSpec((None, None, 1, rim_n), lambda h, r, w=w: (w, h, 0, 0)) for w in range(2)
     ]
-    gkv = pl.pallas_call(
+    results = pl.pallas_call(
         make_key_kernel(dims),
         grid_spec=pltpu.PrefetchScalarGridSpec(
             num_scalar_prefetch=1,
             grid=(heads,),
-            in_specs=[own_spec(1), own_spec(2), rim_spec(0), rim_spec(3)]
+            in_specs=[own_spec(0), own_spec(1), rim_spec(0), rim_spec(1)]
             + stat_rim_spec
-            + [live_spec],
-            out_specs=pair_spec,
+            + [live_spec, pl.BlockSpec(memory_space=pl.ANY)],
+            out_specs=pair_spec(1),
         ),
-        out_shape=jax.ShapeDtypeStruct((2, own_n, features), jnp.bfloat16),
-    )(reach, own_flat, own_flat, rim_flat, rim_flat, stat_rim, stat_rim, live)
-    gkv_back = back_to_columns(gkv)
-    return (og_back[0], og_back[1], gkv_back[0], gkv_back[1])
+        out_shape=jax.ShapeDtypeStruct((4, own_n, features), jnp.bfloat16),
+        input_output_aliases={8: 0},
+    )(reach, own_flat, own_flat, qd_rim, qd_rim, stat_rim, stat_rim, live, results)
+    shaped = results.reshape(4, frames_dev, rows_dev, col_count, features)
+    back = lax.all_to_all(shaped, "ulysses", split_axis=3, concat_axis=2, tiled=True)
+    return (back[0], back[1], back[2], back[3])
 
 
 def solution(mesh):

time: 297 us -> 329 us (1.11)
  the two profiles are of different devices: /device:TPU:1 before, /device:TPU:5 now
where the time goes in v1:
time: 329 us; the launch traced here: 328 us
  starting transfers between devices  102 us (31%)
  blocking collectives  92.8 us (28%)
  waiting for transfers between devices  76.7 us (23%)
  Pallas kernels  24.9 us (8%)
  local copies, waits for them, and re-layouts  17.3 us (5%)
  other arithmetic  13.2 us (4%)
    all_to_all x1, blocking collectives, body(): lax.all_to_all(shaped, 'ulysses', split_axis=3, concat_axis=2, tiled=True)  92.8 us
    ppermute x24, starting transfers between devices, neighbour(): return lax.ppermute(array, ('tm', 'ulysses'), pairs)  82.2 us
    all_to_all x1, waiting for transfers between devices, body(): lax.all_to_all(stacked, 'ulysses', split_axis=2, concat_axis=3, tiled=True)  76.6 us
    all_to_all x1, starting transfers between devices, body(): lax.all_to_all(stacked, 'ulysses', split_axis=2, concat_axis=3, tiled=True)  19.6 us
    pallas_call x1, Pallas kernels, body(): pl.pallas_call(make_query_kernel(dims), grid_spec=pltpu.PrefetchScalarGri...  13.4 us
    pallas_call x1, Pallas kernels, body(): pl.pallas_call(make_key_kernel(dims), grid_spec=pltpu.PrefetchScalarGridS...  11.5 us
  transfers between devices with their start and end apart: 25, of which 1 were waited for; matrix products, arithmetic and copies ran while one was open for 4% of the time, Pallas kernels for 4%

profile of v1, /device:TPU:5, one launch (start us, length us, event | category | flops | bytes accessed | tf_op | source)
XLA Modules:
  0.0 327.7 jit_solution(1014759231558366790)
XLA Ops:
  0.6 1.9 copy_bitcast_fusion
  2.6 1.9 copy_bitcast_fusion.2
  4.5 0.0 copy-start.1
  4.5 0.0 copy-start.2
  4.5 3.3 %pad_maximum_fusion = bf16[4,2,64,1,1536]{4,1,3,0,2:T(2,128)(2,1)} fusion(bf16[1,2,64,1,1536]{4,1,3,0,2:T(2,128)(2,1)S(1)} %get-tuple-element.46, bf16[1,2,64,1,1536]{4,1,3,0,2:T(2,128)(2,1)S(1)} %get-tuple-element.47, bf16[1,2,64,1,1536]{4,1,3,0,2:T(2,128)(2,1)S(1)} %get-tuple-element.48, bf16[1,2,64,1,1536]{4,1,3,0,2:T(2,128)(2,1)S(1)} %get-tuple-element.49), kind=kLoop, calls=%fused_computation.2 | loop fusion | flops 2359296 | bytes 3145728 | tf_op jit(solution)/shard_map/stack | solution.py:143
  7.8 19.6 %all-to-all-start = ((bf16[4,2,64,1,1536]{4,1,3,0,2:T(2,128)(2,1)}), bf16[4,2,64,1,1536]{4,1,3,0,2:T(2,128)(2,1)S(1)}, u32[]{:S(2)}, u32[]{:S(2)}) async-start(bf16[4,2,64,1,1536]{4,1,3,0,2:T(2,128)(2,1)} %pad_maximum_fusion), calls=%async_computation | async-start | bytes 3145728 | tf_op jit(solution)/shard_map/all_to_all | solution.py:144
  27.4 0.6 and_convert_fusion.live_ref
  28.0 0.6 pad_add_fusion.reach_ref
  28.6 76.6 %all-to-all-done = bf16[4,2,64,1,1536]{4,1,3,0,2:T(2,128)(2,1)S(1)} async-done(((bf16[4,2,64,1,1536]{4,1,3,0,2:T(2,128)(2,1)}), bf16[4,2,64,1,1536]{4,1,3,0,2:T(2,128)(2,1)S(1)}, u32[]{:S(2)}, u32[]{:S(2)}) %all-to-all-start) | async-done | bytes 1572896 | tf_op jit(solution)/shard_map/all_to_all | solution.py:144
  105.2 0.9 copy.52
  106.1 0.1 slice_bitcast_fusion
  106.2 0.1 fusion.6
  106.3 0.1 fusion.8
  106.4 0.9 copy-done
  107.2 0.1 fusion.7
  107.3 2.4 collective-permute-start.8
  109.7 5.3 %collective-permute-start.15 = (bf16[2,1,1,32,1536]{4,3,2,1,0:T(8,128)(2,1)S(1)}, bf16[2,1,1,32,1536]{4,3,2,1,0:T(8,128)(2,1)S(1)}, u32[]{:S(2)}, u32[]{:S(2)}) collective-permute-start(bf16[2,1,1,32,1536]{4,3,2,1,0:T(8,128)(2,1)S(1)} %get-tuple-element.23), channel_id=1, source_target_pairs={{33,0},{34,1},{35,2},{36,3},{37,4},{38,5},{39,6},{40,7},{41,8},{42... | collective-permute-start | bytes 589832 | tf_op jit(solution)/shard_map/ppermute | solution.py:24
  115.0 3.5 %collective-permute-start.13 = (bf16[2,1,1,32,1536]{4,3,2,1,0:T(8,128)(2,1)S(1)}, bf16[2,1,1,32,1536]{4,3,2,1,0:T(8,128)(2,1)S(1)}, u32[]{:S(2)}, u32[]{:S(2)}) collective-permute-start(bf16[2,1,1,32,1536]{4,3,2,1,0:T(8,128)(2,1)S(1)} %get-tuple-element.24), channel_id=1, source_target_pairs={{32,1},{33,2},{34,3},{35,4},{36,5},{37,6},{38,7},{39,8},{40,9},{41... | collective-permute-start | bytes 589832 | tf_op jit(solution)/shard_map/ppermute | solution.py:24
  118.5 0.8 fusion.11
  119.3 0.1 fusion.10
  119.3 2.1 collective-permute-start.10
  121.4 3.6 %collective-permute-start.11 = (bf16[2,2,1,32,1536]{4,3,2,1,0:T(8,128)(2,1)S(1)}, bf16[2,2,1,32,1536]{4,3,2,1,0:T(8,128)(2,1)S(1)}, u32[]{:S(2)}, u32[]{:S(2)}) collective-permute-start(bf16[2,2,1,32,1536]{4,3,2,1,0:T(8,128)(2,1)S(1)} %get-tuple-element.28), channel_id=1, source_target_pairs={{0,1},{1,2},{2,3},{3,4},{4,5},{5,6},{6,7},{7,8},{8,9},{9,10},{10,1... | collective-permute-start | bytes 1179656 | tf_op jit(solution)/shard_map/ppermute | solution.py:24
  125.0 1.9 collective-permute-start.12
  127.0 1.9 collective-permute-start.9
  128.9 5.5 %collective-permute-start.14 = (bf16[2,1,2,32,1536]{4,3,2,1,0:T(8,128)(2,1)S(1)}, bf16[2,1,2,32,1536]{4,3,2,1,0:T(8,128)(2,1)S(1)}, u32[]{:S(2)}, u32[]{:S(2)}) collective-permute-start(bf16[2,1,2,32,1536]{4,3,2,1,0:T(8,128)(2,1)S(1)} %get-tuple-element.27), channel_id=1, source_target_pairs={{32,0},{33,1},{34,2},{35,3},{36,4},{37,5},{38,6},{39,7},{40,8},{41... | collective-permute-start | bytes 1179656 | tf_op jit(solution)/shard_map/ppermute | solution.py:24
  134.4 0.9 fusion.9
  135.3 1.9 collective-permute-start
  137.2 6.4 %collective-permute-start.7 = (bf16[2,1,1,32,1536]{4,3,2,1,0:T(8,128)(2,1)}, bf16[2,1,1,32,1536]{4,3,2,1,0:T(8,128)(2,1)}, u32[]{:S(2)}, u32[]{:S(2)}) collective-permute-start(bf16[2,1,1,32,1536]{4,3,2,1,0:T(8,128)(2,1)} %get-tuple-element.31), channel_id=1, source_target_pairs={{33,0},{34,1},{35,2},{36,3},{37,4},{38,5},{39,6},{40,7},{41,8},{42... | collective-permute-start | bytes 589832 | tf_op jit(solution)/shard_map/ppermute | solution.py:24
  143.7 3.1 collective-permute-start.5
  146.8 3.2 collective-permute-start.3
  150.1 1.9 collective-permute-start.4
  152.0 2.4 maximum_maximum_fusion.1
  154.4 13.4 %shard_map.102 = (bf16[4,128,1536]{2,1,0:T(8,128)(2,1)}, f32[12,128,1]{2,1,0:T(8,128)}, f32[12,128,1]{2,1,0:T(8,128)}) custom-call(s32[3,12]{1,0:T(4,128)} %pad_add_fusion.reach_ref, bf16[4,128,1536]{2,1,0:T(8,128)(2,1)} %bitcast.34, bf16[4,128,1536]{2,1,0:T(8,128)(2,1)} %bitcast.35, bf16[2,512,1536]{2,1,0:T(8,128)(2,1)} %bitcast.40, ...), custom_call_target="tpu_custom_call" | custom-call | tf_op jit(solution)/shard_map/pallas_call | solution.py:177
  167.7 1.4 reduce
  169.1 1.4 reduce.1
  170.5 0.1 stack.46
  170.6 0.1 stack.45
  170.8 2.9 collective-permute-start.2
  173.7 2.7 collective-permute-start.1
  176.4 4.7 %collective-permute-start.6 = (bf16[2,1,2,32,1536]{4,3,2,1,0:T(8,128)(2,1)S(1)}, bf16[2,1,2,32,1536]{4,3,2,1,0:T(8,128)(2,1)S(1)}, u32[]{:S(2)}, u32[]{:S(2)}) collective-permute-start(bf16[2,1,2,32,1536]{4,3,2,1,0:T(8,128)(2,1)S(1)} %get-tuple-element.35), channel_id=1, source_target_pairs={{32,0},{33,1},{34,2},{35,3},{36,4},{37,5},{38,6},{39,7},{40,8},{41... | collective-permute-start | bytes 1179656 | tf_op jit(solution)/shard_map/ppermute | solution.py:24
  181.2 3.1 collective-permute-start.16
  184.3 4.5 %collective-permute-start.23 = (f32[2,12,1,1,32]{4,3,2,0,1:T(1,128)S(1)}, f32[2,12,1,1,32]{4,3,2,0,1:T(1,128)S(1)}, u32[]{:S(2)}, u32[]{:S(2)}) collective-permute-start(f32[2,12,1,1,32]{4,3,2,0,1:T(1,128)S(1)} %get-tuple-element.39), channel_id=1, source_target_pairs={{33,0},{34,1},{35,2},{36,3},{37,4},{38,5},{39,6},{40,7},{41,8},{42... | collective-permute-start | bytes 9224 | tf_op jit(solution)/shard_map/ppermute | solution.py:24
  188.9 3.6 %collective-permute-start.21 = (f32[2,12,1,1,32]{4,3,2,0,1:T(1,128)S(1)}, f32[2,12,1,1,32]{4,3,2,0,1:T(1,128)S(1)}, u32[]{:S(2)}, u32[]{:S(2)}) collective-permute-start(f32[2,12,1,1,32]{4,3,2,0,1:T(1,128)S(1)} %get-tuple-element.40), channel_id=1, source_target_pairs={{32,1},{33,2},{34,3},{35,4},{36,5},{37,6},{38,7},{39,8},{40,9},{41... | collective-permute-start | bytes 9224 | tf_op jit(solution)/shard_map/ppermute | solution.py:24
  192.5 2.0 collective-permute-start.18
  194.5 6.6 %collective-permute-start.19 = (f32[2,12,2,1,32]{4,3,2,0,1:T(1,128)S(1)}, f32[2,12,2,1,32]{4,3,2,0,1:T(1,128)S(1)}, u32[]{:S(2)}, u32[]{:S(2)}) collective-permute-start(f32[2,12,2,1,32]{4,3,2,0,1:T(1,128)S(1)} %get-tuple-element.44), channel_id=1, source_target_pairs={{0,1},{1,2},{2,3},{3,4},{4,5},{5,6},{6,7},{7,8},{8,9},{9,10},{10,1... | collective-permute-start | bytes 18440 | tf_op jit(solution)/shard_map/ppermute | solution.py:24
  201.2 1.9 collective-permute-start.20
  203.1 1.9 collective-permute-start.17
  205.0 5.5 %collective-permute-start.22 = (f32[2,12,1,2,32]{4,3,2,0,1:T(2,128)S(1)}, f32[2,12,1,2,32]{4,3,2,0,1:T(2,128)S(1)}, u32[]{:S(2)}, u32[]{:S(2)}) collective-permute-start(f32[2,12,1,2,32]{4,3,2,0,1:T(2,128)S(1)} %get-tuple-element.43), channel_id=1, source_target_pairs={{32,0},{33,1},{34,2},{35,3},{36,4},{37,5},{38,6},{39,7},{40,8},{41... | collective-permute-start | bytes 18440 | tf_op jit(solution)/shard_map/ppermute | solution.py:24
  210.5 3.4 %maximum_maximum_fusion = bf16[2,4,4,32,1536]{4,3,2,1,0:T(8,128)(2,1)} fusion(bf16[2,1,1,32,1536]{4,3,2,1,0:T(8,128)(2,1)} %collective-permute-done.7, bf16[2,1,2,32,1536]{4,3,2,1,0:T(8,128)(2,1)S(1)} %collective-permute-done.6, bf16[2,1,1,32,1536]{4,3,2,1,0:T(8,128)(2,1)} %collective-permute-done.5, ...), kind=kLoop, calls=%fused_computation | loop fusion | flops 12582912 | bytes 6291456 | tf_op jit(solution)/shard_map/concatenate | solution.py:52
  213.9 0.2 maximum_maximum_fusion.2
  214.1 0.2 reshape.172
  214.3 0.7 copy.45.lse_ref.dot_ref
  214.9 11.5 %shard_map.103 = bf16[4,128,1536]{2,1,0:T(8,128)(2,1)} custom-call(s32[3,12]{1,0:T(4,128)} %pad_add_fusion.reach_ref, bf16[4,128,1536]{2,1,0:T(8,128)(2,1)} %bitcast.36, bf16[4,128,1536]{2,1,0:T(8,128)(2,1)} %bitcast.37, bf16[2,512,1536]{2,1,0:T(8,128)(2,1)} %bitcast.38, bf16[2,512,1536]{2,1,0:T(8,128)(2,1)} %bitcast.39, ...), custom_call_target="tpu_custom_call", output_to_operand_aliasing={{}: (8, {})} | custom-call | tf_op jit(solution)/shard_map/pallas_call | solution.py:197
  226.4 3.0 copy.36
  229.5 92.8 %all_to_all.30 = bf16[4,2,2,32,1536]{4,2,1,0,3:T(2,128)(2,1)S(1)} all-to-all(bf16[4,2,2,32,1536]{4,2,1,0,3:T(2,128)(2,1)S(1)} %copy.36), channel_id=1, replica_groups=mesh['tm'=32,'ulysses'=32] {'ulysses'}, dimensions={3} | all-to-all | bytes 3145728 | tf_op jit(solution)/shard_map/all_to_all | solution.py:211
  322.2 1.1 fusion.5
  323.3 0.3 copy.40
  323.6 0.8 copy.44
  324.4 0.3 copy.39
  324.7 0.8 copy.43
  325.5 0.3 copy.38
  325.8 0.8 copy.42
  326.6 0.3 copy.37
  326.9 0.8 copy.41
  (34 shorter events, 0.2 us)
Async XLA Ops:
  4.5 23.5 %copy-start.1 = (s32[12]{0:T(128)S(1)}, s32[12]{0:T(128)}, u32[]{:S(2)}) copy-start(s32[12]{0:T(128)} %param.13) | copy-start | bytes 148
  4.5 23.5 %copy-start.2 = (s32[12]{0:T(128)S(1)}, s32[12]{0:T(128)}, u32[]{:S(2)}) copy-start(s32[12]{0:T(128)} %param.12) | copy-start | bytes 148
  4.5 23.5 %copy-start.3 = (s32[12]{0:T(128)S(1)}, s32[12]{0:T(128)}, u32[]{:S(2)}) copy-start(s32[12]{0:T(128)} %param.11) | copy-start | bytes 148
  7.8 97.4 %all-to-all-start = ((bf16[4,2,64,1,1536]{4,1,3,0,2:T(2,128)(2,1)}), bf16[4,2,64,1,1536]{4,1,3,0,2:T(2,128)(2,1)S(1)}, u32[]{:S(2)}, u32[]{:S(2)}) async-start(bf16[4,2,64,1,1536]{4,1,3,0,2:T(2,128)(2,1)} %pad_maximum_fusion), calls=%async_computation | async-start | bytes 3145728 | tf_op jit(solution)/shard_map/all_to_all | solution.py:144
  106.1 1.1 copy-start
  107.3 17.7 %collective-permute-start.8 = (bf16[2,1,1,32,1536]{4,3,2,1,0:T(8,128)(2,1)S(1)}, bf16[2,1,1,32,1536]{4,3,2,1,0:T(8,128)(2,1)S(1)}, u32[]{:S(2)}, u32[]{:S(2)}) collective-permute-start(bf16[2,1,1,32,1536]{4,3,2,1,0:T(8,128)(2,1)S(1)} %get-tuple-element.22), channel_id=1, source_target_pairs={{0,33},{1,34},{2,35},{3,36},{4,37},{5,38},{6,39},{7,40},{8,41},{9,... | collective-permute-start | bytes 589832 | tf_op jit(solution)/shard_map/ppermute | solution.py:24
  109.7 17.2 %collective-permute-start.15 = (bf16[2,1,1,32,1536]{4,3,2,1,0:T(8,128)(2,1)S(1)}, bf16[2,1,1,32,1536]{4,3,2,1,0:T(8,128)(2,1)S(1)}, u32[]{:S(2)}, u32[]{:S(2)}) collective-permute-start(bf16[2,1,1,32,1536]{4,3,2,1,0:T(8,128)(2,1)S(1)} %get-tuple-element.23), channel_id=1, source_target_pairs={{33,0},{34,1},{35,2},{36,3},{37,4},{38,5},{39,6},{40,7},{41,8},{42... | collective-permute-start | bytes 589832 | tf_op jit(solution)/shard_map/ppermute | solution.py:24
  115.0 13.9 %collective-permute-start.13 = (bf16[2,1,1,32,1536]{4,3,2,1,0:T(8,128)(2,1)S(1)}, bf16[2,1,1,32,1536]{4,3,2,1,0:T(8,128)(2,1)S(1)}, u32[]{:S(2)}, u32[]{:S(2)}) collective-permute-start(bf16[2,1,1,32,1536]{4,3,2,1,0:T(8,128)(2,1)S(1)} %get-tuple-element.24), channel_id=1, source_target_pairs={{32,1},{33,2},{34,3},{35,4},{36,5},{37,6},{38,7},{39,8},{40,9},{41... | collective-permute-start | bytes 589832 | tf_op jit(solution)/shard_map/ppermute | solution.py:24
  119.3 16.0 %collective-permute-start.10 = (bf16[2,1,1,32,1536]{4,3,2,1,0:T(8,128)(2,1)S(1)}, bf16[2,1,1,32,1536]{4,3,2,1,0:T(8,128)(2,1)S(1)}, u32[]{:S(2)}, u32[]{:S(2)}) collective-permute-start(bf16[2,1,1,32,1536]{4,3,2,1,0:T(8,128)(2,1)S(1)} %get-tuple-element.25), channel_id=1, source_target_pairs={{1,32},{2,33},{3,34},{4,35},{5,36},{6,37},{7,38},{8,39},{9,40},{10... | collective-permute-start | bytes 589832 | tf_op jit(solution)/shard_map/ppermute | solution.py:24
  121.4 15.8 %collective-permute-start.11 = (bf16[2,2,1,32,1536]{4,3,2,1,0:T(8,128)(2,1)S(1)}, bf16[2,2,1,32,1536]{4,3,2,1,0:T(8,128)(2,1)S(1)}, u32[]{:S(2)}, u32[]{:S(2)}) collective-permute-start(bf16[2,2,1,32,1536]{4,3,2,1,0:T(8,128)(2,1)S(1)} %get-tuple-element.28), channel_id=1, source_target_pairs={{0,1},{1,2},{2,3},{3,4},{4,5},{5,6},{6,7},{7,8},{8,9},{9,10},{10,1... | collective-permute-start | bytes 1179656 | tf_op jit(solution)/shard_map/ppermute | solution.py:24
  125.0 18.6 %collective-permute-start.12 = (bf16[2,2,1,32,1536]{4,3,2,1,0:T(8,128)(2,1)S(1)}, bf16[2,2,1,32,1536]{4,3,2,1,0:T(8,128)(2,1)S(1)}, u32[]{:S(2)}, u32[]{:S(2)}) collective-permute-start(bf16[2,2,1,32,1536]{4,3,2,1,0:T(8,128)(2,1)S(1)} %get-tuple-element.29), channel_id=1, source_target_pairs={{1,0},{2,1},{3,2},{4,3},{5,4},{6,5},{7,6},{8,7},{9,8},{10,9},{11,1... | collective-permute-start | bytes 1179656 | tf_op jit(solution)/shard_map/ppermute | solution.py:24
  127.0 19.8 %collective-permute-start.9 = (bf16[2,1,2,32,1536]{4,3,2,1,0:T(8,128)(2,1)S(1)}, bf16[2,1,2,32,1536]{4,3,2,1,0:T(8,128)(2,1)S(1)}, u32[]{:S(2)}, u32[]{:S(2)}) collective-permute-start(bf16[2,1,2,32,1536]{4,3,2,1,0:T(8,128)(2,1)S(1)} %get-tuple-element.26), channel_id=1, source_target_pairs={{0,32},{1,33},{2,34},{3,35},{4,36},{5,37},{6,38},{7,39},{8,40},{9,... | collective-permute-start | bytes 1179656 | tf_op jit(solution)/shard_map/ppermute | solution.py:24
  128.9 21.1 %collective-permute-start.14 = (bf16[2,1,2,32,1536]{4,3,2,1,0:T(8,128)(2,1)S(1)}, bf16[2,1,2,32,1536]{4,3,2,1,0:T(8,128)(2,1)S(1)}, u32[]{:S(2)}, u32[]{:S(2)}) collective-permute-start(bf16[2,1,2,32,1536]{4,3,2,1,0:T(8,128)(2,1)S(1)} %get-tuple-element.27), channel_id=1, source_target_pairs={{32,0},{33,1},{34,2},{35,3},{36,4},{37,5},{38,6},{39,7},{40,8},{41... | collective-permute-start | bytes 1179656 | tf_op jit(solution)/shard_map/ppermute | solution.py:24
  135.3 35.5 %collective-permute-start = (bf16[2,1,1,32,1536]{4,3,2,1,0:T(8,128)(2,1)}, bf16[2,1,1,32,1536]{4,3,2,1,0:T(8,128)(2,1)}, u32[]{:S(2)}, u32[]{:S(2)}) collective-permute-start(bf16[2,1,1,32,1536]{4,3,2,1,0:T(8,128)(2,1)} %get-tuple-element.30), channel_id=1, source_target_pairs={{0,33},{1,34},{2,35},{3,36},{4,37},{5,38},{6,39},{7,40},{8,41},{9,... | collective-permute-start | bytes 589832 | tf_op jit(solution)/shard_map/ppermute | solution.py:24
  137.2 36.4 %collective-permute-start.7 = (bf16[2,1,1,32,1536]{4,3,2,1,0:T(8,128)(2,1)}, bf16[2,1,1,32,1536]{4,3,2,1,0:T(8,128)(2,1)}, u32[]{:S(2)}, u32[]{:S(2)}) collective-permute-start(bf16[2,1,1,32,1536]{4,3,2,1,0:T(8,128)(2,1)} %get-tuple-element.31), channel_id=1, source_target_pairs={{33,0},{34,1},{35,2},{36,3},{37,4},{38,5},{39,6},{40,7},{41,8},{42... | collective-permute-start | bytes 589832 | tf_op jit(solution)/shard_map/ppermute | solution.py:24
  143.7 32.7 %collective-permute-start.5 = (bf16[2,1,1,32,1536]{4,3,2,1,0:T(8,128)(2,1)}, bf16[2,1,1,32,1536]{4,3,2,1,0:T(8,128)(2,1)}, u32[]{:S(2)}, u32[]{:S(2)}) collective-permute-start(bf16[2,1,1,32,1536]{4,3,2,1,0:T(8,128)(2,1)} %get-tuple-element.32), channel_id=1, source_target_pairs={{32,1},{33,2},{34,3},{35,4},{36,5},{37,6},{38,7},{39,8},{40,9},{41... | collective-permute-start | bytes 589832 | tf_op jit(solution)/shard_map/ppermute | solution.py:24
  146.8 37.5 %collective-permute-start.3 = (bf16[2,2,1,32,1536]{4,3,2,1,0:T(8,128)(2,1)}, bf16[2,2,1,32,1536]{4,3,2,1,0:T(8,128)(2,1)S(1)}, u32[]{:S(2)}, u32[]{:S(2)}) collective-permute-start(bf16[2,2,1,32,1536]{4,3,2,1,0:T(8,128)(2,1)} %get-tuple-element.36), channel_id=1, source_target_pairs={{0,1},{1,2},{2,3},{3,4},{4,5},{5,6},{6,7},{7,8},{8,9},{9,10},{10,1... | collective-permute-start | bytes 1179656 | tf_op jit(solution)/shard_map/ppermute | solution.py:24
  150.1 38.8 %collective-permute-start.4 = (bf16[2,2,1,32,1536]{4,3,2,1,0:T(8,128)(2,1)S(1)}, bf16[2,2,1,32,1536]{4,3,2,1,0:T(8,128)(2,1)S(1)}, u32[]{:S(2)}, u32[]{:S(2)}) collective-permute-start(bf16[2,2,1,32,1536]{4,3,2,1,0:T(8,128)(2,1)S(1)} %get-tuple-element.37), channel_id=1, source_target_pairs={{1,0},{2,1},{3,2},{4,3},{5,4},{6,5},{7,6},{8,7},{9,8},{10,9},{11,1... | collective-permute-start | bytes 1179656 | tf_op jit(solution)/shard_map/ppermute | solution.py:24
  170.8 10.4 %collective-permute-start.2 = (bf16[2,1,1,32,1536]{4,3,2,1,0:T(8,128)(2,1)}, bf16[2,1,1,32,1536]{4,3,2,1,0:T(8,128)(2,1)S(1)}, u32[]{:S(2)}, u32[]{:S(2)}) collective-permute-start(bf16[2,1,1,32,1536]{4,3,2,1,0:T(8,128)(2,1)} %get-tuple-element.33), channel_id=1, source_target_pairs={{1,32},{2,33},{3,34},{4,35},{5,36},{6,37},{7,38},{8,39},{9,40},{10... | collective-permute-start | bytes 589832 | tf_op jit(solution)/shard_map/ppermute | solution.py:24
  173.7 18.8 %collective-permute-start.1 = (bf16[2,1,2,32,1536]{4,3,2,1,0:T(8,128)(2,1)S(1)}, bf16[2,1,2,32,1536]{4,3,2,1,0:T(8,128)(2,1)S(1)}, u32[]{:S(2)}, u32[]{:S(2)}) collective-permute-start(bf16[2,1,2,32,1536]{4,3,2,1,0:T(8,128)(2,1)S(1)} %get-tuple-element.34), channel_id=1, source_target_pairs={{0,32},{1,33},{2,34},{3,35},{4,36},{5,37},{6,38},{7,39},{8,40},{9,... | collective-permute-start | bytes 1179656 | tf_op jit(solution)/shard_map/ppermute | solution.py:24
  176.4 18.1 %collective-permute-start.6 = (bf16[2,1,2,32,1536]{4,3,2,1,0:T(8,128)(2,1)S(1)}, bf16[2,1,2,32,1536]{4,3,2,1,0:T(8,128)(2,1)S(1)}, u32[]{:S(2)}, u32[]{:S(2)}) collective-permute-start(bf16[2,1,2,32,1536]{4,3,2,1,0:T(8,128)(2,1)S(1)} %get-tuple-element.35), channel_id=1, source_target_pairs={{32,0},{33,1},{34,2},{35,3},{36,4},{37,5},{38,6},{39,7},{40,8},{41... | collective-permute-start | bytes 1179656 | tf_op jit(solution)/shard_map/ppermute | solution.py:24
  181.2 20.0 %collective-permute-start.16 = (f32[2,12,1,1,32]{4,3,2,0,1:T(1,128)S(1)}, f32[2,12,1,1,32]{4,3,2,0,1:T(1,128)S(1)}, u32[]{:S(2)}, u32[]{:S(2)}) collective-permute-start(f32[2,12,1,1,32]{4,3,2,0,1:T(1,128)S(1)} %get-tuple-element.38), channel_id=1, source_target_pairs={{0,33},{1,34},{2,35},{3,36},{4,37},{5,38},{6,39},{7,40},{8,41},{9,... | collective-permute-start | bytes 9224 | tf_op jit(solution)/shard_map/ppermute | solution.py:24
  184.3 18.8 %collective-permute-start.23 = (f32[2,12,1,1,32]{4,3,2,0,1:T(1,128)S(1)}, f32[2,12,1,1,32]{4,3,2,0,1:T(1,128)S(1)}, u32[]{:S(2)}, u32[]{:S(2)}) collective-permute-start(f32[2,12,1,1,32]{4,3,2,0,1:T(1,128)S(1)} %get-tuple-element.39), channel_id=1, source_target_pairs={{33,0},{34,1},{35,2},{36,3},{37,4},{38,5},{39,6},{40,7},{41,8},{42... | collective-permute-start | bytes 9224 | tf_op jit(solution)/shard_map/ppermute | solution.py:24
  188.9 16.2 %collective-permute-start.21 = (f32[2,12,1,1,32]{4,3,2,0,1:T(1,128)S(1)}, f32[2,12,1,1,32]{4,3,2,0,1:T(1,128)S(1)}, u32[]{:S(2)}, u32[]{:S(2)}) collective-permute-start(f32[2,12,1,1,32]{4,3,2,0,1:T(1,128)S(1)} %get-tuple-element.40), channel_id=1, source_target_pairs={{32,1},{33,2},{34,3},{35,4},{36,5},{37,6},{38,7},{39,8},{40,9},{41... | collective-permute-start | bytes 9224 | tf_op jit(solution)/shard_map/ppermute | solution.py:24
  192.5 21.4 %collective-permute-start.18 = (f32[2,12,1,1,32]{4,3,2,0,1:T(1,128)S(1)}, f32[2,12,1,1,32]{4,3,2,0,1:T(1,128)S(1)}, u32[]{:S(2)}, u32[]{:S(2)}) collective-permute-start(f32[2,12,1,1,32]{4,3,2,0,1:T(1,128)S(1)} %get-tuple-element.41), channel_id=1, source_target_pairs={{1,32},{2,33},{3,34},{4,35},{5,36},{6,37},{7,38},{8,39},{9,40},{10... | collective-permute-start | bytes 9224 | tf_op jit(solution)/shard_map/ppermute | solution.py:24
  194.5 19.4 %collective-permute-start.19 = (f32[2,12,2,1,32]{4,3,2,0,1:T(1,128)S(1)}, f32[2,12,2,1,32]{4,3,2,0,1:T(1,128)S(1)}, u32[]{:S(2)}, u32[]{:S(2)}) collective-permute-start(f32[2,12,2,1,32]{4,3,2,0,1:T(1,128)S(1)} %get-tuple-element.44), channel_id=1, source_target_pairs={{0,1},{1,2},{2,3},{3,4},{4,5},{5,6},{6,7},{7,8},{8,9},{9,10},{10,1... | collective-permute-start | bytes 18440 | tf_op jit(solution)/shard_map/ppermute | solution.py:24
  201.2 12.7 %collective-permute-start.20 = (f32[2,12,2,1,32]{4,3,2,0,1:T(1,128)S(1)}, f32[2,12,2,1,32]{4,3,2,0,1:T(1,128)S(1)}, u32[]{:S(2)}, u32[]{:S(2)}) collective-permute-start(f32[2,12,2,1,32]{4,3,2,0,1:T(1,128)S(1)} %get-tuple-element.45), channel_id=1, source_target_pairs={{1,0},{2,1},{3,2},{4,3},{5,4},{6,5},{7,6},{8,7},{9,8},{10,9},{11,1... | collective-permute-start | bytes 18440 | tf_op jit(solution)/shard_map/ppermute | solution.py:24
  203.1 10.8 %collective-permute-start.17 = (f32[2,12,1,2,32]{4,3,2,0,1:T(2,128)S(1)}, f32[2,12,1,2,32]{4,3,2,0,1:T(2,128)S(1)}, u32[]{:S(2)}, u32[]{:S(2)}) collective-permute-start(f32[2,12,1,2,32]{4,3,2,0,1:T(2,128)S(1)} %get-tuple-element.42), channel_id=1, source_target_pairs={{0,32},{1,33},{2,34},{3,35},{4,36},{5,37},{6,38},{7,39},{8,40},{9,... | collective-permute-start | bytes 18440 | tf_op jit(solution)/shard_map/ppermute | solution.py:24
  205.0 8.9 %collective-permute-start.22 = (f32[2,12,1,2,32]{4,3,2,0,1:T(2,128)S(1)}, f32[2,12,1,2,32]{4,3,2,0,1:T(2,128)S(1)}, u32[]{:S(2)}, u32[]{:S(2)}) collective-permute-start(f32[2,12,1,2,32]{4,3,2,0,1:T(2,128)S(1)} %get-tuple-element.43), channel_id=1, source_target_pairs={{32,0},{33,1},{34,2},{35,3},{36,4},{37,5},{38,6},{39,7},{40,8},{41... | collective-permute-start | bytes 18440 | tf_op jit(solution)/shard_map/ppermute | solution.py:24

commit v2 on v0

--- a/solution.py
+++ b/solution.py
@@ -10,6 +10,7 @@
 DH = 128
 HEADS = 12
 TW = 8
+CHUNKS = 2
 
 
 def with_halo(array, sides, width):
@@ -104,18 +105,12 @@
     return kernel
 
 
-def body(queries, key_vectors, value_vectors, out_cotangent, reach_time, reach_height, reach_width):
-    lane_count = lax.axis_size("ulysses")
-    band_index = lax.axis_index("ulysses")
-    time_index = lax.axis_index("tm")
-    time_count = lax.axis_size("tm")
-    frames_dev, height = queries.shape[0], queries.shape[1]
-    rows_dev = height // lane_count
-    features = queries.shape[3]
+def attend(stacked, reach, time_index, band_index, time_count, height):
+    frames_dev = stacked.shape[1]
+    features = stacked.shape[4]
     heads = features // DH
-    stacked = jnp.stack([queries, key_vectors, value_vectors, out_cotangent])
     own = lax.all_to_all(stacked, "ulysses", split_axis=2, concat_axis=3, tiled=True)
-    col_count = own.shape[3]
+    rows_dev, col_count = own.shape[2], own.shape[3]
     rim = with_halo(own, (("tm", 1), ("ulysses", 2)), 1)
     rim_frames, rim_rows = frames_dev + 2, rows_dev + 2
     own_n = frames_dev * rows_dev * col_count
@@ -133,7 +128,6 @@
         & (row_of >= 0)
         & (row_of < height)
     ).astype(jnp.int32).reshape(1, rim_n)
-    reach = jnp.stack([reach_time, reach_height, reach_width]).astype(jnp.int32)
 
     def own_spec(which):
         return pl.BlockSpec((None, own_n, DH), lambda h, r: (which, 0, h))
@@ -187,6 +181,25 @@
     return (og_back[0], og_back[1], gkv_back[0], gkv_back[1])
 
 
+def body(queries, key_vectors, value_vectors, out_cotangent, reach_time, reach_height, reach_width):
+    band_index = lax.axis_index("ulysses")
+    time_index = lax.axis_index("tm")
+    time_count = lax.axis_size("tm")
+    height = queries.shape[1]
+    features = queries.shape[3]
+    heads = features // DH
+    chunk_heads = heads // CHUNKS
+    width = chunk_heads * DH
+    reach = jnp.stack([reach_time, reach_height, reach_width]).astype(jnp.int32)
+    stacked = jnp.stack([queries, key_vectors, value_vectors, out_cotangent])
+    pieces = []
+    for chunk in range(CHUNKS):
+        part = lax.slice_in_dim(stacked, chunk * width, (chunk + 1) * width, axis=4)
+        part_reach = lax.slice_in_dim(reach, chunk * chunk_heads, (chunk + 1) * chunk_heads, axis=1)
+        pieces.append(attend(part, part_reach, time_index, band_index, time_count, height))
+    return tuple(jnp.concatenate([piece[i] for piece in pieces], axis=3) for i in range(4))
+
+
 def solution(mesh):
     in_specs = (
         P("tm", None, "ulysses", None),

time: 297 us -> 314 us (1.057)
  starting transfers between devices: 40.7 us -> 87.8 us
  blocking collectives: 98.8 us -> 64.9 us
  waiting for transfers between devices: 101 us -> 92.8 us
  local copies, waits for them, and re-layouts: 18 us -> 24.4 us
  Pallas kernels: 24.9 us -> 28.8 us
    all_to_all x1, blocking collectives: 98.8 us -> 64.9 us  [attend(): lax.all_to_all(stacked, 'ulysses', split_axis=2, concat_axis=3, tiled=True)]
    all_to_all x0 -> x1, waiting for transfers between devices: none -> 20.3 us  [attend(): lax.all_to_all(stacked, 'ulysses', split_axis=2, concat_axis=3, tiled=True)]
    all_to_all x2 -> x4, starting transfers between devices: 19.4 us -> 39.3 us  [back_to_columns(): lax.all_to_all(shaped, 'ulysses', split_axis=3, concat_axis=2, tiled=True)]
    ppermute x4 -> x8, starting transfers between devices: 12.9 us -> 31.4 us  [with_halo(): before = lax.ppermute(last, axis, up)]
    all_to_all x2 -> x4, waiting for transfers between devices: 41.9 us -> 24.1 us  [back_to_columns(): lax.all_to_all(shaped, 'ulysses', split_axis=3, concat_axis=2, tiled=True)]
    ppermute x4 -> x8, waiting for transfers between devices: 41.4 us -> 26.9 us  [with_halo(): before = lax.ppermute(last, axis, up)]
    ppermute x4 -> x8, starting transfers between devices: 8.37 us -> 13 us  [with_halo(): after = lax.ppermute(initial, axis, down)]
    all_to_all x0 -> x1, starting transfers between devices: none -> 4.07 us  [attend(): lax.all_to_all(stacked, 'ulysses', split_axis=2, concat_axis=3, tiled=True)]
  transfers between devices with their start and end apart: 10 -> 21, of which waited for: 8 -> 10; matrix products, arithmetic and copies ran while one was open for 3% -> 8% of each run, Pallas kernels for 4% -> 9%
where the time goes in v2:
time: 314 us; the launch traced here: 310 us
  waiting for transfers between devices  92.8 us (30%)
  starting transfers between devices  87.8 us (28%)
  blocking collectives  64.9 us (21%)
  Pallas kernels  28.8 us (9%)
  local copies, waits for them, and re-layouts  24.4 us (8%)
  other arithmetic  10.5 us (3%)
    all_to_all x1, blocking collectives, attend(): lax.all_to_all(stacked, 'ulysses', split_axis=2, concat_axis=3, tiled=True)  64.9 us
    all_to_all x4, starting transfers between devices, back_to_columns(): lax.all_to_all(shaped, 'ulysses', split_axis=3, concat_axis=2, tiled=True)  39.3 us
    ppermute x8, starting transfers between devices, with_halo(): before = lax.ppermute(last, axis, up)  31.4 us
    ppermute x8, waiting for transfers between devices, with_halo(): before = lax.ppermute(last, axis, up)  26.9 us
    all_to_all x4, waiting for transfers between devices, back_to_columns(): lax.all_to_all(shaped, 'ulysses', split_axis=3, concat_axis=2, tiled=True)  24.1 us
    ppermute x8, waiting for transfers between devices, with_halo(): after = lax.ppermute(initial, axis, down)  21.5 us
    all_to_all x1, waiting for transfers between devices, attend(): lax.all_to_all(stacked, 'ulysses', split_axis=2, concat_axis=3, tiled=True)  20.3 us
    pallas_call x2, Pallas kernels, attend(): pl.pallas_call(make_query_kernel(dims), grid_spec=pltpu.PrefetchScalarGri...  15.4 us
  transfers between devices with their start and end apart: 21, of which 10 were waited for; matrix products, arithmetic and copies ran while one was open for 8% of the time, Pallas kernels for 9%

profile of v2, /device:TPU:1, one launch (start us, length us, event | category | flops | bytes accessed | tf_op | source)
XLA Modules:
  0.0 310.4 jit_solution(8913621188785391635)
XLA Ops:
  0.7 2.0 copy_bitcast_fusion
  2.7 0.8 copy_bitcast_fusion.2
  3.5 2.4 pad_maximum_fusion.2
  5.9 2.0 fusion.6
  7.8 64.9 %all_to_all.96 = bf16[4,2,64,1,768]{4,1,3,0,2:T(2,128)(2,1)S(1)} all-to-all(bf16[4,2,64,1,768]{4,1,3,0,2:T(2,128)(2,1)S(1)} %get-tuple-element.22), channel_id=1, replica_groups=mesh['tm'=32,'ulysses'=32] {'ulysses'}, dimensions={2} | all-to-all | bytes 1572864 | tf_op jit(solution)/shard_map/all_to_all | solution.py:112
  72.7 4.1 %all-to-all-start.2 = ((bf16[4,2,64,1,768]{4,1,3,0,2:T(2,128)(2,1)}), bf16[4,2,64,1,768]{4,1,3,0,2:T(2,128)(2,1)S(1)}, u32[]{:S(2)}, u32[]{:S(2)}) async-start(bf16[4,2,64,1,768]{4,1,3,0,2:T(2,128)(2,1)} %get-tuple-element.23), calls=%async_computation.2 | async-start | bytes 1572864 | tf_op jit(solution)/shard_map/all_to_all | solution.py:112
  77.1 3.2 %collective-permute-start = (bf16[4,1,2,32,768]{4,3,2,1,0:T(8,128)(2,1)S(1)}, bf16[4,1,2,32,768]{4,3,2,1,0:T(8,128)(2,1)S(1)}, u32[]{:S(2)}, u32[]{:S(2)}) collective-permute-start(bf16[4,1,2,32,768]{4,3,2,1,0:T(8,128)(2,1)S(1)} %get-tuple-element.26), channel_id=1, source_target_pairs={{0,32},{32,64},{64,96},{96,128},{128,160},{160,192},{192,224},{224... | collective-permute-start | bytes 1179656 | tf_op jit(solution)/shard_map/ppermute | solution.py:23
  80.3 1.3 collective-permute-start.1
  81.6 6.8 %collective-permute-done = bf16[4,1,2,32,768]{4,3,2,1,0:T(8,128)(2,1)S(1)} collective-permute-done((bf16[4,1,2,32,768]{4,3,2,1,0:T(8,128)(2,1)S(1)}, bf16[4,1,2,32,768]{4,3,2,1,0:T(8,128)(2,1)S(1)}, u32[]{:S(2)}, u32[]{:S(2)}) %collective-permute-start) | collective-permute-done | bytes 393248 | tf_op jit(solution)/shard_map/ppermute | solution.py:23
  88.4 3.8 %collective-permute-done.1 = bf16[4,1,2,32,768]{4,3,2,1,0:T(8,128)(2,1)S(1)} collective-permute-done((bf16[4,1,2,32,768]{4,3,2,1,0:T(8,128)(2,1)S(1)}, bf16[4,1,2,32,768]{4,3,2,1,0:T(8,128)(2,1)S(1)}, u32[]{:S(2)}, u32[]{:S(2)}) %collective-permute-start.1) | collective-permute-done | bytes 393248 | tf_op jit(solution)/shard_map/ppermute | solution.py:24
  92.5 1.3 fusion.5
  93.7 4.7 %collective-permute-start.2 = (bf16[4,4,1,32,768]{4,3,2,1,0:T(8,128)(2,1)}, bf16[4,4,1,32,768]{4,3,2,1,0:T(8,128)(2,1)}, u32[]{:S(2)}, u32[]{:S(2)}) collective-permute-start(bf16[4,4,1,32,768]{4,3,2,1,0:T(8,128)(2,1)} %get-tuple-element.20), channel_id=1, source_target_pairs={{0,1},{1,2},{2,3},{3,4},{4,5},{5,6},{6,7},{7,8},{8,9},{9,10},{10,1... | collective-permute-start | bytes 2359304 | tf_op jit(solution)/shard_map/ppermute | solution.py:23
  98.4 1.9 collective-permute-start.3
  100.4 0.7 fusion.18
  101.1 20.3 %all-to-all-done.2 = bf16[4,2,64,1,768]{4,1,3,0,2:T(2,128)(2,1)S(1)} async-done(((bf16[4,2,64,1,768]{4,1,3,0,2:T(2,128)(2,1)}), bf16[4,2,64,1,768]{4,1,3,0,2:T(2,128)(2,1)S(1)}, u32[]{:S(2)}, u32[]{:S(2)}) %all-to-all-start.2) | async-done | bytes 786464 | tf_op jit(solution)/shard_map/all_to_all | solution.py:112
  121.6 0.9 fusion.9
  122.5 3.2 %collective-permute-start.4 = (bf16[4,1,2,32,768]{4,3,2,1,0:T(8,128)(2,1)}, bf16[4,1,2,32,768]{4,3,2,1,0:T(8,128)(2,1)S(1)}, u32[]{:S(2)}, u32[]{:S(2)}) collective-permute-start(bf16[4,1,2,32,768]{4,3,2,1,0:T(8,128)(2,1)} %get-tuple-element.30), channel_id=1, source_target_pairs={{0,32},{32,64},{64,96},{96,128},{128,160},{160,192},{192,224},{224... | collective-permute-start | bytes 1179656 | tf_op jit(solution)/shard_map/ppermute | solution.py:23
  125.8 1.3 collective-permute-start.5
  127.1 0.6 and_convert_fusion.live_ref
  127.7 3.0 pad_maximum_fusion
  130.7 7.7 %shard_map.102 = (bf16[2,128,768]{2,1,0:T(8,128)(2,1)}, f32[6,128,1]{2,1,0:T(8,128)}, f32[6,128,1]{2,1,0:T(8,128)}) custom-call(s32[3,6]{1,0:T(4,128)} %get-tuple-element.50.reach_ref, bf16[4,128,768]{2,1,0:T(8,128)(2,1)} %bitcast.75, bf16[4,128,768]{2,1,0:T(8,128)(2,1)} %bitcast.76, bf16[4,512,768]{2,1,0:T(8,128)(2,1)} %bitcast.61, ...), custom_call_target="tpu_custom_call" | custom-call | tf_op jit(solution)/shard_map/pallas_call | solution.py:142
  138.4 2.2 copy.50
  140.6 5.2 %all-to-all-start.1 = ((bf16[2,2,2,32,768]{4,2,1,0,3:T(2,128)(2,1)}), bf16[2,2,2,32,768]{4,2,1,0,3:T(2,128)(2,1)S(1)}, u32[]{:S(2)}, u32[]{:S(2)}) async-start(bf16[2,2,2,32,768]{4,2,1,0,3:T(2,128)(2,1)} %copy.50), calls=%async_computation.1 | async-start | bytes 786432 | tf_op jit(solution)/shard_map/all_to_all | solution.py:159
  146.2 3.5 %collective-permute-start.6 = (bf16[4,4,1,32,768]{4,3,2,1,0:T(8,128)(2,1)S(1)}, bf16[4,4,1,32,768]{4,3,2,1,0:T(8,128)(2,1)S(1)}, u32[]{:S(2)}, u32[]{:S(2)}) collective-permute-start(bf16[4,4,1,32,768]{4,3,2,1,0:T(8,128)(2,1)S(1)} %get-tuple-element.24), channel_id=1, source_target_pairs={{0,1},{1,2},{2,3},{3,4},{4,5},{5,6},{6,7},{7,8},{8,9},{9,10},{10,1... | collective-permute-start | bytes 2359304 | tf_op jit(solution)/shard_map/ppermute | solution.py:23
  149.7 1.9 collective-permute-start.7
  151.6 20.1 %collective-permute-done.6 = bf16[4,4,1,32,768]{4,3,2,1,0:T(8,128)(2,1)S(1)} collective-permute-done((bf16[4,4,1,32,768]{4,3,2,1,0:T(8,128)(2,1)S(1)}, bf16[4,4,1,32,768]{4,3,2,1,0:T(8,128)(2,1)S(1)}, u32[]{:S(2)}, u32[]{:S(2)}) %collective-permute-start.6) | collective-permute-done | bytes 786464 | tf_op jit(solution)/shard_map/ppermute | solution.py:23
  171.7 2.2 collective-permute-done.7
  173.9 1.9 pad_maximum_fusion.1
  175.7 7.7 %shard_map.103 = (bf16[2,128,768]{2,1,0:T(8,128)(2,1)}, f32[6,128,1]{2,1,0:T(8,128)}, f32[6,128,1]{2,1,0:T(8,128)}) custom-call(s32[3,6]{1,0:T(4,128)} %get-tuple-element.51.reach_ref, bf16[4,128,768]{2,1,0:T(8,128)(2,1)} %bitcast.68, bf16[4,128,768]{2,1,0:T(8,128)(2,1)} %bitcast.69, bf16[4,512,768]{2,1,0:T(8,128)(2,1)} %bitcast.57, ...), custom_call_target="tpu_custom_call" | custom-call | tf_op jit(solution)/shard_map/pallas_call | solution.py:142
  183.5 2.2 copy.53
  185.7 11.1 %all-to-all-start.3 = ((bf16[2,2,2,32,768]{4,2,1,0,3:T(2,128)(2,1)}), bf16[2,2,2,32,768]{4,2,1,0,3:T(2,128)(2,1)S(1)}, u32[]{:S(2)}, u32[]{:S(2)}) async-start(bf16[2,2,2,32,768]{4,2,1,0,3:T(2,128)(2,1)} %copy.53), calls=%async_computation.3 | async-start | bytes 786432 | tf_op jit(solution)/shard_map/all_to_all | solution.py:159
  197.4 4.0 %collective-permute-start.8 = (f32[2,6,1,2,32]{4,3,2,0,1:T(2,128)S(1)}, f32[2,6,1,2,32]{4,3,2,0,1:T(2,128)S(1)}, u32[]{:S(2)}, u32[]{:S(2)}) collective-permute-start(f32[2,6,1,2,32]{4,3,2,0,1:T(2,128)S(1)} %get-tuple-element.46), channel_id=1, source_target_pairs={{0,32},{32,64},{64,96},{96,128},{128,160},{160,192},{192,224},{224... | collective-permute-start | bytes 9224 | tf_op jit(solution)/shard_map/ppermute | solution.py:23
  201.3 1.3 collective-permute-start.9
  202.7 3.4 %collective-permute-done.9 = f32[2,6,1,2,32]{4,3,2,0,1:T(2,128)S(1)} collective-permute-done((f32[2,6,1,2,32]{4,3,2,0,1:T(2,128)S(1)}, f32[2,6,1,2,32]{4,3,2,0,1:T(2,128)S(1)}, u32[]{:S(2)}, u32[]{:S(2)}) %collective-permute-start.9) | collective-permute-done | bytes 3104 | tf_op jit(solution)/shard_map/ppermute | solution.py:24
  206.2 4.7 %collective-permute-start.10 = (f32[2,6,4,1,32]{4,3,2,0,1:T(1,128)S(1)}, f32[2,6,4,1,32]{4,3,2,0,1:T(1,128)S(1)}, u32[]{:S(2)}, u32[]{:S(2)}) collective-permute-start(f32[2,6,4,1,32]{4,3,2,0,1:T(1,128)S(1)} %get-tuple-element.42), channel_id=1, source_target_pairs={{0,1},{1,2},{2,3},{3,4},{4,5},{5,6},{6,7},{7,8},{8,9},{9,10},{10,1... | collective-permute-start | bytes 18440 | tf_op jit(solution)/shard_map/ppermute | solution.py:23
  210.8 2.1 collective-permute-start.11
  213.0 3.3 %collective-permute-done.11 = f32[2,6,4,1,32]{4,3,2,0,1:T(1,128)S(1)} collective-permute-done((f32[2,6,4,1,32]{4,3,2,0,1:T(1,128)S(1)}, f32[2,6,4,1,32]{4,3,2,0,1:T(1,128)S(1)}, u32[]{:S(2)}, u32[]{:S(2)}) %collective-permute-start.11) | collective-permute-done | bytes 6176 | tf_op jit(solution)/shard_map/ppermute | solution.py:24
  216.5 0.6 copy.69.lse_ref.dot_ref
  217.1 6.7 %shard_map.104 = bf16[2,128,768]{2,1,0:T(8,128)(2,1)} custom-call(s32[3,6]{1,0:T(4,128)} %get-tuple-element.50.reach_ref, bf16[4,128,768]{2,1,0:T(8,128)(2,1)} %bitcast.77, bf16[4,128,768]{2,1,0:T(8,128)(2,1)} %bitcast.78, bf16[4,512,768]{2,1,0:T(8,128)(2,1)} %bitcast.63, bf16[4,512,768]{2,1,0:T(8,128)(2,1)} %bitcast.64, ...), custom_call_target="tpu_custom_call" | custom-call | tf_op jit(solution)/shard_map/pallas_call | solution.py:168
  223.8 2.2 copy.58
  226.0 11.7 %all-to-all-start.4 = ((bf16[2,2,2,32,768]{4,2,1,0,3:T(2,128)(2,1)}), bf16[2,2,2,32,768]{4,2,1,0,3:T(2,128)(2,1)S(1)}, u32[]{:S(2)}, u32[]{:S(2)}) async-start(bf16[2,2,2,32,768]{4,2,1,0,3:T(2,128)(2,1)} %copy.58), calls=%async_computation.4 | async-start | bytes 786432 | tf_op jit(solution)/shard_map/all_to_all | solution.py:159
  238.3 3.7 %collective-permute-start.12 = (f32[2,6,1,2,32]{4,3,2,0,1:T(2,128)S(1)}, f32[2,6,1,2,32]{4,3,2,0,1:T(2,128)S(1)}, u32[]{:S(2)}, u32[]{:S(2)}) collective-permute-start(f32[2,6,1,2,32]{4,3,2,0,1:T(2,128)S(1)} %get-tuple-element.48), channel_id=1, source_target_pairs={{0,32},{32,64},{64,96},{96,128},{128,160},{160,192},{192,224},{224... | collective-permute-start | bytes 9224 | tf_op jit(solution)/shard_map/ppermute | solution.py:23
  242.0 1.3 collective-permute-start.13
  243.3 4.8 %collective-permute-done.13 = f32[2,6,1,2,32]{4,3,2,0,1:T(2,128)S(1)} collective-permute-done((f32[2,6,1,2,32]{4,3,2,0,1:T(2,128)S(1)}, f32[2,6,1,2,32]{4,3,2,0,1:T(2,128)S(1)}, u32[]{:S(2)}, u32[]{:S(2)}) %collective-permute-start.13) | collective-permute-done | bytes 3104 | tf_op jit(solution)/shard_map/ppermute | solution.py:24
  248.2 4.4 %collective-permute-start.14 = (f32[2,6,4,1,32]{4,3,2,0,1:T(1,128)S(1)}, f32[2,6,4,1,32]{4,3,2,0,1:T(1,128)S(1)}, u32[]{:S(2)}, u32[]{:S(2)}) collective-permute-start(f32[2,6,4,1,32]{4,3,2,0,1:T(1,128)S(1)} %get-tuple-element.44), channel_id=1, source_target_pairs={{0,1},{1,2},{2,3},{3,4},{4,5},{5,6},{6,7},{7,8},{8,9},{9,10},{10,1... | collective-permute-start | bytes 18440 | tf_op jit(solution)/shard_map/ppermute | solution.py:23
  252.6 1.9 collective-permute-start.15
  254.5 4.0 %collective-permute-done.15 = f32[2,6,4,1,32]{4,3,2,0,1:T(1,128)S(1)} collective-permute-done((f32[2,6,4,1,32]{4,3,2,0,1:T(1,128)S(1)}, f32[2,6,4,1,32]{4,3,2,0,1:T(1,128)S(1)}, u32[]{:S(2)}, u32[]{:S(2)}) %collective-permute-start.15) | collective-permute-done | bytes 6176 | tf_op jit(solution)/shard_map/ppermute | solution.py:24
  258.7 0.6 copy.70.lse_ref.dot_ref
  259.3 6.7 %shard_map.105 = bf16[2,128,768]{2,1,0:T(8,128)(2,1)} custom-call(s32[3,6]{1,0:T(4,128)} %get-tuple-element.51.reach_ref, bf16[4,128,768]{2,1,0:T(8,128)(2,1)} %bitcast.70, bf16[4,128,768]{2,1,0:T(8,128)(2,1)} %bitcast.71, bf16[4,512,768]{2,1,0:T(8,128)(2,1)} %bitcast.59, bf16[4,512,768]{2,1,0:T(8,128)(2,1)} %bitcast.60, ...), custom_call_target="tpu_custom_call" | custom-call | tf_op jit(solution)/shard_map/pallas_call | solution.py:168
  266.0 2.1 copy.61
  268.1 11.3 %all-to-all-start.5 = ((bf16[2,2,2,32,768]{4,2,1,0,3:T(2,128)(2,1)}), bf16[2,2,2,32,768]{4,2,1,0,3:T(2,128)(2,1)S(1)}, u32[]{:S(2)}, u32[]{:S(2)}) async-start(bf16[2,2,2,32,768]{4,2,1,0,3:T(2,128)(2,1)} %copy.61), calls=%async_computation.5 | async-start | bytes 786432 | tf_op jit(solution)/shard_map/all_to_all | solution.py:159
  279.4 0.3 fusion.12
  279.9 0.3 fusion.13
  280.3 0.3 pad_maximum_fusion.6
  280.7 0.8 copy.66
  281.8 0.3 pad_maximum_fusion.5
  282.1 0.8 copy.65
  282.9 0.3 fusion.10
  283.3 24.1 %all-to-all-done.5 = bf16[2,2,2,32,768]{4,2,1,0,3:T(2,128)(2,1)S(1)} async-done(((bf16[2,2,2,32,768]{4,2,1,0,3:T(2,128)(2,1)}), bf16[2,2,2,32,768]{4,2,1,0,3:T(2,128)(2,1)S(1)}, u32[]{:S(2)}, u32[]{:S(2)}) %all-to-all-start.5) | async-done | bytes 393248 | tf_op jit(solution)/shard_map/all_to_all | solution.py:159
  307.4 0.3 fusion.11
  307.9 0.3 pad_maximum_fusion.8
  308.2 0.8 copy.68
  309.3 0.3 pad_maximum_fusion.7
  309.7 0.8 copy.67
  (70 shorter events, 3.9 us)
Async XLA Ops:
  0.6 2.0 copy-start.7
  0.6 2.0 copy-start.6
  72.7 48.7 %all-to-all-start.2 = ((bf16[4,2,64,1,768]{4,1,3,0,2:T(2,128)(2,1)}), bf16[4,2,64,1,768]{4,1,3,0,2:T(2,128)(2,1)S(1)}, u32[]{:S(2)}, u32[]{:S(2)}) async-start(bf16[4,2,64,1,768]{4,1,3,0,2:T(2,128)(2,1)} %get-tuple-element.23), calls=%async_computation.2 | async-start | bytes 1572864 | tf_op jit(solution)/shard_map/all_to_all | solution.py:112
  77.0 50.7 %copy-start.1 = (bf16[4,2,32,2,1,768]{5,2,3,1,0,4:T(8,128)(2,1)}, bf16[4,2,32,2,1,768]{5,2,3,1,0,4:T(8,128)(2,1)S(1)}, u32[]{:S(2)}) copy-start(bf16[4,2,32,2,1,768]{5,2,3,1,0,4:T(8,128)(2,1)S(1)} %copy.80) | copy-start | bytes 2359300
  77.1 11.3 %collective-permute-start = (bf16[4,1,2,32,768]{4,3,2,1,0:T(8,128)(2,1)S(1)}, bf16[4,1,2,32,768]{4,3,2,1,0:T(8,128)(2,1)S(1)}, u32[]{:S(2)}, u32[]{:S(2)}) collective-permute-start(bf16[4,1,2,32,768]{4,3,2,1,0:T(8,128)(2,1)S(1)} %get-tuple-element.26), channel_id=1, source_target_pairs={{0,32},{32,64},{64,96},{96,128},{128,160},{160,192},{192,224},{224... | collective-permute-start | bytes 1179656 | tf_op jit(solution)/shard_map/ppermute | solution.py:23
  80.3 11.9 %collective-permute-start.1 = (bf16[4,1,2,32,768]{4,3,2,1,0:T(8,128)(2,1)S(1)}, bf16[4,1,2,32,768]{4,3,2,1,0:T(8,128)(2,1)S(1)}, u32[]{:S(2)}, u32[]{:S(2)}) collective-permute-start(bf16[4,1,2,32,768]{4,3,2,1,0:T(8,128)(2,1)S(1)} %get-tuple-element.27), channel_id=1, source_target_pairs={{32,0},{64,32},{96,64},{128,96},{160,128},{192,160},{224,192},{256... | collective-permute-start | bytes 1179656 | tf_op jit(solution)/shard_map/ppermute | solution.py:24
  92.4 7.9 %copy-start.8 = (s32[12]{0:T(128)S(1)}, s32[12]{0:T(128)}, u32[]{:S(2)}) copy-start(s32[12]{0:T(128)} %param.13) | copy-start | bytes 148
  92.4 7.9 %copy-start.9 = (s32[12]{0:T(128)S(1)}, s32[12]{0:T(128)}, u32[]{:S(2)}) copy-start(s32[12]{0:T(128)} %param.12) | copy-start | bytes 148
  92.5 7.9 %copy-start.10 = (s32[12]{0:T(128)S(1)}, s32[12]{0:T(128)}, u32[]{:S(2)}) copy-start(s32[12]{0:T(128)} %param.11) | copy-start | bytes 148
  93.7 33.9 %collective-permute-start.2 = (bf16[4,4,1,32,768]{4,3,2,1,0:T(8,128)(2,1)}, bf16[4,4,1,32,768]{4,3,2,1,0:T(8,128)(2,1)}, u32[]{:S(2)}, u32[]{:S(2)}) collective-permute-start(bf16[4,4,1,32,768]{4,3,2,1,0:T(8,128)(2,1)} %get-tuple-element.20), channel_id=1, source_target_pairs={{0,1},{1,2},{2,3},{3,4},{4,5},{5,6},{6,7},{7,8},{8,9},{9,10},{10,1... | collective-permute-start | bytes 2359304 | tf_op jit(solution)/shard_map/ppermute | solution.py:23
  98.4 29.2 %collective-permute-start.3 = (bf16[4,4,1,32,768]{4,3,2,1,0:T(8,128)(2,1)}, bf16[4,4,1,32,768]{4,3,2,1,0:T(8,128)(2,1)}, u32[]{:S(2)}, u32[]{:S(2)}) collective-permute-start(bf16[4,4,1,32,768]{4,3,2,1,0:T(8,128)(2,1)} %get-tuple-element.21), channel_id=1, source_target_pairs={{1,0},{2,1},{3,2},{4,3},{5,4},{6,5},{7,6},{8,7},{9,8},{10,9},{11,1... | collective-permute-start | bytes 2359304 | tf_op jit(solution)/shard_map/ppermute | solution.py:24
  121.6 52.3 %copy-start = (bf16[4,2,32,2,1,768]{5,2,3,1,0,4:T(8,128)(2,1)}, bf16[4,2,32,2,1,768]{5,2,3,1,0,4:T(8,128)(2,1)S(1)}, u32[]{:S(2)}) copy-start(bf16[4,2,32,2,1,768]{5,2,3,1,0,4:T(8,128)(2,1)S(1)} %copy.79) | copy-start | bytes 2359300
  122.5 23.3 %collective-permute-start.4 = (bf16[4,1,2,32,768]{4,3,2,1,0:T(8,128)(2,1)}, bf16[4,1,2,32,768]{4,3,2,1,0:T(8,128)(2,1)S(1)}, u32[]{:S(2)}, u32[]{:S(2)}) collective-permute-start(bf16[4,1,2,32,768]{4,3,2,1,0:T(8,128)(2,1)} %get-tuple-element.30), channel_id=1, source_target_pairs={{0,32},{32,64},{64,96},{96,128},{128,160},{160,192},{192,224},{224... | collective-permute-start | bytes 1179656 | tf_op jit(solution)/shard_map/ppermute | solution.py:23
  125.8 20.1 %collective-permute-start.5 = (bf16[4,1,2,32,768]{4,3,2,1,0:T(8,128)(2,1)S(1)}, bf16[4,1,2,32,768]{4,3,2,1,0:T(8,128)(2,1)S(1)}, u32[]{:S(2)}, u32[]{:S(2)}) collective-permute-start(bf16[4,1,2,32,768]{4,3,2,1,0:T(8,128)(2,1)S(1)} %get-tuple-element.31), channel_id=1, source_target_pairs={{32,0},{64,32},{96,64},{128,96},{160,128},{192,160},{224,192},{256... | collective-permute-start | bytes 1179656 | tf_op jit(solution)/shard_map/ppermute | solution.py:24
  140.6 45.1 %all-to-all-start.1 = ((bf16[2,2,2,32,768]{4,2,1,0,3:T(2,128)(2,1)}), bf16[2,2,2,32,768]{4,2,1,0,3:T(2,128)(2,1)S(1)}, u32[]{:S(2)}, u32[]{:S(2)}) async-start(bf16[2,2,2,32,768]{4,2,1,0,3:T(2,128)(2,1)} %copy.50), calls=%async_computation.1 | async-start | bytes 786432 | tf_op jit(solution)/shard_map/all_to_all | solution.py:159
  146.2 25.6 %collective-permute-start.6 = (bf16[4,4,1,32,768]{4,3,2,1,0:T(8,128)(2,1)S(1)}, bf16[4,4,1,32,768]{4,3,2,1,0:T(8,128)(2,1)S(1)}, u32[]{:S(2)}, u32[]{:S(2)}) collective-permute-start(bf16[4,4,1,32,768]{4,3,2,1,0:T(8,128)(2,1)S(1)} %get-tuple-element.24), channel_id=1, source_target_pairs={{0,1},{1,2},{2,3},{3,4},{4,5},{5,6},{6,7},{7,8},{8,9},{9,10},{10,1... | collective-permute-start | bytes 2359304 | tf_op jit(solution)/shard_map/ppermute | solution.py:23
  149.7 24.2 %collective-permute-start.7 = (bf16[4,4,1,32,768]{4,3,2,1,0:T(8,128)(2,1)S(1)}, bf16[4,4,1,32,768]{4,3,2,1,0:T(8,128)(2,1)S(1)}, u32[]{:S(2)}, u32[]{:S(2)}) collective-permute-start(bf16[4,4,1,32,768]{4,3,2,1,0:T(8,128)(2,1)S(1)} %get-tuple-element.25), channel_id=1, source_target_pairs={{1,0},{2,1},{3,2},{4,3},{5,4},{6,5},{7,6},{8,7},{9,8},{10,9},{11,1... | collective-permute-start | bytes 2359304 | tf_op jit(solution)/shard_map/ppermute | solution.py:24
  183.5 13.3 %copy-start.5 = (f32[6,128,1]{2,1,0:T(8,128)S(1)}, f32[6,128,1]{2,1,0:T(8,128)}, u32[]{:S(2)}) copy-start(f32[6,128,1]{2,1,0:T(8,128)} %get-tuple-element.12) | copy-start | bytes 9220
  183.5 13.6 %copy-start.4 = (f32[6,128,1]{2,1,0:T(8,128)S(1)}, f32[6,128,1]{2,1,0:T(8,128)}, u32[]{:S(2)}) copy-start(f32[6,128,1]{2,1,0:T(8,128)} %get-tuple-element.13) | copy-start | bytes 9220
  185.7 40.3 %all-to-all-start.3 = ((bf16[2,2,2,32,768]{4,2,1,0,3:T(2,128)(2,1)}), bf16[2,2,2,32,768]{4,2,1,0,3:T(2,128)(2,1)S(1)}, u32[]{:S(2)}, u32[]{:S(2)}) async-start(bf16[2,2,2,32,768]{4,2,1,0,3:T(2,128)(2,1)} %copy.53), calls=%async_computation.3 | async-start | bytes 786432 | tf_op jit(solution)/shard_map/all_to_all | solution.py:159
  197.4 5.3 %collective-permute-start.8 = (f32[2,6,1,2,32]{4,3,2,0,1:T(2,128)S(1)}, f32[2,6,1,2,32]{4,3,2,0,1:T(2,128)S(1)}, u32[]{:S(2)}, u32[]{:S(2)}) collective-permute-start(f32[2,6,1,2,32]{4,3,2,0,1:T(2,128)S(1)} %get-tuple-element.46), channel_id=1, source_target_pairs={{0,32},{32,64},{64,96},{96,128},{128,160},{160,192},{192,224},{224... | collective-permute-start | bytes 9224 | tf_op jit(solution)/shard_map/ppermute | solution.py:23
  201.3 4.7 %collective-permute-start.9 = (f32[2,6,1,2,32]{4,3,2,0,1:T(2,128)S(1)}, f32[2,6,1,2,32]{4,3,2,0,1:T(2,128)S(1)}, u32[]{:S(2)}, u32[]{:S(2)}) collective-permute-start(f32[2,6,1,2,32]{4,3,2,0,1:T(2,128)S(1)} %get-tuple-element.47), channel_id=1, source_target_pairs={{32,0},{64,32},{96,64},{128,96},{160,128},{192,160},{224,192},{256... | collective-permute-start | bytes 9224 | tf_op jit(solution)/shard_map/ppermute | solution.py:24
  206.2 6.8 %collective-permute-start.10 = (f32[2,6,4,1,32]{4,3,2,0,1:T(1,128)S(1)}, f32[2,6,4,1,32]{4,3,2,0,1:T(1,128)S(1)}, u32[]{:S(2)}, u32[]{:S(2)}) collective-permute-start(f32[2,6,4,1,32]{4,3,2,0,1:T(1,128)S(1)} %get-tuple-element.42), channel_id=1, source_target_pairs={{0,1},{1,2},{2,3},{3,4},{4,5},{5,6},{6,7},{7,8},{8,9},{9,10},{10,1... | collective-permute-start | bytes 18440 | tf_op jit(solution)/shard_map/ppermute | solution.py:23
  210.8 5.5 %collective-permute-start.11 = (f32[2,6,4,1,32]{4,3,2,0,1:T(1,128)S(1)}, f32[2,6,4,1,32]{4,3,2,0,1:T(1,128)S(1)}, u32[]{:S(2)}, u32[]{:S(2)}) collective-permute-start(f32[2,6,4,1,32]{4,3,2,0,1:T(1,128)S(1)} %get-tuple-element.43), channel_id=1, source_target_pairs={{1,0},{2,1},{3,2},{4,3},{5,4},{6,5},{7,6},{8,7},{9,8},{10,9},{11,1... | collective-permute-start | bytes 18440 | tf_op jit(solution)/shard_map/ppermute | solution.py:24
  223.8 14.0 %copy-start.3 = (f32[6,128,1]{2,1,0:T(8,128)S(1)}, f32[6,128,1]{2,1,0:T(8,128)}, u32[]{:S(2)}) copy-start(f32[6,128,1]{2,1,0:T(8,128)} %get-tuple-element.14) | copy-start | bytes 9220
  223.8 14.2 %copy-start.2 = (f32[6,128,1]{2,1,0:T(8,128)S(1)}, f32[6,128,1]{2,1,0:T(8,128)}, u32[]{:S(2)}) copy-start(f32[6,128,1]{2,1,0:T(8,128)} %get-tuple-element.15) | copy-start | bytes 9220
  226.0 42.1 %all-to-all-start.4 = ((bf16[2,2,2,32,768]{4,2,1,0,3:T(2,128)(2,1)}), bf16[2,2,2,32,768]{4,2,1,0,3:T(2,128)(2,1)S(1)}, u32[]{:S(2)}, u32[]{:S(2)}) async-start(bf16[2,2,2,32,768]{4,2,1,0,3:T(2,128)(2,1)} %copy.58), calls=%async_computation.4 | async-start | bytes 786432 | tf_op jit(solution)/shard_map/all_to_all | solution.py:159
  238.3 5.0 %collective-permute-start.12 = (f32[2,6,1,2,32]{4,3,2,0,1:T(2,128)S(1)}, f32[2,6,1,2,32]{4,3,2,0,1:T(2,128)S(1)}, u32[]{:S(2)}, u32[]{:S(2)}) collective-permute-start(f32[2,6,1,2,32]{4,3,2,0,1:T(2,128)S(1)} %get-tuple-element.48), channel_id=1, source_target_pairs={{0,32},{32,64},{64,96},{96,128},{128,160},{160,192},{192,224},{224... | collective-permute-start | bytes 9224 | tf_op jit(solution)/shard_map/ppermute | solution.py:23
  242.0 6.1 %collective-permute-start.13 = (f32[2,6,1,2,32]{4,3,2,0,1:T(2,128)S(1)}, f32[2,6,1,2,32]{4,3,2,0,1:T(2,128)S(1)}, u32[]{:S(2)}, u32[]{:S(2)}) collective-permute-start(f32[2,6,1,2,32]{4,3,2,0,1:T(2,128)S(1)} %get-tuple-element.49), channel_id=1, source_target_pairs={{32,0},{64,32},{96,64},{128,96},{160,128},{192,160},{224,192},{256... | collective-permute-start | bytes 9224 | tf_op jit(solution)/shard_map/ppermute | solution.py:24
  248.2 6.3 %collective-permute-start.14 = (f32[2,6,4,1,32]{4,3,2,0,1:T(1,128)S(1)}, f32[2,6,4,1,32]{4,3,2,0,1:T(1,128)S(1)}, u32[]{:S(2)}, u32[]{:S(2)}) collective-permute-start(f32[2,6,4,1,32]{4,3,2,0,1:T(1,128)S(1)} %get-tuple-element.44), channel_id=1, source_target_pairs={{0,1},{1,2},{2,3},{3,4},{4,5},{5,6},{6,7},{7,8},{8,9},{9,10},{10,1... | collective-permute-start | bytes 18440 | tf_op jit(solution)/shard_map/ppermute | solution.py:23
  252.6 5.9 %collective-permute-start.15 = (f32[2,6,4,1,32]{4,3,2,0,1:T(1,128)S(1)}, f32[2,6,4,1,32]{4,3,2,0,1:T(1,128)S(1)}, u32[]{:S(2)}, u32[]{:S(2)}) collective-permute-start(f32[2,6,4,1,32]{4,3,2,0,1:T(1,128)S(1)} %get-tuple-element.45), channel_id=1, source_target_pairs={{1,0},{2,1},{3,2},{4,3},{5,4},{6,5},{7,6},{8,7},{9,8},{10,9},{11,1... | collective-permute-start | bytes 18440 | tf_op jit(solution)/shard_map/ppermute | solution.py:24
  268.1 39.3 %all-to-all-start.5 = ((bf16[2,2,2,32,768]{4,2,1,0,3:T(2,128)(2,1)}), bf16[2,2,2,32,768]{4,2,1,0,3:T(2,128)(2,1)S(1)}, u32[]{:S(2)}, u32[]{:S(2)}) async-start(bf16[2,2,2,32,768]{4,2,1,0,3:T(2,128)(2,1)} %copy.61), calls=%async_computation.5 | async-start | bytes 786432 | tf_op jit(solution)/shard_map/all_to_all | solution.py:159

commit v3 on v0

--- a/solution.py
+++ b/solution.py
@@ -113,15 +113,15 @@
     rows_dev = height // lane_count
     features = queries.shape[3]
     heads = features // DH
-    stacked = jnp.stack([queries, key_vectors, value_vectors, out_cotangent])
+    stacked = jnp.stack([key_vectors, value_vectors, queries, out_cotangent])
     own = lax.all_to_all(stacked, "ulysses", split_axis=2, concat_axis=3, tiled=True)
     col_count = own.shape[3]
-    rim = with_halo(own, (("tm", 1), ("ulysses", 2)), 1)
     rim_frames, rim_rows = frames_dev + 2, rows_dev + 2
     own_n = frames_dev * rows_dev * col_count
     rim_n = rim_frames * rim_rows * col_count
     own_flat = own.reshape(4, own_n, features)
-    rim_flat = rim.reshape(4, rim_n, features)
+    kv_rim = with_halo(own[0:2], (("tm", 1), ("ulysses", 2)), 1).reshape(2, rim_n, features)
+    qd_rim = with_halo(own[2:4], (("tm", 1), ("ulysses", 2)), 1).reshape(2, rim_n, features)
     dims = (frames_dev, rows_dev, col_count, rim_frames, rim_rows)
 
     rim_pos = jnp.arange(rim_n, dtype=jnp.int32)
@@ -150,7 +150,7 @@
         grid_spec=pltpu.PrefetchScalarGridSpec(
             num_scalar_prefetch=1,
             grid=(heads,),
-            in_specs=[own_spec(0), own_spec(3), rim_spec(1), rim_spec(2), live_spec],
+            in_specs=[own_spec(2), own_spec(3), rim_spec(0), rim_spec(1), live_spec],
             out_specs=[pair_spec, stat_spec, stat_spec],
         ),
         out_shape=[
@@ -158,7 +158,7 @@
             jax.ShapeDtypeStruct((heads, own_n, 1), jnp.float32),
             jax.ShapeDtypeStruct((heads, own_n, 1), jnp.float32),
         ],
-    )(reach, own_flat, own_flat, rim_flat, rim_flat, live)
+    )(reach, own_flat, own_flat, kv_rim, kv_rim, live)
 
     def back_to_columns(pair):
         shaped = pair.reshape(2, frames_dev, rows_dev, col_count, features)
@@ -176,13 +176,13 @@
         grid_spec=pltpu.PrefetchScalarGridSpec(
             num_scalar_prefetch=1,
             grid=(heads,),
-            in_specs=[own_spec(1), own_spec(2), rim_spec(0), rim_spec(3)]
+            in_specs=[own_spec(0), own_spec(1), rim_spec(0), rim_spec(1)]
             + stat_rim_spec
             + [live_spec],
             out_specs=pair_spec,
         ),
         out_shape=jax.ShapeDtypeStruct((2, own_n, features), jnp.bfloat16),
-    )(reach, own_flat, own_flat, rim_flat, rim_flat, stat_rim, stat_rim, live)
+    )(reach, own_flat, own_flat, qd_rim, qd_rim, stat_rim, stat_rim, live)
     gkv_back = back_to_columns(gkv)
     return (og_back[0], og_back[1], gkv_back[0], gkv_back[1])
 

time: 297 us -> 290 us (0.976)
  waiting for transfers between devices: 101 us -> 78.6 us
  starting transfers between devices: 40.7 us -> 52.9 us
    ppermute x4 -> x6, waiting for transfers between devices: 41.4 us -> 18.8 us  [with_halo(): before = lax.ppermute(last, axis, up)]
    ppermute x4 -> x6, starting transfers between devices: 12.9 us -> 22.4 us  [with_halo(): before = lax.ppermute(last, axis, up)]
    ppermute x4 -> x6, starting transfers between devices: 8.37 us -> 10.5 us  [with_halo(): after = lax.ppermute(initial, axis, down)]
    concatenate x4 -> x6, other arithmetic: 5.75 us -> 6.28 us  [with_halo(): array = jnp.concatenate([before, array, after], axis=dim)]
    ppermute x4 -> x6, waiting for transfers between devices: 18.1 us -> 17.8 us  [with_halo(): after = lax.ppermute(initial, axis, down)]
  transfers between devices with their start and end apart: 10 -> 14, of which waited for: 8 -> 9; matrix products, arithmetic and copies ran while one was open for 3% -> 5% of each run, Pallas kernels for 4% -> 4%
where the time goes in v3:
time: 290 us; the launch traced here: 289 us
  blocking collectives  98.8 us (34%)
  waiting for transfers between devices  78.6 us (27%)
  starting transfers between devices  52.9 us (18%)
  Pallas kernels  24.9 us (9%)
  local copies, waits for them, and re-layouts  19.9 us (7%)
  other arithmetic  12.6 us (4%)
    all_to_all x1, blocking collectives, body(): lax.all_to_all(stacked, 'ulysses', split_axis=2, concat_axis=3, tiled=True)  98.8 us
    all_to_all x2, waiting for transfers between devices, back_to_columns(): lax.all_to_all(shaped, 'ulysses', split_axis=3, concat_axis=2, tiled=True)  41.9 us
    ppermute x6, starting transfers between devices, with_halo(): before = lax.ppermute(last, axis, up)  22.4 us
    all_to_all x2, starting transfers between devices, back_to_columns(): lax.all_to_all(shaped, 'ulysses', split_axis=3, concat_axis=2, tiled=True)  20 us
    ppermute x6, waiting for transfers between devices, with_halo(): before = lax.ppermute(last, axis, up)  18.8 us
    ppermute x6, waiting for transfers between devices, with_halo(): after = lax.ppermute(initial, axis, down)  17.8 us
    pallas_call x1, Pallas kernels, body(): pl.pallas_call(make_query_kernel(dims), grid_spec=pltpu.PrefetchScalarGri...  13.4 us
    pallas_call x1, Pallas kernels, body(): pl.pallas_call(make_key_kernel(dims), grid_spec=pltpu.PrefetchScalarGridS...  11.5 us
  transfers between devices with their start and end apart: 14, of which 9 were waited for; matrix products, arithmetic and copies ran while one was open for 5% of the time, Pallas kernels for 4%

profile of v3, /device:TPU:1, one launch (start us, length us, event | category | flops | bytes accessed | tf_op | source)
XLA Modules:
  0.0 288.6 jit_solution(17941843939345942461)
XLA Ops:
  0.7 2.0 copy_bitcast_fusion
  2.7 0.8 copy_bitcast_fusion.2
  3.5 2.4 pad_maximum_fusion.2
  5.9 98.8 %all_to_all.45 = bf16[4,2,64,1,1536]{4,1,3,0,2:T(2,128)(2,1)S(1)} all-to-all(bf16[4,2,64,1,1536]{4,1,3,0,2:T(2,128)(2,1)S(1)} %pad_maximum_fusion.2), channel_id=1, replica_groups=mesh['tm'=32,'ulysses'=32] {'ulysses'}, dimensions={2} | all-to-all | bytes 3145728 | tf_op jit(solution)/shard_map/all_to_all | solution.py:117
  104.6 0.9 copy.53
  105.5 0.1 slice_bitcast_fusion
  105.6 1.1 copy-done
  106.7 0.1 fusion.10
  106.8 3.2 %collective-permute-start = (bf16[2,1,2,32,1536]{4,3,2,1,0:T(8,128)(2,1)S(1)}, bf16[2,1,2,32,1536]{4,3,2,1,0:T(8,128)(2,1)S(1)}, u32[]{:S(2)}, u32[]{:S(2)}) collective-permute-start(bf16[2,1,2,32,1536]{4,3,2,1,0:T(8,128)(2,1)S(1)} %get-tuple-element.28), channel_id=1, source_target_pairs={{0,32},{32,64},{64,96},{96,128},{128,160},{160,192},{192,224},{224... | collective-permute-start | bytes 1179656 | tf_op jit(solution)/shard_map/ppermute | solution.py:22
  110.0 1.3 collective-permute-start.1
  111.3 6.6 %collective-permute-done = bf16[2,1,2,32,1536]{4,3,2,1,0:T(8,128)(2,1)S(1)} collective-permute-done((bf16[2,1,2,32,1536]{4,3,2,1,0:T(8,128)(2,1)S(1)}, bf16[2,1,2,32,1536]{4,3,2,1,0:T(8,128)(2,1)S(1)}, u32[]{:S(2)}, u32[]{:S(2)}) %collective-permute-start) | collective-permute-done | bytes 393248 | tf_op jit(solution)/shard_map/ppermute | solution.py:22
  117.9 3.8 %collective-permute-done.1 = bf16[2,1,2,32,1536]{4,3,2,1,0:T(8,128)(2,1)S(1)} collective-permute-done((bf16[2,1,2,32,1536]{4,3,2,1,0:T(8,128)(2,1)S(1)}, bf16[2,1,2,32,1536]{4,3,2,1,0:T(8,128)(2,1)S(1)}, u32[]{:S(2)}, u32[]{:S(2)}) %collective-permute-start.1) | collective-permute-done | bytes 393248 | tf_op jit(solution)/shard_map/ppermute | solution.py:23
  121.7 0.2 pad_maximum_fusion.3
  121.9 0.0 copy-start.4
  122.0 1.3 fusion.6
  123.3 2.1 collective-permute-start.2
  125.4 2.8 collective-permute-start.3
  128.2 0.6 and_convert_fusion.live_ref
  128.8 0.6 pad_add_fusion.reach_ref
  129.4 5.2 %collective-permute-done.2 = bf16[2,4,1,32,1536]{4,3,2,1,0:T(8,128)(2,1)S(1)} collective-permute-done((bf16[2,4,1,32,1536]{4,3,2,1,0:T(8,128)(2,1)}, bf16[2,4,1,32,1536]{4,3,2,1,0:T(8,128)(2,1)S(1)}, u32[]{:S(2)}, u32[]{:S(2)}) %collective-permute-start.2) | collective-permute-done | bytes 786464 | tf_op jit(solution)/shard_map/ppermute | solution.py:22
  134.6 4.4 %collective-permute-done.3 = bf16[2,4,1,32,1536]{4,3,2,1,0:T(8,128)(2,1)} collective-permute-done((bf16[2,4,1,32,1536]{4,3,2,1,0:T(8,128)(2,1)}, bf16[2,4,1,32,1536]{4,3,2,1,0:T(8,128)(2,1)}, u32[]{:S(2)}, u32[]{:S(2)}) %collective-permute-start.3) | collective-permute-done | bytes 786464 | tf_op jit(solution)/shard_map/ppermute | solution.py:23
  139.0 2.8 pad_maximum_fusion
  141.9 13.4 %shard_map.102 = (bf16[2,128,1536]{2,1,0:T(8,128)(2,1)}, f32[12,128,1]{2,1,0:T(8,128)}, f32[12,128,1]{2,1,0:T(8,128)}) custom-call(s32[3,12]{1,0:T(4,128)} %pad_add_fusion.reach_ref, bf16[4,128,1536]{2,1,0:T(8,128)(2,1)} %bitcast.38, bf16[4,128,1536]{2,1,0:T(8,128)(2,1)} %bitcast.39, bf16[2,512,1536]{2,1,0:T(8,128)(2,1)} %bitcast.44, ...), custom_call_target="tpu_custom_call" | custom-call | tf_op jit(solution)/shard_map/pallas_call | solution.py:148
  155.2 2.9 copy.35
  158.1 6.6 %all-to-all-start.1 = ((bf16[2,2,2,32,1536]{4,2,1,0,3:T(2,128)(2,1)}), bf16[2,2,2,32,1536]{4,2,1,0,3:T(2,128)(2,1)S(1)}, u32[]{:S(2)}, u32[]{:S(2)}) async-start(bf16[2,2,2,32,1536]{4,2,1,0,3:T(2,128)(2,1)} %copy.35), calls=%async_computation.1 | async-start | bytes 1572864 | tf_op jit(solution)/shard_map/all_to_all | solution.py:165
  164.7 0.1 fusion.8
  164.8 3.2 %collective-permute-start.4 = (bf16[2,1,2,32,1536]{4,3,2,1,0:T(8,128)(2,1)S(1)}, bf16[2,1,2,32,1536]{4,3,2,1,0:T(8,128)(2,1)S(1)}, u32[]{:S(2)}, u32[]{:S(2)}) collective-permute-start(bf16[2,1,2,32,1536]{4,3,2,1,0:T(8,128)(2,1)S(1)} %get-tuple-element.24), channel_id=1, source_target_pairs={{0,32},{32,64},{64,96},{96,128},{128,160},{160,192},{192,224},{224... | collective-permute-start | bytes 1179656 | tf_op jit(solution)/shard_map/ppermute | solution.py:22
  168.0 1.3 collective-permute-start.5
  169.3 6.9 %collective-permute-done.4 = bf16[2,1,2,32,1536]{4,3,2,1,0:T(8,128)(2,1)S(1)} collective-permute-done((bf16[2,1,2,32,1536]{4,3,2,1,0:T(8,128)(2,1)S(1)}, bf16[2,1,2,32,1536]{4,3,2,1,0:T(8,128)(2,1)S(1)}, u32[]{:S(2)}, u32[]{:S(2)}) %collective-permute-start.4) | collective-permute-done | bytes 393248 | tf_op jit(solution)/shard_map/ppermute | solution.py:22
  176.3 5.0 %collective-permute-done.5 = bf16[2,1,2,32,1536]{4,3,2,1,0:T(8,128)(2,1)S(1)} collective-permute-done((bf16[2,1,2,32,1536]{4,3,2,1,0:T(8,128)(2,1)S(1)}, bf16[2,1,2,32,1536]{4,3,2,1,0:T(8,128)(2,1)S(1)}, u32[]{:S(2)}, u32[]{:S(2)}) %collective-permute-start.5) | collective-permute-done | bytes 393248 | tf_op jit(solution)/shard_map/ppermute | solution.py:23
  181.3 0.2 pad_maximum_fusion.4
  181.5 1.3 fusion.5
  182.8 4.2 %collective-permute-start.6 = (bf16[2,4,1,32,1536]{4,3,2,1,0:T(8,128)(2,1)}, bf16[2,4,1,32,1536]{4,3,2,1,0:T(8,128)(2,1)S(1)}, u32[]{:S(2)}, u32[]{:S(2)}) collective-permute-start(bf16[2,4,1,32,1536]{4,3,2,1,0:T(8,128)(2,1)} %get-tuple-element.14), channel_id=1, source_target_pairs={{0,1},{1,2},{2,3},{3,4},{4,5},{5,6},{6,7},{7,8},{8,9},{9,10},{10,1... | collective-permute-start | bytes 2359304 | tf_op jit(solution)/shard_map/ppermute | solution.py:22
  187.0 1.9 collective-permute-start.7
  188.9 1.4 reduce
  190.3 0.1 stack.45
  190.4 1.4 reduce.1
  191.8 0.1 stack.46
  192.0 4.6 %collective-permute-start.8 = (f32[2,12,1,2,32]{4,3,2,0,1:T(2,128)S(1)}, f32[2,12,1,2,32]{4,3,2,0,1:T(2,128)S(1)}, u32[]{:S(2)}, u32[]{:S(2)}) collective-permute-start(f32[2,12,1,2,32]{4,3,2,0,1:T(2,128)S(1)} %get-tuple-element.32), channel_id=1, source_target_pairs={{0,32},{32,64},{64,96},{96,128},{128,160},{160,192},{192,224},{224... | collective-permute-start | bytes 18440 | tf_op jit(solution)/shard_map/ppermute | solution.py:22
  196.6 1.3 collective-permute-start.9
  197.9 3.3 %collective-permute-done.9 = f32[2,12,1,2,32]{4,3,2,0,1:T(2,128)S(1)} collective-permute-done((f32[2,12,1,2,32]{4,3,2,0,1:T(2,128)S(1)}, f32[2,12,1,2,32]{4,3,2,0,1:T(2,128)S(1)}, u32[]{:S(2)}, u32[]{:S(2)}) %collective-permute-start.9) | collective-permute-done | bytes 6176 | tf_op jit(solution)/shard_map/ppermute | solution.py:23
  201.1 0.1 pad_maximum_fusion.6
  201.2 0.1 fusion.11
  201.3 5.1 %collective-permute-start.10 = (f32[2,12,4,1,32]{4,3,2,0,1:T(1,128)S(1)}, f32[2,12,4,1,32]{4,3,2,0,1:T(1,128)S(1)}, u32[]{:S(2)}, u32[]{:S(2)}) collective-permute-start(f32[2,12,4,1,32]{4,3,2,0,1:T(1,128)S(1)} %get-tuple-element.30), channel_id=1, source_target_pairs={{0,1},{1,2},{2,3},{3,4},{4,5},{5,6},{6,7},{7,8},{8,9},{9,10},{10,1... | collective-permute-start | bytes 36872 | tf_op jit(solution)/shard_map/ppermute | solution.py:22
  206.4 1.9 collective-permute-start.11
  208.3 1.4 collective-permute-done.7
  209.6 2.8 pad_maximum_fusion.1
  212.5 0.2 pad_maximum_fusion.5
  212.7 0.2 reshape.176
  212.9 0.7 copy.46.lse_ref.dot_ref
  213.5 11.5 %shard_map.103 = bf16[2,128,1536]{2,1,0:T(8,128)(2,1)} custom-call(s32[3,12]{1,0:T(4,128)} %pad_add_fusion.reach_ref, bf16[4,128,1536]{2,1,0:T(8,128)(2,1)} %bitcast.40, bf16[4,128,1536]{2,1,0:T(8,128)(2,1)} %bitcast.41, bf16[2,512,1536]{2,1,0:T(8,128)(2,1)} %bitcast.42, bf16[2,512,1536]{2,1,0:T(8,128)(2,1)} %bitcast.43, ...), custom_call_target="tpu_custom_call" | custom-call | tf_op jit(solution)/shard_map/pallas_call | solution.py:174
  225.0 2.8 copy.39
  227.8 13.4 %all-to-all-start.2 = ((bf16[2,2,2,32,1536]{4,2,1,0,3:T(2,128)(2,1)}), bf16[2,2,2,32,1536]{4,2,1,0,3:T(2,128)(2,1)S(1)}, u32[]{:S(2)}, u32[]{:S(2)}) async-start(bf16[2,2,2,32,1536]{4,2,1,0,3:T(2,128)(2,1)} %copy.39), calls=%async_computation.2 | async-start | bytes 1572864 | tf_op jit(solution)/shard_map/all_to_all | solution.py:165
  241.2 0.5 fusion.9
  241.8 0.3 copy.36
  242.1 0.8 copy.42
  242.9 0.3 copy.37
  243.2 0.8 copy.43
  244.0 41.9 %all-to-all-done.2 = bf16[2,2,2,32,1536]{4,2,1,0,3:T(2,128)(2,1)S(1)} async-done(((bf16[2,2,2,32,1536]{4,2,1,0,3:T(2,128)(2,1)}), bf16[2,2,2,32,1536]{4,2,1,0,3:T(2,128)(2,1)S(1)}, u32[]{:S(2)}, u32[]{:S(2)}) %all-to-all-start.2) | async-done | bytes 786464 | tf_op jit(solution)/shard_map/all_to_all | solution.py:165
  285.9 0.5 fusion.7
  286.4 0.3 copy.40
  286.8 0.8 copy.44
  287.5 0.3 copy.41
  287.9 0.8 copy.45
  (18 shorter events, 0.1 us)
Async XLA Ops:
  0.6 2.0 copy-start.2
  0.6 2.0 copy-start.1
  105.5 1.2 copy-start
  106.8 11.2 %collective-permute-start = (bf16[2,1,2,32,1536]{4,3,2,1,0:T(8,128)(2,1)S(1)}, bf16[2,1,2,32,1536]{4,3,2,1,0:T(8,128)(2,1)S(1)}, u32[]{:S(2)}, u32[]{:S(2)}) collective-permute-start(bf16[2,1,2,32,1536]{4,3,2,1,0:T(8,128)(2,1)S(1)} %get-tuple-element.28), channel_id=1, source_target_pairs={{0,32},{32,64},{64,96},{96,128},{128,160},{160,192},{192,224},{224... | collective-permute-start | bytes 1179656 | tf_op jit(solution)/shard_map/ppermute | solution.py:22
  110.0 11.8 %collective-permute-start.1 = (bf16[2,1,2,32,1536]{4,3,2,1,0:T(8,128)(2,1)S(1)}, bf16[2,1,2,32,1536]{4,3,2,1,0:T(8,128)(2,1)S(1)}, u32[]{:S(2)}, u32[]{:S(2)}) collective-permute-start(bf16[2,1,2,32,1536]{4,3,2,1,0:T(8,128)(2,1)S(1)} %get-tuple-element.29), channel_id=1, source_target_pairs={{32,0},{64,32},{96,64},{128,96},{160,128},{192,160},{224,192},{256... | collective-permute-start | bytes 1179656 | tf_op jit(solution)/shard_map/ppermute | solution.py:23
  121.9 6.9 %copy-start.3 = (s32[12]{0:T(128)S(1)}, s32[12]{0:T(128)}, u32[]{:S(2)}) copy-start(s32[12]{0:T(128)} %param.13) | copy-start | bytes 148
  121.9 6.9 %copy-start.4 = (s32[12]{0:T(128)S(1)}, s32[12]{0:T(128)}, u32[]{:S(2)}) copy-start(s32[12]{0:T(128)} %param.12) | copy-start | bytes 148
  121.9 6.9 %copy-start.5 = (s32[12]{0:T(128)S(1)}, s32[12]{0:T(128)}, u32[]{:S(2)}) copy-start(s32[12]{0:T(128)} %param.11) | copy-start | bytes 148
  123.3 11.4 %collective-permute-start.2 = (bf16[2,4,1,32,1536]{4,3,2,1,0:T(8,128)(2,1)}, bf16[2,4,1,32,1536]{4,3,2,1,0:T(8,128)(2,1)S(1)}, u32[]{:S(2)}, u32[]{:S(2)}) collective-permute-start(bf16[2,4,1,32,1536]{4,3,2,1,0:T(8,128)(2,1)} %get-tuple-element.18), channel_id=1, source_target_pairs={{0,1},{1,2},{2,3},{3,4},{4,5},{5,6},{6,7},{7,8},{8,9},{9,10},{10,1... | collective-permute-start | bytes 2359304 | tf_op jit(solution)/shard_map/ppermute | solution.py:22
  125.4 13.6 %collective-permute-start.3 = (bf16[2,4,1,32,1536]{4,3,2,1,0:T(8,128)(2,1)}, bf16[2,4,1,32,1536]{4,3,2,1,0:T(8,128)(2,1)}, u32[]{:S(2)}, u32[]{:S(2)}) collective-permute-start(bf16[2,4,1,32,1536]{4,3,2,1,0:T(8,128)(2,1)} %get-tuple-element.19), channel_id=1, source_target_pairs={{1,0},{2,1},{3,2},{4,3},{5,4},{6,5},{7,6},{8,7},{9,8},{10,9},{11,1... | collective-permute-start | bytes 2359304 | tf_op jit(solution)/shard_map/ppermute | solution.py:23
  158.1 69.8 %all-to-all-start.1 = ((bf16[2,2,2,32,1536]{4,2,1,0,3:T(2,128)(2,1)}), bf16[2,2,2,32,1536]{4,2,1,0,3:T(2,128)(2,1)S(1)}, u32[]{:S(2)}, u32[]{:S(2)}) async-start(bf16[2,2,2,32,1536]{4,2,1,0,3:T(2,128)(2,1)} %copy.35), calls=%async_computation.1 | async-start | bytes 1572864 | tf_op jit(solution)/shard_map/all_to_all | solution.py:165
  164.8 11.4 %collective-permute-start.4 = (bf16[2,1,2,32,1536]{4,3,2,1,0:T(8,128)(2,1)S(1)}, bf16[2,1,2,32,1536]{4,3,2,1,0:T(8,128)(2,1)S(1)}, u32[]{:S(2)}, u32[]{:S(2)}) collective-permute-start(bf16[2,1,2,32,1536]{4,3,2,1,0:T(8,128)(2,1)S(1)} %get-tuple-element.24), channel_id=1, source_target_pairs={{0,32},{32,64},{64,96},{96,128},{128,160},{160,192},{192,224},{224... | collective-permute-start | bytes 1179656 | tf_op jit(solution)/shard_map/ppermute | solution.py:22
  168.0 13.3 %collective-permute-start.5 = (bf16[2,1,2,32,1536]{4,3,2,1,0:T(8,128)(2,1)S(1)}, bf16[2,1,2,32,1536]{4,3,2,1,0:T(8,128)(2,1)S(1)}, u32[]{:S(2)}, u32[]{:S(2)}) collective-permute-start(bf16[2,1,2,32,1536]{4,3,2,1,0:T(8,128)(2,1)S(1)} %get-tuple-element.25), channel_id=1, source_target_pairs={{32,0},{64,32},{96,64},{128,96},{160,128},{192,160},{224,192},{256... | collective-permute-start | bytes 1179656 | tf_op jit(solution)/shard_map/ppermute | solution.py:23
  182.8 25.5 %collective-permute-start.6 = (bf16[2,4,1,32,1536]{4,3,2,1,0:T(8,128)(2,1)}, bf16[2,4,1,32,1536]{4,3,2,1,0:T(8,128)(2,1)S(1)}, u32[]{:S(2)}, u32[]{:S(2)}) collective-permute-start(bf16[2,4,1,32,1536]{4,3,2,1,0:T(8,128)(2,1)} %get-tuple-element.14), channel_id=1, source_target_pairs={{0,1},{1,2},{2,3},{3,4},{4,5},{5,6},{6,7},{7,8},{8,9},{9,10},{10,1... | collective-permute-start | bytes 2359304 | tf_op jit(solution)/shard_map/ppermute | solution.py:22
  187.0 22.7 %collective-permute-start.7 = (bf16[2,4,1,32,1536]{4,3,2,1,0:T(8,128)(2,1)}, bf16[2,4,1,32,1536]{4,3,2,1,0:T(8,128)(2,1)}, u32[]{:S(2)}, u32[]{:S(2)}) collective-permute-start(bf16[2,4,1,32,1536]{4,3,2,1,0:T(8,128)(2,1)} %get-tuple-element.15), channel_id=1, source_target_pairs={{1,0},{2,1},{3,2},{4,3},{5,4},{6,5},{7,6},{8,7},{9,8},{10,9},{11,1... | collective-permute-start | bytes 2359304 | tf_op jit(solution)/shard_map/ppermute | solution.py:23
  192.0 5.9 %collective-permute-start.8 = (f32[2,12,1,2,32]{4,3,2,0,1:T(2,128)S(1)}, f32[2,12,1,2,32]{4,3,2,0,1:T(2,128)S(1)}, u32[]{:S(2)}, u32[]{:S(2)}) collective-permute-start(f32[2,12,1,2,32]{4,3,2,0,1:T(2,128)S(1)} %get-tuple-element.32), channel_id=1, source_target_pairs={{0,32},{32,64},{64,96},{96,128},{128,160},{160,192},{192,224},{224... | collective-permute-start | bytes 18440 | tf_op jit(solution)/shard_map/ppermute | solution.py:22
  196.6 4.6 %collective-permute-start.9 = (f32[2,12,1,2,32]{4,3,2,0,1:T(2,128)S(1)}, f32[2,12,1,2,32]{4,3,2,0,1:T(2,128)S(1)}, u32[]{:S(2)}, u32[]{:S(2)}) collective-permute-start(f32[2,12,1,2,32]{4,3,2,0,1:T(2,128)S(1)} %get-tuple-element.33), channel_id=1, source_target_pairs={{32,0},{64,32},{96,64},{128,96},{160,128},{192,160},{224,192},{256... | collective-permute-start | bytes 18440 | tf_op jit(solution)/shard_map/ppermute | solution.py:23
  201.3 11.2 %collective-permute-start.10 = (f32[2,12,4,1,32]{4,3,2,0,1:T(1,128)S(1)}, f32[2,12,4,1,32]{4,3,2,0,1:T(1,128)S(1)}, u32[]{:S(2)}, u32[]{:S(2)}) collective-permute-start(f32[2,12,4,1,32]{4,3,2,0,1:T(1,128)S(1)} %get-tuple-element.30), channel_id=1, source_target_pairs={{0,1},{1,2},{2,3},{3,4},{4,5},{5,6},{6,7},{7,8},{8,9},{9,10},{10,1... | collective-permute-start | bytes 36872 | tf_op jit(solution)/shard_map/ppermute | solution.py:22
  206.4 6.1 %collective-permute-start.11 = (f32[2,12,4,1,32]{4,3,2,0,1:T(1,128)S(1)}, f32[2,12,4,1,32]{4,3,2,0,1:T(1,128)S(1)}, u32[]{:S(2)}, u32[]{:S(2)}) collective-permute-start(f32[2,12,4,1,32]{4,3,2,0,1:T(1,128)S(1)} %get-tuple-element.31), channel_id=1, source_target_pairs={{1,0},{2,1},{3,2},{4,3},{5,4},{6,5},{7,6},{8,7},{9,8},{10,9},{11,1... | collective-permute-start | bytes 36872 | tf_op jit(solution)/shard_map/ppermute | solution.py:23
  227.8 58.0 %all-to-all-start.2 = ((bf16[2,2,2,32,1536]{4,2,1,0,3:T(2,128)(2,1)}), bf16[2,2,2,32,1536]{4,2,1,0,3:T(2,128)(2,1)S(1)}, u32[]{:S(2)}, u32[]{:S(2)}) async-start(bf16[2,2,2,32,1536]{4,2,1,0,3:T(2,128)(2,1)} %copy.39), calls=%async_computation.2 | async-start | bytes 1572864 | tf_op jit(solution)/shard_map/all_to_all | solution.py:165

commit v4 on v3

--- a/solution.py
+++ b/solution.py
@@ -5,7 +5,7 @@
 from jax import lax
 from jax.experimental import pallas as pl
 from jax.experimental.pallas import tpu as pltpu
-from jax.sharding import PartitionSpec as P
+from jax.sharding import Mesh, PartitionSpec as P
 
 DH = 128
 HEADS = 12
@@ -105,8 +105,8 @@
 
 
 def body(queries, key_vectors, value_vectors, out_cotangent, reach_time, reach_height, reach_width):
-    lane_count = lax.axis_size("ulysses")
-    band_index = lax.axis_index("ulysses")
+    lane_count = lax.axis_size(("z", "core"))
+    band_index = lax.axis_index(("z", "core"))
     time_index = lax.axis_index("tm")
     time_count = lax.axis_size("tm")
     frames_dev, height = queries.shape[0], queries.shape[1]
@@ -114,14 +114,19 @@
     features = queries.shape[3]
     heads = features // DH
     stacked = jnp.stack([key_vectors, value_vectors, queries, out_cotangent])
-    own = lax.all_to_all(stacked, "ulysses", split_axis=2, concat_axis=3, tiled=True)
+    chips, cores = lax.axis_size("z"), lax.axis_size("core")
+    local_cols = stacked.shape[3]
+    across = lax.all_to_all(stacked, "z", split_axis=2, concat_axis=3, tiled=True)
+    across = across.reshape(across.shape[:3] + (chips, 1, local_cols, features))
+    own = lax.all_to_all(across, "core", split_axis=2, concat_axis=4, tiled=True)
+    own = own.reshape(own.shape[:3] + (-1, features))
     col_count = own.shape[3]
     rim_frames, rim_rows = frames_dev + 2, rows_dev + 2
     own_n = frames_dev * rows_dev * col_count
     rim_n = rim_frames * rim_rows * col_count
     own_flat = own.reshape(4, own_n, features)
-    kv_rim = with_halo(own[0:2], (("tm", 1), ("ulysses", 2)), 1).reshape(2, rim_n, features)
-    qd_rim = with_halo(own[2:4], (("tm", 1), ("ulysses", 2)), 1).reshape(2, rim_n, features)
+    kv_rim = with_halo(own[0:2], (("tm", 1), (("z", "core"), 2)), 1).reshape(2, rim_n, features)
+    qd_rim = with_halo(own[2:4], (("tm", 1), (("z", "core"), 2)), 1).reshape(2, rim_n, features)
     dims = (frames_dev, rows_dev, col_count, rim_frames, rim_rows)
 
     rim_pos = jnp.arange(rim_n, dtype=jnp.int32)
@@ -161,13 +166,15 @@
     )(reach, own_flat, own_flat, kv_rim, kv_rim, live)
 
     def back_to_columns(pair):
-        shaped = pair.reshape(2, frames_dev, rows_dev, col_count, features)
-        return lax.all_to_all(shaped, "ulysses", split_axis=3, concat_axis=2, tiled=True)
+        shaped = pair.reshape(2, frames_dev, rows_dev, chips, cores, local_cols, features)
+        within = lax.all_to_all(shaped, "core", split_axis=4, concat_axis=2, tiled=True)
+        within = within.reshape(2, frames_dev, rows_dev * cores, chips * local_cols, features)
+        return lax.all_to_all(within, "z", split_axis=3, concat_axis=2, tiled=True)
 
     og_back = back_to_columns(og)
 
     statistics = jnp.stack([lse, dots]).reshape(2, heads, frames_dev, rows_dev, col_count)
-    stat_rim = with_halo(statistics, (("tm", 2), ("ulysses", 3)), 1).reshape(2, heads, 1, rim_n)
+    stat_rim = with_halo(statistics, (("tm", 2), (("z", "core"), 3)), 1).reshape(2, heads, 1, rim_n)
     stat_rim_spec = [
         pl.BlockSpec((None, None, 1, rim_n), lambda h, r, w=w: (w, h, 0, 0)) for w in range(2)
     ]
@@ -189,18 +196,21 @@
 
 def solution(mesh):
     in_specs = (
-        P("tm", None, "ulysses", None),
-        P("tm", None, "ulysses", None),
-        P("tm", None, "ulysses", None),
-        P("tm", None, "ulysses", None),
+        P("tm", None, ("z", "core"), None),
+        P("tm", None, ("z", "core"), None),
+        P("tm", None, ("z", "core"), None),
+        P("tm", None, ("z", "core"), None),
         P(),
         P(),
         P(),
     )
     out_specs = (
-        P("tm", None, "ulysses", None),
-        P("tm", None, "ulysses", None),
-        P("tm", None, "ulysses", None),
-        P("tm", None, "ulysses", None),
+        P("tm", None, ("z", "core"), None),
+        P("tm", None, ("z", "core"), None),
+        P("tm", None, ("z", "core"), None),
+        P("tm", None, ("z", "core"), None),
     )
-    return jax.shard_map(body, mesh=mesh, in_specs=in_specs, out_specs=out_specs, check_vma=False)
+    tm_size, lane_size = mesh.shape["tm"], mesh.shape["ulysses"]
+    cores = 2 if lane_size % 2 == 0 else 1
+    split = Mesh(mesh.devices.reshape(tm_size, lane_size // cores, cores), ("tm", "z", "core"))
+    return jax.shard_map(body, mesh=split, in_specs=in_specs, out_specs=out_specs, check_vma=False)

time: 290 us -> 338 us (1.17)
  the two profiles are of different devices: /device:TPU:1 before, /device:TPU:68 now
where the time goes in v4:
time: 338 us; the launch traced here: 336 us
  waiting for transfers between devices  147 us (43%)
  starting transfers between devices  77.8 us (23%)
  local copies, waits for them, and re-layouts  45.7 us (14%)
  other arithmetic  25.7 us (8%)
  Pallas kernels  24.8 us (7%)
  blocking collectives  13.7 us (4%)
    all_to_all x2, waiting for transfers between devices, back_to_columns(): return lax.all_to_all(within, 'z', split_axis=3, concat_axis=2, tiled=True)  75.5 us
    all_to_all x1, waiting for transfers between devices, body(): lax.all_to_all(stacked, 'z', split_axis=2, concat_axis=3, tiled=True)  71.5 us
    ppermute x6, starting transfers between devices, with_halo(): after = lax.ppermute(initial, axis, down)  27.8 us
    all_to_all x1, starting transfers between devices, body(): lax.all_to_all(stacked, 'z', split_axis=2, concat_axis=3, tiled=True)  18.6 us
    concatenate x6, other arithmetic, with_halo(): array = jnp.concatenate([before, array, after], axis=dim)  18.5 us
    all_to_all x2, starting transfers between devices, back_to_columns(): return lax.all_to_all(within, 'z', split_axis=3, concat_axis=2, tiled=True)  18.3 us
    pallas_call x1, Pallas kernels, body(): pl.pallas_call(make_query_kernel(dims), grid_spec=pltpu.PrefetchScalarGri...  13.4 us
    ppermute x6, starting transfers between devices, with_halo(): before = lax.ppermute(last, axis, up)  13.1 us
  transfers between devices with their start and end apart: 15, of which 3 were waited for; matrix products, arithmetic and copies ran while one was open for 15% of the time, Pallas kernels for 4%

profile of v4, /device:TPU:68, one launch (start us, length us, event | category | flops | bytes accessed | tf_op | source)
XLA Modules:
  0.0 336.0 jit_solution(1344238234048144799)
XLA Ops:
  0.7 2.0 copy_bitcast_fusion
  2.7 0.8 copy_bitcast_fusion.2
  3.5 3.2 pad_maximum_fusion.2
  6.7 18.6 %all-to-all-start = ((bf16[4,2,64,1,1536]{4,1,3,0,2:T(2,128)(2,1)}), bf16[4,2,64,1,1536]{4,1,3,0,2:T(2,128)(2,1)S(1)}, u32[]{:S(2)}, u32[]{:S(2)}) async-start(bf16[4,2,64,1,1536]{4,1,3,0,2:T(2,128)(2,1)} %pad_maximum_fusion.2), calls=%async_computation | async-start | bytes 3145728 | tf_op jit(solution)/shard_map/all_to_all | solution.py:119
  25.3 0.6 and_convert_fusion.live_ref
  25.9 0.6 pad_add_fusion.reach_ref
  26.5 71.5 %all-to-all-done = bf16[4,2,64,1,1536]{4,1,3,0,2:T(2,128)(2,1)S(1)} async-done(((bf16[4,2,64,1,1536]{4,1,3,0,2:T(2,128)(2,1)}), bf16[4,2,64,1,1536]{4,1,3,0,2:T(2,128)(2,1)S(1)}, u32[]{:S(2)}, u32[]{:S(2)}) %all-to-all-start) | async-done | bytes 1572896 | tf_op jit(solution)/shard_map/all_to_all | solution.py:119
  98.0 1.1 copy.37
  99.1 1.4 copy.38
  100.6 5.0 %all_to_all.90 = bf16[4,2,4,16,1,1,1536]{6,1,3,0,5,4,2:T(2,128)(2,1)S(1)} all-to-all(bf16[4,2,4,16,1,1,1536]{6,1,3,0,5,4,2:T(2,128)(2,1)S(1)} %copy.38), channel_id=1, replica_groups=mesh['tm'=32,'z'=16,'core'=2] {'core'}, dimensions={2} | all-to-all | bytes 3145728 | tf_op jit(solution)/shard_map/all_to_all | solution.py:121
  105.8 1.0 fusion.6
  106.9 1.6 copy.40
  108.5 0.8 copy.41
  109.3 1.4 fusion.11
  110.7 3.5 %collective-permute-start = (bf16[2,1,2,32,1536]{4,2,3,1,0:T(2,128)(2,1)}, bf16[2,1,2,32,1536]{4,2,3,1,0:T(2,128)(2,1)S(1)}, u32[]{:S(2)}, u32[]{:S(2)}) collective-permute-start(bf16[2,1,2,32,1536]{4,2,3,1,0:T(2,128)(2,1)} %get-tuple-element.30), channel_id=1, source_target_pairs={{0,32},{32,64},{64,96},{96,128},{128,160},{160,192},{192,224},{224... | collective-permute-start | bytes 1179656 | tf_op jit(solution)/shard_map/ppermute | solution.py:22
  114.2 4.5 %collective-permute-start.1 = (bf16[2,1,2,32,1536]{4,2,3,1,0:T(2,128)(2,1)}, bf16[2,1,2,32,1536]{4,2,3,1,0:T(2,128)(2,1)}, u32[]{:S(2)}, u32[]{:S(2)}) collective-permute-start(bf16[2,1,2,32,1536]{4,2,3,1,0:T(2,128)(2,1)} %get-tuple-element.31), channel_id=1, source_target_pairs={{32,0},{64,32},{96,64},{128,96},{160,128},{192,160},{224,192},{256... | collective-permute-start | bytes 1179656 | tf_op jit(solution)/shard_map/ppermute | solution.py:23
  118.7 1.5 reshape_reshape.3.q_ref.do_ref.k_ref.v_ref
  120.2 1.9 copy.52
  122.2 0.5 fusion.9
  122.7 1.9 collective-permute-start.4
  124.6 6.2 %collective-permute-start.5 = (bf16[2,1,2,32,1536]{4,2,3,1,0:T(2,128)(2,1)S(1)}, bf16[2,1,2,32,1536]{4,2,3,1,0:T(2,128)(2,1)S(1)}, u32[]{:S(2)}, u32[]{:S(2)}) collective-permute-start(bf16[2,1,2,32,1536]{4,2,3,1,0:T(2,128)(2,1)S(1)} %get-tuple-element.27), channel_id=1, source_target_pairs={{32,0},{64,32},{96,64},{128,96},{160,128},{192,160},{224,192},{256... | collective-permute-start | bytes 1179656 | tf_op jit(solution)/shard_map/ppermute | solution.py:23
  130.9 3.4 %pad_maximum_fusion.3 = bf16[2,4,2,32,1536]{4,2,3,1,0:T(2,128)(2,1)S(1)} fusion(bf16[2,1,2,32,1536]{4,2,3,1,0:T(2,128)(2,1)} %collective-permute-done.1, bf16[2,2,2,32,1536]{4,2,3,1,0:T(2,128)(2,1)S(1)} %bitcast.57, bf16[2,1,2,32,1536]{4,2,3,1,0:T(2,128)(2,1)S(1)} %collective-permute-done), kind=kLoop, calls=%fused_computation.3 | loop fusion | flops 1572864 | bytes 3145728 | tf_op jit(solution)/shard_map/concatenate | solution.py:24
  134.3 2.9 fusion.7
  137.3 1.9 collective-permute-start.2
  139.4 3.6 %collective-permute-start.3 = (bf16[2,4,1,32,1536]{4,3,2,1,0:T(8,128)(2,1)S(1)}, bf16[2,4,1,32,1536]{4,3,2,1,0:T(8,128)(2,1)S(1)}, u32[]{:S(2)}, u32[]{:S(2)}) collective-permute-start(bf16[2,4,1,32,1536]{4,3,2,1,0:T(8,128)(2,1)S(1)} %copy.43), channel_id=1, source_target_pairs={{1,0},{2,1},{3,2},{4,3},{5,4},{6,5},{7,6},{8,7},{9,8},{10,9},{11,1... | collective-permute-start | bytes 2359304 | tf_op jit(solution)/shard_map/ppermute | solution.py:23
  143.0 2.4 pad_maximum_fusion.4
  145.5 2.9 fusion.5
  148.5 1.9 collective-permute-start.6
  150.4 1.0 copy.54
  151.4 3.6 %collective-permute-start.7 = (bf16[2,4,1,32,1536]{4,3,2,1,0:T(8,128)(2,1)}, bf16[2,4,1,32,1536]{4,3,2,1,0:T(8,128)(2,1)}, u32[]{:S(2)}, u32[]{:S(2)}) collective-permute-start(bf16[2,4,1,32,1536]{4,3,2,1,0:T(8,128)(2,1)} %copy.54), channel_id=1, source_target_pairs={{1,0},{2,1},{3,2},{4,3},{5,4},{6,5},{7,6},{8,7},{9,8},{10,9},{11,1... | collective-permute-start | bytes 2359304 | tf_op jit(solution)/shard_map/ppermute | solution.py:23
  155.1 1.3 copy.44
  156.4 1.3 copy.45
  157.7 6.7 %pad_maximum_fusion = bf16[2,4,4,32,1536]{4,2,3,1,0:T(4,128)(2,1)S(1)} fusion(bf16[2,4,1,32,1536]{4,2,3,1,0:T(2,128)(2,1)S(1)} %copy.45, bf16[2,1,2,32,1536]{4,2,3,1,0:T(2,128)(2,1)} %collective-permute-done.1, bf16[2,2,2,32,1536]{4,2,3,1,0:T(2,128)(2,1)S(1)} %bitcast.58, bf16[2,1,2,32,1536]{4,2,3,1,0:T(2,128)(2,1)S(1)} %collective-permute-done, ...), kind=kLoop, calls=%fused_computation | loop fusion | flops 15728640 | bytes 6291456 | tf_op jit(solution)/shard_map/concatenate | solution.py:24
  164.4 2.4 copy.46
  166.7 13.4 %shard_map.102 = (bf16[2,128,1536]{2,1,0:T(8,128)(2,1)}, f32[12,128,1]{2,1,0:T(8,128)}, f32[12,128,1]{2,1,0:T(8,128)}) custom-call(s32[3,12]{1,0:T(4,128)} %pad_add_fusion.reach_ref, bf16[4,128,1536]{2,1,0:T(8,128)(2,1)} %reshape_reshape.3.q_ref.do_ref.k_ref.v_ref, bf16[4,128,1536]{2,1,0:T(8,128)(2,1)} %reshape_reshape.3.q_ref.do_ref.k_ref.v_ref, ...), custom_call_target="tpu_custom_call" | custom-call | tf_op jit(solution)/shard_map/pallas_call | solution.py:153
  180.1 1.4 reduce
  181.6 1.4 reduce.1
  183.2 1.9 collective-permute-start.8
  185.1 6.3 %collective-permute-start.9 = (f32[2,12,1,2,32]{4,3,2,0,1:T(2,128)S(1)}, f32[2,12,1,2,32]{4,3,2,0,1:T(2,128)S(1)}, u32[]{:S(2)}, u32[]{:S(2)}) collective-permute-start(f32[2,12,1,2,32]{4,3,2,0,1:T(2,128)S(1)} %get-tuple-element.35), channel_id=1, source_target_pairs={{32,0},{64,32},{96,64},{128,96},{160,128},{192,160},{224,192},{256... | collective-permute-start | bytes 18440 | tf_op jit(solution)/shard_map/ppermute | solution.py:23
  191.4 2.4 copy.55
  193.8 2.4 copy.56
  196.5 1.9 collective-permute-start.10
  198.4 3.6 %collective-permute-start.11 = (f32[2,12,4,1,32]{4,3,2,0,1:T(1,128)S(1)}, f32[2,12,4,1,32]{4,3,2,0,1:T(1,128)S(1)}, u32[]{:S(2)}, u32[]{:S(2)}) collective-permute-start(f32[2,12,4,1,32]{4,3,2,0,1:T(1,128)S(1)} %get-tuple-element.33), channel_id=1, source_target_pairs={{1,0},{2,1},{3,2},{4,3},{5,4},{6,5},{7,6},{8,7},{9,8},{10,9},{11,1... | collective-permute-start | bytes 36872 | tf_op jit(solution)/shard_map/ppermute | solution.py:23
  202.0 5.7 %pad_maximum_fusion.1 = bf16[2,4,4,32,1536]{4,2,3,1,0:T(4,128)(2,1)S(1)} fusion(bf16[2,4,1,32,1536]{4,2,3,1,0:T(2,128)(2,1)S(1)} %copy.56, bf16[2,1,2,32,1536]{4,2,3,1,0:T(2,128)(2,1)S(1)} %collective-permute-done.5, bf16[2,2,2,32,1536]{4,2,3,1,0:T(2,128)(2,1)S(1)} %bitcast.55, bf16[2,1,2,32,1536]{4,2,3,1,0:T(2,128)(2,1)S(1)} %collective-permute-done.4, ...), kind=kLoop, calls=%fused_computation.1 | loop fusion | flops 15728640 | bytes 6291456 | tf_op jit(solution)/shard_map/concatenate | solution.py:24
  207.8 2.4 copy.57
  210.6 4.4 %all_to_all.91 = bf16[2,2,2,16,2,1,1536]{6,3,2,1,0,5,4:T(8,128)(2,1)S(1)} all-to-all(bf16[2,2,2,16,2,1,1536]{6,3,2,1,0,5,4:T(8,128)(2,1)S(1)} %copy.47), channel_id=1, replica_groups=mesh['tm'=32,'z'=16,'core'=2] {'core'}, dimensions={4} | all-to-all | bytes 1572864 | tf_op jit(solution)/shard_map/all_to_all | solution.py:170
  215.0 1.5 copy.49
  216.9 0.7 copy.68.lse_ref.dot_ref
  217.6 11.5 %shard_map.103 = bf16[2,128,1536]{2,1,0:T(8,128)(2,1)} custom-call(s32[3,12]{1,0:T(4,128)} %pad_add_fusion.reach_ref, bf16[4,128,1536]{2,1,0:T(8,128)(2,1)} %reshape_reshape.3.q_ref.do_ref.k_ref.v_ref, bf16[4,128,1536]{2,1,0:T(8,128)(2,1)} %reshape_reshape.3.q_ref.do_ref.k_ref.v_ref, bf16[2,512,1536]{2,1,0:T(8,128)(2,1)} %bitcast.47, ...), custom_call_target="tpu_custom_call" | custom-call | tf_op jit(solution)/shard_map/pallas_call | solution.py:181
  229.1 2.2 reshape.187
  231.3 4.4 %all_to_all.92 = bf16[2,2,2,16,2,1,1536]{6,3,2,1,0,5,4:T(8,128)(2,1)S(1)} all-to-all(bf16[2,2,2,16,2,1,1536]{6,3,2,1,0,5,4:T(8,128)(2,1)S(1)} %copy.59), channel_id=1, replica_groups=mesh['tm'=32,'z'=16,'core'=2] {'core'}, dimensions={4} | all-to-all | bytes 1572864 | tf_op jit(solution)/shard_map/all_to_all | solution.py:170
  235.7 11.2 %all-to-all-start.3 = ((bf16[2,2,4,16,1536]{4,2,1,0,3:T(4,128)(2,1)}), bf16[2,2,4,16,1536]{4,2,1,0,3:T(4,128)(2,1)S(1)}, u32[]{:S(2)}, u32[]{:S(2)}) async-start(bf16[2,2,4,16,1536]{4,2,1,0,3:T(4,128)(2,1)} %copy.49), calls=%async_computation.3 | async-start | bytes 1572864 | tf_op jit(solution)/shard_map/all_to_all | solution.py:172
  247.0 1.5 copy.61
  248.5 38.3 %all-to-all-done.3 = bf16[2,2,4,16,1536]{4,2,1,0,3:T(4,128)(2,1)S(1)} async-done(((bf16[2,2,4,16,1536]{4,2,1,0,3:T(4,128)(2,1)}), bf16[2,2,4,16,1536]{4,2,1,0,3:T(4,128)(2,1)S(1)}, u32[]{:S(2)}, u32[]{:S(2)}) %all-to-all-start.3) | async-done | bytes 786464 | tf_op jit(solution)/shard_map/all_to_all | solution.py:172
  286.8 7.0 %all-to-all-start.5 = ((bf16[2,2,4,16,1536]{4,2,1,0,3:T(4,128)(2,1)}), bf16[2,2,4,16,1536]{4,2,1,0,3:T(4,128)(2,1)S(1)}, u32[]{:S(2)}, u32[]{:S(2)}) async-start(bf16[2,2,4,16,1536]{4,2,1,0,3:T(4,128)(2,1)} %copy.61), calls=%async_computation.5 | async-start | bytes 1572864 | tf_op jit(solution)/shard_map/all_to_all | solution.py:172
  294.1 0.3 copy.50
  294.5 0.8 copy.64
  295.2 0.3 copy.51
  295.6 0.8 copy.65
  296.3 37.2 %all-to-all-done.5 = bf16[2,2,4,16,1536]{4,2,1,0,3:T(4,128)(2,1)S(1)} async-done(((bf16[2,2,4,16,1536]{4,2,1,0,3:T(4,128)(2,1)}), bf16[2,2,4,16,1536]{4,2,1,0,3:T(4,128)(2,1)S(1)}, u32[]{:S(2)}, u32[]{:S(2)}) %all-to-all-start.5) | async-done | bytes 786464 | tf_op jit(solution)/shard_map/all_to_all | solution.py:172
  333.8 0.3 copy.62
  334.1 0.8 copy.66
  334.9 0.3 copy.63
  335.2 0.8 copy.67
  (44 shorter events, 2.5 us)
Async XLA Ops:
  0.6 2.0 copy-start.2
  0.6 2.0 copy-start.1
  6.7 19.2 %copy-start.3 = (s32[12]{0:T(128)S(1)}, s32[12]{0:T(128)}, u32[]{:S(2)}) copy-start(s32[12]{0:T(128)} %param.13) | copy-start | bytes 148
  6.7 19.2 %copy-start.4 = (s32[12]{0:T(128)S(1)}, s32[12]{0:T(128)}, u32[]{:S(2)}) copy-start(s32[12]{0:T(128)} %param.12) | copy-start | bytes 148
  6.7 19.2 %copy-start.5 = (s32[12]{0:T(128)S(1)}, s32[12]{0:T(128)}, u32[]{:S(2)}) copy-start(s32[12]{0:T(128)} %param.11) | copy-start | bytes 148
  6.7 91.3 %all-to-all-start = ((bf16[4,2,64,1,1536]{4,1,3,0,2:T(2,128)(2,1)}), bf16[4,2,64,1,1536]{4,1,3,0,2:T(2,128)(2,1)S(1)}, u32[]{:S(2)}, u32[]{:S(2)}) async-start(bf16[4,2,64,1,1536]{4,1,3,0,2:T(2,128)(2,1)} %pad_maximum_fusion.2), calls=%async_computation | async-start | bytes 3145728 | tf_op jit(solution)/shard_map/all_to_all | solution.py:119
  110.7 20.1 %collective-permute-start = (bf16[2,1,2,32,1536]{4,2,3,1,0:T(2,128)(2,1)}, bf16[2,1,2,32,1536]{4,2,3,1,0:T(2,128)(2,1)S(1)}, u32[]{:S(2)}, u32[]{:S(2)}) collective-permute-start(bf16[2,1,2,32,1536]{4,2,3,1,0:T(2,128)(2,1)} %get-tuple-element.30), channel_id=1, source_target_pairs={{0,32},{32,64},{64,96},{96,128},{128,160},{160,192},{192,224},{224... | collective-permute-start | bytes 1179656 | tf_op jit(solution)/shard_map/ppermute | solution.py:22
  114.2 16.7 %collective-permute-start.1 = (bf16[2,1,2,32,1536]{4,2,3,1,0:T(2,128)(2,1)}, bf16[2,1,2,32,1536]{4,2,3,1,0:T(2,128)(2,1)}, u32[]{:S(2)}, u32[]{:S(2)}) collective-permute-start(bf16[2,1,2,32,1536]{4,2,3,1,0:T(2,128)(2,1)} %get-tuple-element.31), channel_id=1, source_target_pairs={{32,0},{64,32},{96,64},{128,96},{160,128},{192,160},{224,192},{256... | collective-permute-start | bytes 1179656 | tf_op jit(solution)/shard_map/ppermute | solution.py:23
  122.7 20.3 %collective-permute-start.4 = (bf16[2,1,2,32,1536]{4,2,3,1,0:T(2,128)(2,1)S(1)}, bf16[2,1,2,32,1536]{4,2,3,1,0:T(2,128)(2,1)S(1)}, u32[]{:S(2)}, u32[]{:S(2)}) collective-permute-start(bf16[2,1,2,32,1536]{4,2,3,1,0:T(2,128)(2,1)S(1)} %get-tuple-element.26), channel_id=1, source_target_pairs={{0,32},{32,64},{64,96},{96,128},{128,160},{160,192},{192,224},{224... | collective-permute-start | bytes 1179656 | tf_op jit(solution)/shard_map/ppermute | solution.py:22
  124.6 18.4 %collective-permute-start.5 = (bf16[2,1,2,32,1536]{4,2,3,1,0:T(2,128)(2,1)S(1)}, bf16[2,1,2,32,1536]{4,2,3,1,0:T(2,128)(2,1)S(1)}, u32[]{:S(2)}, u32[]{:S(2)}) collective-permute-start(bf16[2,1,2,32,1536]{4,2,3,1,0:T(2,128)(2,1)S(1)} %get-tuple-element.27), channel_id=1, source_target_pairs={{32,0},{64,32},{96,64},{128,96},{160,128},{192,160},{224,192},{256... | collective-permute-start | bytes 1179656 | tf_op jit(solution)/shard_map/ppermute | solution.py:23
  137.3 17.7 %collective-permute-start.2 = (bf16[2,4,1,32,1536]{4,3,2,1,0:T(8,128)(2,1)S(1)}, bf16[2,4,1,32,1536]{4,3,2,1,0:T(8,128)(2,1)S(1)}, u32[]{:S(2)}, u32[]{:S(2)}) collective-permute-start(bf16[2,4,1,32,1536]{4,3,2,1,0:T(8,128)(2,1)S(1)} %copy.42), channel_id=1, source_target_pairs={{0,1},{1,2},{2,3},{3,4},{4,5},{5,6},{6,7},{7,8},{8,9},{9,10},{10,1... | collective-permute-start | bytes 2359304 | tf_op jit(solution)/shard_map/ppermute | solution.py:22
  139.4 17.0 %collective-permute-start.3 = (bf16[2,4,1,32,1536]{4,3,2,1,0:T(8,128)(2,1)S(1)}, bf16[2,4,1,32,1536]{4,3,2,1,0:T(8,128)(2,1)S(1)}, u32[]{:S(2)}, u32[]{:S(2)}) collective-permute-start(bf16[2,4,1,32,1536]{4,3,2,1,0:T(8,128)(2,1)S(1)} %copy.43), channel_id=1, source_target_pairs={{1,0},{2,1},{3,2},{4,3},{5,4},{6,5},{7,6},{8,7},{9,8},{10,9},{11,1... | collective-permute-start | bytes 2359304 | tf_op jit(solution)/shard_map/ppermute | solution.py:23
  148.5 42.9 %collective-permute-start.6 = (bf16[2,4,1,32,1536]{4,3,2,1,0:T(8,128)(2,1)S(1)}, bf16[2,4,1,32,1536]{4,3,2,1,0:T(8,128)(2,1)}, u32[]{:S(2)}, u32[]{:S(2)}) collective-permute-start(bf16[2,4,1,32,1536]{4,3,2,1,0:T(8,128)(2,1)S(1)} %copy.53), channel_id=1, source_target_pairs={{0,1},{1,2},{2,3},{3,4},{4,5},{5,6},{6,7},{7,8},{8,9},{9,10},{10,1... | collective-permute-start | bytes 2359304 | tf_op jit(solution)/shard_map/ppermute | solution.py:22
  151.4 42.4 %collective-permute-start.7 = (bf16[2,4,1,32,1536]{4,3,2,1,0:T(8,128)(2,1)}, bf16[2,4,1,32,1536]{4,3,2,1,0:T(8,128)(2,1)}, u32[]{:S(2)}, u32[]{:S(2)}) collective-permute-start(bf16[2,4,1,32,1536]{4,3,2,1,0:T(8,128)(2,1)} %copy.54), channel_id=1, source_target_pairs={{1,0},{2,1},{3,2},{4,3},{5,4},{6,5},{7,6},{8,7},{9,8},{10,9},{11,1... | collective-permute-start | bytes 2359304 | tf_op jit(solution)/shard_map/ppermute | solution.py:23
  183.2 13.1 %collective-permute-start.8 = (f32[2,12,1,2,32]{4,3,2,0,1:T(2,128)S(1)}, f32[2,12,1,2,32]{4,3,2,0,1:T(2,128)S(1)}, u32[]{:S(2)}, u32[]{:S(2)}) collective-permute-start(f32[2,12,1,2,32]{4,3,2,0,1:T(2,128)S(1)} %get-tuple-element.34), channel_id=1, source_target_pairs={{0,32},{32,64},{64,96},{96,128},{128,160},{160,192},{192,224},{224... | collective-permute-start | bytes 18440 | tf_op jit(solution)/shard_map/ppermute | solution.py:22
  185.1 11.2 %collective-permute-start.9 = (f32[2,12,1,2,32]{4,3,2,0,1:T(2,128)S(1)}, f32[2,12,1,2,32]{4,3,2,0,1:T(2,128)S(1)}, u32[]{:S(2)}, u32[]{:S(2)}) collective-permute-start(f32[2,12,1,2,32]{4,3,2,0,1:T(2,128)S(1)} %get-tuple-element.35), channel_id=1, source_target_pairs={{32,0},{64,32},{96,64},{128,96},{160,128},{192,160},{224,192},{256... | collective-permute-start | bytes 18440 | tf_op jit(solution)/shard_map/ppermute | solution.py:23
  196.5 20.1 %collective-permute-start.10 = (f32[2,12,4,1,32]{4,3,2,0,1:T(1,128)S(1)}, f32[2,12,4,1,32]{4,3,2,0,1:T(1,128)S(1)}, u32[]{:S(2)}, u32[]{:S(2)}) collective-permute-start(f32[2,12,4,1,32]{4,3,2,0,1:T(1,128)S(1)} %get-tuple-element.32), channel_id=1, source_target_pairs={{0,1},{1,2},{2,3},{3,4},{4,5},{5,6},{6,7},{7,8},{8,9},{9,10},{10,1... | collective-permute-start | bytes 36872 | tf_op jit(solution)/shard_map/ppermute | solution.py:22
  198.4 18.2 %collective-permute-start.11 = (f32[2,12,4,1,32]{4,3,2,0,1:T(1,128)S(1)}, f32[2,12,4,1,32]{4,3,2,0,1:T(1,128)S(1)}, u32[]{:S(2)}, u32[]{:S(2)}) collective-permute-start(f32[2,12,4,1,32]{4,3,2,0,1:T(1,128)S(1)} %get-tuple-element.33), channel_id=1, source_target_pairs={{1,0},{2,1},{3,2},{4,3},{5,4},{6,5},{7,6},{8,7},{9,8},{10,9},{11,1... | collective-permute-start | bytes 36872 | tf_op jit(solution)/shard_map/ppermute | solution.py:23
  207.8 2.4 copy-start
  235.7 51.1 %all-to-all-start.3 = ((bf16[2,2,4,16,1536]{4,2,1,0,3:T(4,128)(2,1)}), bf16[2,2,4,16,1536]{4,2,1,0,3:T(4,128)(2,1)S(1)}, u32[]{:S(2)}, u32[]{:S(2)}) async-start(bf16[2,2,4,16,1536]{4,2,1,0,3:T(4,128)(2,1)} %copy.49), calls=%async_computation.3 | async-start | bytes 1572864 | tf_op jit(solution)/shard_map/all_to_all | solution.py:172
  286.8 46.7 %all-to-all-start.5 = ((bf16[2,2,4,16,1536]{4,2,1,0,3:T(4,128)(2,1)}), bf16[2,2,4,16,1536]{4,2,1,0,3:T(4,128)(2,1)S(1)}, u32[]{:S(2)}, u32[]{:S(2)}) async-start(bf16[2,2,4,16,1536]{4,2,1,0,3:T(4,128)(2,1)} %copy.61), calls=%async_computation.5 | async-start | bytes 1572864 | tf_op jit(solution)/shard_map/all_to_all | solution.py:172

commit v5 on v3

--- a/solution.py
+++ b/solution.py
@@ -25,34 +25,37 @@
     return array
 
 
-def window_mask(h, reach_ref, live_ref, own_frames, own_rows, cols, rim_frames, rim_rows):
+def window_mask(h, reach_ref, gap_ref):
+    return (
+        (gap_ref[0] <= reach_ref[0, h])
+        & (gap_ref[1] <= reach_ref[1, h])
+        & (gap_ref[2] <= reach_ref[2, h])
+    )
+
+
+def gap_table(live, own_frames, own_rows, cols, rim_frames, rim_rows):
     own_n = own_frames * own_rows * cols
     rim_n = rim_frames * rim_rows * cols
-    own_i = lax.broadcasted_iota(jnp.int32, (own_n, rim_n), 0)
-    rim_j = lax.broadcasted_iota(jnp.int32, (own_n, rim_n), 1)
+    own_i = jnp.arange(own_n, dtype=jnp.int32)[:, None]
+    rim_j = jnp.arange(rim_n, dtype=jnp.int32)[None, :]
     own_t = own_i // (own_rows * cols)
     own_r = (own_i // cols) % own_rows
     own_c = own_i % cols
     rim_t = rim_j // (rim_rows * cols) - 1
     rim_r = (rim_j // cols) % rim_rows - 1
     rim_c = rim_j % cols
-    gap_t = jnp.abs(own_t - rim_t)
+    gap_t = jnp.where(live, jnp.abs(own_t - rim_t), own_n + rim_n)
     gap_r = jnp.abs(own_r - rim_r)
     gap_w = jnp.abs(own_c // TW - rim_c // TW)
-    inside = (
-        (gap_t <= reach_ref[0, h])
-        & (gap_r <= reach_ref[1, h])
-        & (gap_w <= reach_ref[2, h])
-    )
-    return inside & (live_ref[...] > 0)
-
-
-def make_query_kernel(dims):
+    return jnp.stack(jnp.broadcast_arrays(gap_t, gap_r, gap_w)).astype(jnp.int32)
+
+
+def make_query_kernel():
     score_scale = 1.0 / math.sqrt(DH)
 
-    def kernel(reach_ref, q_ref, do_ref, k_ref, v_ref, live_ref, og_ref, lse_ref, dot_ref):
+    def kernel(reach_ref, q_ref, do_ref, k_ref, v_ref, gap_ref, og_ref, lse_ref, dot_ref):
         h = pl.program_id(0)
-        window = window_mask(h, reach_ref, live_ref, *dims)
+        window = window_mask(h, reach_ref, gap_ref)
         q_now = q_ref[...]
         do_now = do_ref[...]
         k_rim = k_ref[...]
@@ -79,12 +82,12 @@
     return kernel
 
 
-def make_key_kernel(dims):
+def make_key_kernel():
     score_scale = 1.0 / math.sqrt(DH)
 
-    def kernel(reach_ref, k_ref, v_ref, q_ref, do_ref, lse_ref, dot_ref, live_ref, gkv_ref):
+    def kernel(reach_ref, k_ref, v_ref, q_ref, do_ref, lse_ref, dot_ref, gap_ref, gkv_ref):
         h = pl.program_id(0)
-        window = window_mask(h, reach_ref, live_ref, *dims)
+        window = window_mask(h, reach_ref, gap_ref)
         k_now = k_ref[...]
         v_now = v_ref[...]
         q_rim = q_ref[...]
@@ -132,7 +135,8 @@
         & (frame_of < time_count * frames_dev)
         & (row_of >= 0)
         & (row_of < height)
-    ).astype(jnp.int32).reshape(1, rim_n)
+    ).reshape(1, rim_n)
+    gaps = gap_table(live, *dims)
     reach = jnp.stack([reach_time, reach_height, reach_width]).astype(jnp.int32)
 
     def own_spec(which):
@@ -141,12 +145,12 @@
     def rim_spec(which):
         return pl.BlockSpec((None, rim_n, DH), lambda h, r: (which, 0, h))
 
-    live_spec = pl.BlockSpec((1, rim_n), lambda h, r: (0, 0))
+    live_spec = pl.BlockSpec((3, own_n, rim_n), lambda h, r: (0, 0, 0))
     pair_spec = pl.BlockSpec((2, own_n, DH), lambda h, r: (0, 0, h))
     stat_spec = pl.BlockSpec((None, own_n, 1), lambda h, r: (h, 0, 0))
 
     og, lse, dots = pl.pallas_call(
-        make_query_kernel(dims),
+        make_query_kernel(),
         grid_spec=pltpu.PrefetchScalarGridSpec(
             num_scalar_prefetch=1,
             grid=(heads,),
@@ -158,7 +162,7 @@
             jax.ShapeDtypeStruct((heads, own_n, 1), jnp.float32),
             jax.ShapeDtypeStruct((heads, own_n, 1), jnp.float32),
         ],
-    )(reach, own_flat, own_flat, kv_rim, kv_rim, live)
+    )(reach, own_flat, own_flat, kv_rim, kv_rim, gaps)
 
     def back_to_columns(pair):
         shaped = pair.reshape(2, frames_dev, rows_dev, col_count, features)
@@ -172,7 +176,7 @@
         pl.BlockSpec((None, None, 1, rim_n), lambda h, r, w=w: (w, h, 0, 0)) for w in range(2)
     ]
     gkv = pl.pallas_call(
-        make_key_kernel(dims),
+        make_key_kernel(),
         grid_spec=pltpu.PrefetchScalarGridSpec(
             num_scalar_prefetch=1,
             grid=(heads,),
@@ -182,7 +186,7 @@
             out_specs=pair_spec,
         ),
         out_shape=jax.ShapeDtypeStruct((2, own_n, features), jnp.bfloat16),
-    )(reach, own_flat, own_flat, qd_rim, qd_rim, stat_rim, stat_rim, live)
+    )(reach, own_flat, own_flat, qd_rim, qd_rim, stat_rim, stat_rim, gaps)
     gkv_back = back_to_columns(gkv)
     return (og_back[0], og_back[1], gkv_back[0], gkv_back[1])
 

time: 290 us -> 288 us (level)
  blocking collectives: 98.8 us -> 0 us
  waiting for transfers between devices: 78.6 us -> 155 us
  starting transfers between devices: 52.9 us -> 74.1 us
    all_to_all x1 -> x0, blocking collectives: 98.8 us -> none  [body(): lax.all_to_all(stacked, 'ulysses', split_axis=2, concat_axis=3, tiled=True)]
    all_to_all x0 -> x1, waiting for transfers between devices: none -> 77.8 us  [body(): lax.all_to_all(stacked, 'ulysses', split_axis=2, concat_axis=3, tiled=True)]
    all_to_all x0 -> x1, starting transfers between devices: none -> 20.4 us  [body(): lax.all_to_all(stacked, 'ulysses', split_axis=2, concat_axis=3, tiled=True)]
  transfers between devices with their start and end apart: 14 -> 15, of which waited for: 9 -> 10; matrix products, arithmetic and copies ran while one was open for 5% -> 6% of each run, Pallas kernels for 4% -> 4%
where the time goes in v5:
time: 288 us; the launch traced here: 287 us
  waiting for transfers between devices  155 us (54%)
  starting transfers between devices  74.1 us (26%)
  Pallas kernels  24.8 us (9%)
  local copies, waits for them, and re-layouts  18.7 us (6%)
  other arithmetic  13.2 us (5%)
    all_to_all x1, waiting for transfers between devices, body(): lax.all_to_all(stacked, 'ulysses', split_axis=2, concat_axis=3, tiled=True)  77.8 us
    all_to_all x2, waiting for transfers between devices, back_to_columns(): lax.all_to_all(shaped, 'ulysses', split_axis=3, concat_axis=2, tiled=True)  41.9 us
    ppermute x6, starting transfers between devices, with_halo(): before = lax.ppermute(last, axis, up)  22.3 us
    all_to_all x2, starting transfers between devices, back_to_columns(): lax.all_to_all(shaped, 'ulysses', split_axis=3, concat_axis=2, tiled=True)  20.7 us
    all_to_all x1, starting transfers between devices, body(): lax.all_to_all(stacked, 'ulysses', split_axis=2, concat_axis=3, tiled=True)  20.4 us
    ppermute x6, waiting for transfers between devices, with_halo(): after = lax.ppermute(initial, axis, down)  17.8 us
    ppermute x6, waiting for transfers between devices, with_halo(): before = lax.ppermute(last, axis, up)  17.5 us
    pallas_call x1, Pallas kernels, body(): pl.pallas_call(make_query_kernel(), grid_spec=pltpu.PrefetchScalarGridSpe...  13.3 us
  transfers between devices with their start and end apart: 15, of which 10 were waited for; matrix products, arithmetic and copies ran while one was open for 6% of the time, Pallas kernels for 4%

profile of v5, /device:TPU:1, one launch (start us, length us, event | category | flops | bytes accessed | tf_op | source)
XLA Modules:
  0.0 286.9 jit_solution(14652224050913995904)
XLA Ops:
  0.7 2.0 copy_bitcast_fusion
  2.7 0.8 copy_bitcast_fusion.2
  3.5 3.3 %pad_maximum_fusion.2 = bf16[4,2,64,1,1536]{4,1,3,0,2:T(2,128)(2,1)} fusion(bf16[1,2,64,1,1536]{4,1,3,0,2:T(2,128)(2,1)S(1)} %get-tuple-element.34, bf16[1,2,64,1,1536]{4,1,3,0,2:T(2,128)(2,1)S(1)} %get-tuple-element.35, bf16[1,2,64,1,1536]{4,1,3,0,2:T(2,128)(2,1)S(1)} %get-tuple-element.36, bf16[1,2,64,1,1536]{4,1,3,0,2:T(2,128)(2,1)S(1)} %get-tuple-element.37), kind=kLoop, calls=%fused_computation.2 | loop fusion | flops 2359296 | bytes 3145728 | tf_op jit(solution)/shard_map/stack | solution.py:119
  6.7 20.4 %all-to-all-start = ((bf16[4,2,64,1,1536]{4,1,3,0,2:T(2,128)(2,1)}), bf16[4,2,64,1,1536]{4,1,3,0,2:T(2,128)(2,1)S(1)}, u32[]{:S(2)}, u32[]{:S(2)}) async-start(bf16[4,2,64,1,1536]{4,1,3,0,2:T(2,128)(2,1)} %pad_maximum_fusion.2), calls=%async_computation | async-start | bytes 3145728 | tf_op jit(solution)/shard_map/all_to_all | solution.py:120
  27.2 77.8 %all-to-all-done = bf16[4,2,64,1,1536]{4,1,3,0,2:T(2,128)(2,1)S(1)} async-done(((bf16[4,2,64,1,1536]{4,1,3,0,2:T(2,128)(2,1)}), bf16[4,2,64,1,1536]{4,1,3,0,2:T(2,128)(2,1)S(1)}, u32[]{:S(2)}, u32[]{:S(2)}) %all-to-all-start) | async-done | bytes 1572896 | tf_op jit(solution)/shard_map/all_to_all | solution.py:120
  105.0 0.9 copy.53
  105.9 0.1 slice_bitcast_fusion
  106.0 1.1 copy-done
  107.0 0.1 fusion.21
  107.1 3.2 %collective-permute-start = (bf16[2,1,2,32,1536]{4,3,2,1,0:T(8,128)(2,1)S(1)}, bf16[2,1,2,32,1536]{4,3,2,1,0:T(8,128)(2,1)S(1)}, u32[]{:S(2)}, u32[]{:S(2)}) collective-permute-start(bf16[2,1,2,32,1536]{4,3,2,1,0:T(8,128)(2,1)S(1)} %get-tuple-element.28), channel_id=1, source_target_pairs={{0,32},{32,64},{64,96},{96,128},{128,160},{160,192},{192,224},{224... | collective-permute-start | bytes 1179656 | tf_op jit(solution)/shard_map/ppermute | solution.py:22
  110.4 1.3 collective-permute-start.1
  111.7 6.5 %collective-permute-done = bf16[2,1,2,32,1536]{4,3,2,1,0:T(8,128)(2,1)S(1)} collective-permute-done((bf16[2,1,2,32,1536]{4,3,2,1,0:T(8,128)(2,1)S(1)}, bf16[2,1,2,32,1536]{4,3,2,1,0:T(8,128)(2,1)S(1)}, u32[]{:S(2)}, u32[]{:S(2)}) %collective-permute-start) | collective-permute-done | bytes 393248 | tf_op jit(solution)/shard_map/ppermute | solution.py:22
  118.2 3.8 %collective-permute-done.1 = bf16[2,1,2,32,1536]{4,3,2,1,0:T(8,128)(2,1)S(1)} collective-permute-done((bf16[2,1,2,32,1536]{4,3,2,1,0:T(8,128)(2,1)S(1)}, bf16[2,1,2,32,1536]{4,3,2,1,0:T(8,128)(2,1)S(1)}, u32[]{:S(2)}, u32[]{:S(2)}) %collective-permute-start.1) | collective-permute-done | bytes 393248 | tf_op jit(solution)/shard_map/ppermute | solution.py:23
  122.0 0.2 pad_maximum_fusion.3
  122.2 0.1 fusion.17
  122.3 2.1 collective-permute-start.2
  124.4 3.0 %collective-permute-start.3 = (bf16[2,4,1,32,1536]{4,3,2,1,0:T(8,128)(2,1)S(1)}, bf16[2,4,1,32,1536]{4,3,2,1,0:T(8,128)(2,1)S(1)}, u32[]{:S(2)}, u32[]{:S(2)}) collective-permute-start(bf16[2,4,1,32,1536]{4,3,2,1,0:T(8,128)(2,1)S(1)} %get-tuple-element.19), channel_id=1, source_target_pairs={{1,0},{2,1},{3,2},{4,3},{5,4},{6,5},{7,6},{8,7},{9,8},{10,9},{11,1... | collective-permute-start | bytes 2359304 | tf_op jit(solution)/shard_map/ppermute | solution.py:23
  127.4 0.6 pad_add_fusion.1.reach_ref
  128.0 0.1 abs_select_fusion
  128.1 0.1 subtract_abs_fusion
  128.3 1.0 pad_add_fusion.gap_ref
  129.2 4.1 %collective-permute-done.2 = bf16[2,4,1,32,1536]{4,3,2,1,0:T(8,128)(2,1)S(1)} collective-permute-done((bf16[2,4,1,32,1536]{4,3,2,1,0:T(8,128)(2,1)S(1)}, bf16[2,4,1,32,1536]{4,3,2,1,0:T(8,128)(2,1)S(1)}, u32[]{:S(2)}, u32[]{:S(2)}) %collective-permute-start.2) | collective-permute-done | bytes 786464 | tf_op jit(solution)/shard_map/ppermute | solution.py:22
  133.3 4.4 %collective-permute-done.3 = bf16[2,4,1,32,1536]{4,3,2,1,0:T(8,128)(2,1)S(1)} collective-permute-done((bf16[2,4,1,32,1536]{4,3,2,1,0:T(8,128)(2,1)S(1)}, bf16[2,4,1,32,1536]{4,3,2,1,0:T(8,128)(2,1)S(1)}, u32[]{:S(2)}, u32[]{:S(2)}) %collective-permute-start.3) | collective-permute-done | bytes 786464 | tf_op jit(solution)/shard_map/ppermute | solution.py:23
  137.7 1.9 pad_maximum_fusion
  139.6 13.3 %shard_map.102 = (bf16[2,128,1536]{2,1,0:T(8,128)(2,1)}, f32[12,128,1]{2,1,0:T(8,128)}, f32[12,128,1]{2,1,0:T(8,128)}) custom-call(s32[3,12]{1,0:T(4,128)} %pad_add_fusion.1.reach_ref, bf16[4,128,1536]{2,1,0:T(8,128)(2,1)} %bitcast.38, bf16[4,128,1536]{2,1,0:T(8,128)(2,1)} %bitcast.39, bf16[2,512,1536]{2,1,0:T(8,128)(2,1)} %bitcast.44, ...), custom_call_target="tpu_custom_call" | custom-call | tf_op jit(solution)/shard_map/pallas_call | solution.py:152
  152.9 2.8 copy.35
  155.7 7.3 %all-to-all-start.1 = ((bf16[2,2,2,32,1536]{4,2,1,0,3:T(2,128)(2,1)}), bf16[2,2,2,32,1536]{4,2,1,0,3:T(2,128)(2,1)S(1)}, u32[]{:S(2)}, u32[]{:S(2)}) async-start(bf16[2,2,2,32,1536]{4,2,1,0,3:T(2,128)(2,1)} %copy.35), calls=%async_computation.1 | async-start | bytes 1572864 | tf_op jit(solution)/shard_map/all_to_all | solution.py:169
  163.1 3.2 %collective-permute-start.4 = (bf16[2,1,2,32,1536]{4,3,2,1,0:T(8,128)(2,1)S(1)}, bf16[2,1,2,32,1536]{4,3,2,1,0:T(8,128)(2,1)S(1)}, u32[]{:S(2)}, u32[]{:S(2)}) collective-permute-start(bf16[2,1,2,32,1536]{4,3,2,1,0:T(8,128)(2,1)S(1)} %get-tuple-element.24), channel_id=1, source_target_pairs={{0,32},{32,64},{64,96},{96,128},{128,160},{160,192},{192,224},{224... | collective-permute-start | bytes 1179656 | tf_op jit(solution)/shard_map/ppermute | solution.py:22
  166.3 1.3 collective-permute-start.5
  167.6 6.9 %collective-permute-done.4 = bf16[2,1,2,32,1536]{4,3,2,1,0:T(8,128)(2,1)S(1)} collective-permute-done((bf16[2,1,2,32,1536]{4,3,2,1,0:T(8,128)(2,1)S(1)}, bf16[2,1,2,32,1536]{4,3,2,1,0:T(8,128)(2,1)S(1)}, u32[]{:S(2)}, u32[]{:S(2)}) %collective-permute-start.4) | collective-permute-done | bytes 393248 | tf_op jit(solution)/shard_map/ppermute | solution.py:22
  174.5 5.0 %collective-permute-done.5 = bf16[2,1,2,32,1536]{4,3,2,1,0:T(8,128)(2,1)S(1)} collective-permute-done((bf16[2,1,2,32,1536]{4,3,2,1,0:T(8,128)(2,1)S(1)}, bf16[2,1,2,32,1536]{4,3,2,1,0:T(8,128)(2,1)S(1)}, u32[]{:S(2)}, u32[]{:S(2)}) %collective-permute-start.5) | collective-permute-done | bytes 393248 | tf_op jit(solution)/shard_map/ppermute | solution.py:23
  179.5 0.2 pad_maximum_fusion.4
  179.7 1.3 fusion.16
  181.0 4.2 %collective-permute-start.6 = (bf16[2,4,1,32,1536]{4,3,2,1,0:T(8,128)(2,1)}, bf16[2,4,1,32,1536]{4,3,2,1,0:T(8,128)(2,1)S(1)}, u32[]{:S(2)}, u32[]{:S(2)}) collective-permute-start(bf16[2,4,1,32,1536]{4,3,2,1,0:T(8,128)(2,1)} %get-tuple-element.14), channel_id=1, source_target_pairs={{0,1},{1,2},{2,3},{3,4},{4,5},{5,6},{6,7},{7,8},{8,9},{9,10},{10,1... | collective-permute-start | bytes 2359304 | tf_op jit(solution)/shard_map/ppermute | solution.py:22
  185.2 1.9 collective-permute-start.7
  187.2 1.4 reduce
  188.6 0.1 stack.52
  188.7 1.4 reduce.1
  190.1 0.1 stack.53
  190.3 4.6 %collective-permute-start.8 = (f32[2,12,1,2,32]{4,3,2,0,1:T(2,128)S(1)}, f32[2,12,1,2,32]{4,3,2,0,1:T(2,128)S(1)}, u32[]{:S(2)}, u32[]{:S(2)}) collective-permute-start(f32[2,12,1,2,32]{4,3,2,0,1:T(2,128)S(1)} %get-tuple-element.32), channel_id=1, source_target_pairs={{0,32},{32,64},{64,96},{96,128},{128,160},{160,192},{192,224},{224... | collective-permute-start | bytes 18440 | tf_op jit(solution)/shard_map/ppermute | solution.py:22
  194.8 1.3 collective-permute-start.9
  196.1 3.3 %collective-permute-done.9 = f32[2,12,1,2,32]{4,3,2,0,1:T(2,128)S(1)} collective-permute-done((f32[2,12,1,2,32]{4,3,2,0,1:T(2,128)S(1)}, f32[2,12,1,2,32]{4,3,2,0,1:T(2,128)S(1)}, u32[]{:S(2)}, u32[]{:S(2)}) %collective-permute-start.9) | collective-permute-done | bytes 6176 | tf_op jit(solution)/shard_map/ppermute | solution.py:23
  199.5 0.1 fusion.22
  199.6 5.1 %collective-permute-start.10 = (f32[2,12,4,1,32]{4,3,2,0,1:T(1,128)S(1)}, f32[2,12,4,1,32]{4,3,2,0,1:T(1,128)S(1)}, u32[]{:S(2)}, u32[]{:S(2)}) collective-permute-start(f32[2,12,4,1,32]{4,3,2,0,1:T(1,128)S(1)} %get-tuple-element.30), channel_id=1, source_target_pairs={{0,1},{1,2},{2,3},{3,4},{4,5},{5,6},{6,7},{7,8},{8,9},{9,10},{10,1... | collective-permute-start | bytes 36872 | tf_op jit(solution)/shard_map/ppermute | solution.py:22
  204.6 1.9 collective-permute-start.11
  206.6 1.3 collective-permute-done.7
  207.9 2.9 pad_maximum_fusion.1
  210.8 0.2 pad_maximum_fusion.5
  210.9 0.2 reshape.496
  211.1 0.7 copy.46.lse_ref.dot_ref
  211.8 11.5 %shard_map.103 = bf16[2,128,1536]{2,1,0:T(8,128)(2,1)} custom-call(s32[3,12]{1,0:T(4,128)} %pad_add_fusion.1.reach_ref, bf16[4,128,1536]{2,1,0:T(8,128)(2,1)} %bitcast.40, bf16[4,128,1536]{2,1,0:T(8,128)(2,1)} %bitcast.41, bf16[2,512,1536]{2,1,0:T(8,128)(2,1)} %bitcast.42, bf16[2,512,1536]{2,1,0:T(8,128)(2,1)} %bitcast.43, ...), custom_call_target="tpu_custom_call" | custom-call | tf_op jit(solution)/shard_map/pallas_call | solution.py:178
  223.3 2.8 copy.39
  226.1 13.4 %all-to-all-start.2 = ((bf16[2,2,2,32,1536]{4,2,1,0,3:T(2,128)(2,1)}), bf16[2,2,2,32,1536]{4,2,1,0,3:T(2,128)(2,1)S(1)}, u32[]{:S(2)}, u32[]{:S(2)}) async-start(bf16[2,2,2,32,1536]{4,2,1,0,3:T(2,128)(2,1)} %copy.39), calls=%async_computation.2 | async-start | bytes 1572864 | tf_op jit(solution)/shard_map/all_to_all | solution.py:169
  239.5 0.5 fusion.20
  240.1 0.3 copy.36
  240.4 0.8 copy.42
  241.2 0.3 copy.37
  241.5 0.8 copy.43
  242.3 41.9 %all-to-all-done.2 = bf16[2,2,2,32,1536]{4,2,1,0,3:T(2,128)(2,1)S(1)} async-done(((bf16[2,2,2,32,1536]{4,2,1,0,3:T(2,128)(2,1)}), bf16[2,2,2,32,1536]{4,2,1,0,3:T(2,128)(2,1)S(1)}, u32[]{:S(2)}, u32[]{:S(2)}) %all-to-all-start.2) | async-done | bytes 786464 | tf_op jit(solution)/shard_map/all_to_all | solution.py:169
  284.2 0.5 fusion.18
  284.7 0.3 copy.40
  285.0 0.8 copy.44
  285.8 0.3 copy.41
  286.1 0.8 copy.45
  (28 shorter events, 0.2 us)
Async XLA Ops:
  0.6 2.0 copy-start.2
  0.6 2.0 copy-start.1
  6.7 98.3 %all-to-all-start = ((bf16[4,2,64,1,1536]{4,1,3,0,2:T(2,128)(2,1)}), bf16[4,2,64,1,1536]{4,1,3,0,2:T(2,128)(2,1)S(1)}, u32[]{:S(2)}, u32[]{:S(2)}) async-start(bf16[4,2,64,1,1536]{4,1,3,0,2:T(2,128)(2,1)} %pad_maximum_fusion.2), calls=%async_computation | async-start | bytes 3145728 | tf_op jit(solution)/shard_map/all_to_all | solution.py:120
  105.9 1.2 copy-start
  107.1 11.1 %collective-permute-start = (bf16[2,1,2,32,1536]{4,3,2,1,0:T(8,128)(2,1)S(1)}, bf16[2,1,2,32,1536]{4,3,2,1,0:T(8,128)(2,1)S(1)}, u32[]{:S(2)}, u32[]{:S(2)}) collective-permute-start(bf16[2,1,2,32,1536]{4,3,2,1,0:T(8,128)(2,1)S(1)} %get-tuple-element.28), channel_id=1, source_target_pairs={{0,32},{32,64},{64,96},{96,128},{128,160},{160,192},{192,224},{224... | collective-permute-start | bytes 1179656 | tf_op jit(solution)/shard_map/ppermute | solution.py:22
  110.4 11.6 %collective-permute-start.1 = (bf16[2,1,2,32,1536]{4,3,2,1,0:T(8,128)(2,1)S(1)}, bf16[2,1,2,32,1536]{4,3,2,1,0:T(8,128)(2,1)S(1)}, u32[]{:S(2)}, u32[]{:S(2)}) collective-permute-start(bf16[2,1,2,32,1536]{4,3,2,1,0:T(8,128)(2,1)S(1)} %get-tuple-element.29), channel_id=1, source_target_pairs={{32,0},{64,32},{96,64},{128,96},{160,128},{192,160},{224,192},{256... | collective-permute-start | bytes 1179656 | tf_op jit(solution)/shard_map/ppermute | solution.py:23
  122.2 5.2 %copy-start.3 = (s32[12]{0:T(128)S(1)}, s32[12]{0:T(128)}, u32[]{:S(2)}) copy-start(s32[12]{0:T(128)} %param.13) | copy-start | bytes 148
  122.2 5.2 %copy-start.4 = (s32[12]{0:T(128)S(1)}, s32[12]{0:T(128)}, u32[]{:S(2)}) copy-start(s32[12]{0:T(128)} %param.12) | copy-start | bytes 148
  122.2 5.2 %copy-start.5 = (s32[12]{0:T(128)S(1)}, s32[12]{0:T(128)}, u32[]{:S(2)}) copy-start(s32[12]{0:T(128)} %param.11) | copy-start | bytes 148
  122.3 11.0 %collective-permute-start.2 = (bf16[2,4,1,32,1536]{4,3,2,1,0:T(8,128)(2,1)S(1)}, bf16[2,4,1,32,1536]{4,3,2,1,0:T(8,128)(2,1)S(1)}, u32[]{:S(2)}, u32[]{:S(2)}) collective-permute-start(bf16[2,4,1,32,1536]{4,3,2,1,0:T(8,128)(2,1)S(1)} %get-tuple-element.18), channel_id=1, source_target_pairs={{0,1},{1,2},{2,3},{3,4},{4,5},{5,6},{6,7},{7,8},{8,9},{9,10},{10,1... | collective-permute-start | bytes 2359304 | tf_op jit(solution)/shard_map/ppermute | solution.py:22
  124.4 13.3 %collective-permute-start.3 = (bf16[2,4,1,32,1536]{4,3,2,1,0:T(8,128)(2,1)S(1)}, bf16[2,4,1,32,1536]{4,3,2,1,0:T(8,128)(2,1)S(1)}, u32[]{:S(2)}, u32[]{:S(2)}) collective-permute-start(bf16[2,4,1,32,1536]{4,3,2,1,0:T(8,128)(2,1)S(1)} %get-tuple-element.19), channel_id=1, source_target_pairs={{1,0},{2,1},{3,2},{4,3},{5,4},{6,5},{7,6},{8,7},{9,8},{10,9},{11,1... | collective-permute-start | bytes 2359304 | tf_op jit(solution)/shard_map/ppermute | solution.py:23
  155.7 70.4 %all-to-all-start.1 = ((bf16[2,2,2,32,1536]{4,2,1,0,3:T(2,128)(2,1)}), bf16[2,2,2,32,1536]{4,2,1,0,3:T(2,128)(2,1)S(1)}, u32[]{:S(2)}, u32[]{:S(2)}) async-start(bf16[2,2,2,32,1536]{4,2,1,0,3:T(2,128)(2,1)} %copy.35), calls=%async_computation.1 | async-start | bytes 1572864 | tf_op jit(solution)/shard_map/all_to_all | solution.py:169
  163.1 11.4 %collective-permute-start.4 = (bf16[2,1,2,32,1536]{4,3,2,1,0:T(8,128)(2,1)S(1)}, bf16[2,1,2,32,1536]{4,3,2,1,0:T(8,128)(2,1)S(1)}, u32[]{:S(2)}, u32[]{:S(2)}) collective-permute-start(bf16[2,1,2,32,1536]{4,3,2,1,0:T(8,128)(2,1)S(1)} %get-tuple-element.24), channel_id=1, source_target_pairs={{0,32},{32,64},{64,96},{96,128},{128,160},{160,192},{192,224},{224... | collective-permute-start | bytes 1179656 | tf_op jit(solution)/shard_map/ppermute | solution.py:22
  166.3 13.3 %collective-permute-start.5 = (bf16[2,1,2,32,1536]{4,3,2,1,0:T(8,128)(2,1)S(1)}, bf16[2,1,2,32,1536]{4,3,2,1,0:T(8,128)(2,1)S(1)}, u32[]{:S(2)}, u32[]{:S(2)}) collective-permute-start(bf16[2,1,2,32,1536]{4,3,2,1,0:T(8,128)(2,1)S(1)} %get-tuple-element.25), channel_id=1, source_target_pairs={{32,0},{64,32},{96,64},{128,96},{160,128},{192,160},{224,192},{256... | collective-permute-start | bytes 1179656 | tf_op jit(solution)/shard_map/ppermute | solution.py:23
  181.0 25.5 %collective-permute-start.6 = (bf16[2,4,1,32,1536]{4,3,2,1,0:T(8,128)(2,1)}, bf16[2,4,1,32,1536]{4,3,2,1,0:T(8,128)(2,1)S(1)}, u32[]{:S(2)}, u32[]{:S(2)}) collective-permute-start(bf16[2,4,1,32,1536]{4,3,2,1,0:T(8,128)(2,1)} %get-tuple-element.14), channel_id=1, source_target_pairs={{0,1},{1,2},{2,3},{3,4},{4,5},{5,6},{6,7},{7,8},{8,9},{9,10},{10,1... | collective-permute-start | bytes 2359304 | tf_op jit(solution)/shard_map/ppermute | solution.py:22
  185.2 22.7 %collective-permute-start.7 = (bf16[2,4,1,32,1536]{4,3,2,1,0:T(8,128)(2,1)}, bf16[2,4,1,32,1536]{4,3,2,1,0:T(8,128)(2,1)}, u32[]{:S(2)}, u32[]{:S(2)}) collective-permute-start(bf16[2,4,1,32,1536]{4,3,2,1,0:T(8,128)(2,1)} %get-tuple-element.15), channel_id=1, source_target_pairs={{1,0},{2,1},{3,2},{4,3},{5,4},{6,5},{7,6},{8,7},{9,8},{10,9},{11,1... | collective-permute-start | bytes 2359304 | tf_op jit(solution)/shard_map/ppermute | solution.py:23
  190.3 5.9 %collective-permute-start.8 = (f32[2,12,1,2,32]{4,3,2,0,1:T(2,128)S(1)}, f32[2,12,1,2,32]{4,3,2,0,1:T(2,128)S(1)}, u32[]{:S(2)}, u32[]{:S(2)}) collective-permute-start(f32[2,12,1,2,32]{4,3,2,0,1:T(2,128)S(1)} %get-tuple-element.32), channel_id=1, source_target_pairs={{0,32},{32,64},{64,96},{96,128},{128,160},{160,192},{192,224},{224... | collective-permute-start | bytes 18440 | tf_op jit(solution)/shard_map/ppermute | solution.py:22
  194.8 4.6 %collective-permute-start.9 = (f32[2,12,1,2,32]{4,3,2,0,1:T(2,128)S(1)}, f32[2,12,1,2,32]{4,3,2,0,1:T(2,128)S(1)}, u32[]{:S(2)}, u32[]{:S(2)}) collective-permute-start(f32[2,12,1,2,32]{4,3,2,0,1:T(2,128)S(1)} %get-tuple-element.33), channel_id=1, source_target_pairs={{32,0},{64,32},{96,64},{128,96},{160,128},{192,160},{224,192},{256... | collective-permute-start | bytes 18440 | tf_op jit(solution)/shard_map/ppermute | solution.py:23
  199.6 11.2 %collective-permute-start.10 = (f32[2,12,4,1,32]{4,3,2,0,1:T(1,128)S(1)}, f32[2,12,4,1,32]{4,3,2,0,1:T(1,128)S(1)}, u32[]{:S(2)}, u32[]{:S(2)}) collective-permute-start(f32[2,12,4,1,32]{4,3,2,0,1:T(1,128)S(1)} %get-tuple-element.30), channel_id=1, source_target_pairs={{0,1},{1,2},{2,3},{3,4},{4,5},{5,6},{6,7},{7,8},{8,9},{9,10},{10,1... | collective-permute-start | bytes 36872 | tf_op jit(solution)/shard_map/ppermute | solution.py:22
  204.6 6.1 %collective-permute-start.11 = (f32[2,12,4,1,32]{4,3,2,0,1:T(1,128)S(1)}, f32[2,12,4,1,32]{4,3,2,0,1:T(1,128)S(1)}, u32[]{:S(2)}, u32[]{:S(2)}) collective-permute-start(f32[2,12,4,1,32]{4,3,2,0,1:T(1,128)S(1)} %get-tuple-element.31), channel_id=1, source_target_pairs={{1,0},{2,1},{3,2},{4,3},{5,4},{6,5},{7,6},{8,7},{9,8},{10,9},{11,1... | collective-permute-start | bytes 36872 | tf_op jit(solution)/shard_map/ppermute | solution.py:23
  226.1 58.1 %all-to-all-start.2 = ((bf16[2,2,2,32,1536]{4,2,1,0,3:T(2,128)(2,1)}), bf16[2,2,2,32,1536]{4,2,1,0,3:T(2,128)(2,1)S(1)}, u32[]{:S(2)}, u32[]{:S(2)}) async-start(bf16[2,2,2,32,1536]{4,2,1,0,3:T(2,128)(2,1)} %copy.39), calls=%async_computation.2 | async-start | bytes 1572864 | tf_op jit(solution)/shard_map/all_to_all | solution.py:169

commit v6 on v5

--- a/solution.py
+++ b/solution.py
@@ -10,6 +10,7 @@
 DH = 128
 HEADS = 12
 TW = 8
+PER_STEP = 2
 
 
 def with_halo(array, sides, width):
@@ -54,12 +55,13 @@
     score_scale = 1.0 / math.sqrt(DH)
 
     def kernel(reach_ref, q_ref, do_ref, k_ref, v_ref, gap_ref, og_ref, lse_ref, dot_ref):
-        h = pl.program_id(0)
-        window = window_mask(h, reach_ref, gap_ref)
-        q_now = q_ref[...]
-        do_now = do_ref[...]
-        k_rim = k_ref[...]
-        v_rim = v_ref[...]
+      for j in range(PER_STEP):
+        lanes = pl.ds(j * DH, DH)
+        window = window_mask(pl.program_id(0) * PER_STEP + j, reach_ref, gap_ref)
+        q_now = q_ref[:, lanes]
+        do_now = do_ref[:, lanes]
+        k_rim = k_ref[:, lanes]
+        v_rim = v_ref[:, lanes]
         nt = (((1,), (1,)), ((), ()))
         scores = lax.dot_general(q_now, k_rim, nt, preferred_element_type=jnp.float32) * score_scale
         scores = jnp.where(window, scores, -jnp.inf)
@@ -74,10 +76,10 @@
         grad_weights = lax.dot_general(do_now, v_rim, nt, preferred_element_type=jnp.float32)
         grad_scores = (weights * (grad_weights - row_dot)).astype(jnp.bfloat16)
         grad_q = jnp.dot(grad_scores, k_rim, preferred_element_type=jnp.float32) * score_scale
-        og_ref[0] = out_now
-        og_ref[1] = grad_q.astype(jnp.bfloat16)
-        lse_ref[...] = log_total
-        dot_ref[...] = row_dot
+        og_ref[0, :, lanes] = out_now
+        og_ref[1, :, lanes] = grad_q.astype(jnp.bfloat16)
+        lse_ref[j] = log_total
+        dot_ref[j] = row_dot
 
     return kernel
 
@@ -86,23 +88,24 @@
     score_scale = 1.0 / math.sqrt(DH)
 
     def kernel(reach_ref, k_ref, v_ref, q_ref, do_ref, lse_ref, dot_ref, gap_ref, gkv_ref):
-        h = pl.program_id(0)
-        window = window_mask(h, reach_ref, gap_ref)
-        k_now = k_ref[...]
-        v_now = v_ref[...]
-        q_rim = q_ref[...]
-        do_rim = do_ref[...]
+      for j in range(PER_STEP):
+        lanes = pl.ds(j * DH, DH)
+        window = window_mask(pl.program_id(0) * PER_STEP + j, reach_ref, gap_ref)
+        k_now = k_ref[:, lanes]
+        v_now = v_ref[:, lanes]
+        q_rim = q_ref[:, lanes]
+        do_rim = do_ref[:, lanes]
         nt = (((1,), (1,)), ((), ()))
         scores = lax.dot_general(k_now, q_rim, nt, preferred_element_type=jnp.float32) * score_scale
         scores = jnp.where(window, scores, -jnp.inf)
-        weights = jnp.exp(scores - lse_ref[...])
+        weights = jnp.exp(scores - lse_ref[j])
         weights_b = weights.astype(jnp.bfloat16)
         grad_weights = lax.dot_general(v_now, do_rim, nt, preferred_element_type=jnp.float32)
-        grad_scores = (weights * (grad_weights - dot_ref[...])).astype(jnp.bfloat16)
+        grad_scores = (weights * (grad_weights - dot_ref[j])).astype(jnp.bfloat16)
         grad_k = jnp.dot(grad_scores, q_rim, preferred_element_type=jnp.float32) * score_scale
         grad_v = jnp.dot(weights_b, do_rim, preferred_element_type=jnp.float32)
-        gkv_ref[0] = grad_k.astype(jnp.bfloat16)
-        gkv_ref[1] = grad_v.astype(jnp.bfloat16)
+        gkv_ref[0, :, lanes] = grad_k.astype(jnp.bfloat16)
+        gkv_ref[1, :, lanes] = grad_v.astype(jnp.bfloat16)
 
     return kernel
 
@@ -140,20 +143,20 @@
     reach = jnp.stack([reach_time, reach_height, reach_width]).astype(jnp.int32)
 
     def own_spec(which):
-        return pl.BlockSpec((None, own_n, DH), lambda h, r: (which, 0, h))
+        return pl.BlockSpec((None, own_n, DH * PER_STEP), lambda h, r: (which, 0, h))
 
     def rim_spec(which):
-        return pl.BlockSpec((None, rim_n, DH), lambda h, r: (which, 0, h))
+        return pl.BlockSpec((None, rim_n, DH * PER_STEP), lambda h, r: (which, 0, h))
 
     live_spec = pl.BlockSpec((3, own_n, rim_n), lambda h, r: (0, 0, 0))
-    pair_spec = pl.BlockSpec((2, own_n, DH), lambda h, r: (0, 0, h))
-    stat_spec = pl.BlockSpec((None, own_n, 1), lambda h, r: (h, 0, 0))
+    pair_spec = pl.BlockSpec((2, own_n, DH * PER_STEP), lambda h, r: (0, 0, h))
+    stat_spec = pl.BlockSpec((PER_STEP, own_n, 1), lambda h, r: (h, 0, 0))
 
     og, lse, dots = pl.pallas_call(
         make_query_kernel(),
         grid_spec=pltpu.PrefetchScalarGridSpec(
             num_scalar_prefetch=1,
-            grid=(heads,),
+            grid=(heads // PER_STEP,),
             in_specs=[own_spec(2), own_spec(3), rim_spec(0), rim_spec(1), live_spec],
             out_specs=[pair_spec, stat_spec, stat_spec],
         ),
@@ -173,13 +176,13 @@
     statistics = jnp.stack([lse, dots]).reshape(2, heads, frames_dev, rows_dev, col_count)
     stat_rim = with_halo(statistics, (("tm", 2), ("ulysses", 3)), 1).reshape(2, heads, 1, rim_n)
     stat_rim_spec = [
-        pl.BlockSpec((None, None, 1, rim_n), lambda h, r, w=w: (w, h, 0, 0)) for w in range(2)
+        pl.BlockSpec((None, PER_STEP, 1, rim_n), lambda h, r, w=w: (w, h, 0, 0)) for w in range(2)
     ]
     gkv = pl.pallas_call(
         make_key_kernel(),
         grid_spec=pltpu.PrefetchScalarGridSpec(
             num_scalar_prefetch=1,
-            grid=(heads,),
+            grid=(heads // PER_STEP,),
             in_specs=[own_spec(0), own_spec(1), rim_spec(0), rim_spec(1)]
             + stat_rim_spec
             + [live_spec],

time: 288 us -> 282 us (0.979)
  Pallas kernels: 24.8 us -> 19.2 us
    pallas_call x1, Pallas kernels: 11.5 us -> 8.33 us  [body(): pl.pallas_call(make_key_kernel(), grid_spec=pltpu.PrefetchScalarGridSpec(...]
  transfers between devices with their start and end apart: 15 -> 15, of which waited for: 10 -> 10; matrix products, arithmetic and copies ran while one was open for 6% -> 6% of each run, Pallas kernels for 4% -> 3%
where the time goes in v6:
time: 282 us; the launch traced here: 281 us
  waiting for transfers between devices  155 us (55%)
  starting transfers between devices  74.1 us (26%)
  Pallas kernels  19.2 us (7%)
  local copies, waits for them, and re-layouts  18.7 us (7%)
  other arithmetic  13.2 us (5%)
    all_to_all x1, waiting for transfers between devices, body(): lax.all_to_all(stacked, 'ulysses', split_axis=2, concat_axis=3, tiled=True)  77.8 us
    all_to_all x2, waiting for transfers between devices, back_to_columns(): lax.all_to_all(shaped, 'ulysses', split_axis=3, concat_axis=2, tiled=True)  41.9 us
    ppermute x6, starting transfers between devices, with_halo(): before = lax.ppermute(last, axis, up)  22.3 us
    all_to_all x2, starting transfers between devices, back_to_columns(): lax.all_to_all(shaped, 'ulysses', split_axis=3, concat_axis=2, tiled=True)  20.7 us
    all_to_all x1, starting transfers between devices, body(): lax.all_to_all(stacked, 'ulysses', split_axis=2, concat_axis=3, tiled=True)  20.4 us
    ppermute x6, waiting for transfers between devices, with_halo(): after = lax.ppermute(initial, axis, down)  17.8 us
    ppermute x6, waiting for transfers between devices, with_halo(): before = lax.ppermute(last, axis, up)  17.5 us
    pallas_call x1, Pallas kernels, body(): pl.pallas_call(make_query_kernel(), grid_spec=pltpu.PrefetchScalarGridSpe...  10.9 us
  transfers between devices with their start and end apart: 15, of which 10 were waited for; matrix products, arithmetic and copies ran while one was open for 6% of the time, Pallas kernels for 3%

profile of v6, /device:TPU:1, one launch (start us, length us, event | category | flops | bytes accessed | tf_op | source)
XLA Modules:
  0.0 281.3 jit_solution(16874257330486845950)
XLA Ops:
  0.7 2.0 copy_bitcast_fusion
  2.7 0.8 copy_bitcast_fusion.2
  3.5 3.3 %pad_maximum_fusion.2 = bf16[4,2,64,1,1536]{4,1,3,0,2:T(2,128)(2,1)} fusion(bf16[1,2,64,1,1536]{4,1,3,0,2:T(2,128)(2,1)S(1)} %get-tuple-element.34, bf16[1,2,64,1,1536]{4,1,3,0,2:T(2,128)(2,1)S(1)} %get-tuple-element.35, bf16[1,2,64,1,1536]{4,1,3,0,2:T(2,128)(2,1)S(1)} %get-tuple-element.36, bf16[1,2,64,1,1536]{4,1,3,0,2:T(2,128)(2,1)S(1)} %get-tuple-element.37), kind=kLoop, calls=%fused_computation.2 | loop fusion | flops 2359296 | bytes 3145728 | tf_op jit(solution)/shard_map/stack | solution.py:122
  6.7 20.4 %all-to-all-start = ((bf16[4,2,64,1,1536]{4,1,3,0,2:T(2,128)(2,1)}), bf16[4,2,64,1,1536]{4,1,3,0,2:T(2,128)(2,1)S(1)}, u32[]{:S(2)}, u32[]{:S(2)}) async-start(bf16[4,2,64,1,1536]{4,1,3,0,2:T(2,128)(2,1)} %pad_maximum_fusion.2), calls=%async_computation | async-start | bytes 3145728 | tf_op jit(solution)/shard_map/all_to_all | solution.py:123
  27.2 77.8 %all-to-all-done = bf16[4,2,64,1,1536]{4,1,3,0,2:T(2,128)(2,1)S(1)} async-done(((bf16[4,2,64,1,1536]{4,1,3,0,2:T(2,128)(2,1)}), bf16[4,2,64,1,1536]{4,1,3,0,2:T(2,128)(2,1)S(1)}, u32[]{:S(2)}, u32[]{:S(2)}) %all-to-all-start) | async-done | bytes 1572896 | tf_op jit(solution)/shard_map/all_to_all | solution.py:123
  105.0 0.9 copy.53
  105.9 0.1 slice_bitcast_fusion
  106.0 1.1 copy-done
  107.0 0.1 fusion.21
  107.1 3.2 %collective-permute-start = (bf16[2,1,2,32,1536]{4,3,2,1,0:T(8,128)(2,1)S(1)}, bf16[2,1,2,32,1536]{4,3,2,1,0:T(8,128)(2,1)S(1)}, u32[]{:S(2)}, u32[]{:S(2)}) collective-permute-start(bf16[2,1,2,32,1536]{4,3,2,1,0:T(8,128)(2,1)S(1)} %get-tuple-element.28), channel_id=1, source_target_pairs={{0,32},{32,64},{64,96},{96,128},{128,160},{160,192},{192,224},{224... | collective-permute-start | bytes 1179656 | tf_op jit(solution)/shard_map/ppermute | solution.py:23
  110.4 1.3 collective-permute-start.1
  111.7 6.5 %collective-permute-done = bf16[2,1,2,32,1536]{4,3,2,1,0:T(8,128)(2,1)S(1)} collective-permute-done((bf16[2,1,2,32,1536]{4,3,2,1,0:T(8,128)(2,1)S(1)}, bf16[2,1,2,32,1536]{4,3,2,1,0:T(8,128)(2,1)S(1)}, u32[]{:S(2)}, u32[]{:S(2)}) %collective-permute-start) | collective-permute-done | bytes 393248 | tf_op jit(solution)/shard_map/ppermute | solution.py:23
  118.2 3.8 %collective-permute-done.1 = bf16[2,1,2,32,1536]{4,3,2,1,0:T(8,128)(2,1)S(1)} collective-permute-done((bf16[2,1,2,32,1536]{4,3,2,1,0:T(8,128)(2,1)S(1)}, bf16[2,1,2,32,1536]{4,3,2,1,0:T(8,128)(2,1)S(1)}, u32[]{:S(2)}, u32[]{:S(2)}) %collective-permute-start.1) | collective-permute-done | bytes 393248 | tf_op jit(solution)/shard_map/ppermute | solution.py:24
  122.0 0.2 pad_maximum_fusion.3
  122.2 0.1 fusion.17
  122.3 2.1 collective-permute-start.2
  124.4 3.0 %collective-permute-start.3 = (bf16[2,4,1,32,1536]{4,3,2,1,0:T(8,128)(2,1)S(1)}, bf16[2,4,1,32,1536]{4,3,2,1,0:T(8,128)(2,1)S(1)}, u32[]{:S(2)}, u32[]{:S(2)}) collective-permute-start(bf16[2,4,1,32,1536]{4,3,2,1,0:T(8,128)(2,1)S(1)} %get-tuple-element.19), channel_id=1, source_target_pairs={{1,0},{2,1},{3,2},{4,3},{5,4},{6,5},{7,6},{8,7},{9,8},{10,9},{11,1... | collective-permute-start | bytes 2359304 | tf_op jit(solution)/shard_map/ppermute | solution.py:24
  127.4 0.6 pad_add_fusion.1.reach_ref
  128.0 0.1 abs_select_fusion
  128.1 0.1 subtract_abs_fusion
  128.3 1.0 pad_add_fusion.gap_ref
  129.2 4.1 %collective-permute-done.2 = bf16[2,4,1,32,1536]{4,3,2,1,0:T(8,128)(2,1)S(1)} collective-permute-done((bf16[2,4,1,32,1536]{4,3,2,1,0:T(8,128)(2,1)S(1)}, bf16[2,4,1,32,1536]{4,3,2,1,0:T(8,128)(2,1)S(1)}, u32[]{:S(2)}, u32[]{:S(2)}) %collective-permute-start.2) | collective-permute-done | bytes 786464 | tf_op jit(solution)/shard_map/ppermute | solution.py:23
  133.3 4.4 %collective-permute-done.3 = bf16[2,4,1,32,1536]{4,3,2,1,0:T(8,128)(2,1)S(1)} collective-permute-done((bf16[2,4,1,32,1536]{4,3,2,1,0:T(8,128)(2,1)S(1)}, bf16[2,4,1,32,1536]{4,3,2,1,0:T(8,128)(2,1)S(1)}, u32[]{:S(2)}, u32[]{:S(2)}) %collective-permute-start.3) | collective-permute-done | bytes 786464 | tf_op jit(solution)/shard_map/ppermute | solution.py:24
  137.7 1.9 pad_maximum_fusion
  139.6 10.9 %shard_map.102 = (bf16[2,128,1536]{2,1,0:T(8,128)(2,1)}, f32[12,128,1]{2,1,0:T(8,128)}, f32[12,128,1]{2,1,0:T(8,128)}) custom-call(s32[3,12]{1,0:T(4,128)} %pad_add_fusion.1.reach_ref, bf16[4,128,1536]{2,1,0:T(8,128)(2,1)} %bitcast.38, bf16[4,128,1536]{2,1,0:T(8,128)(2,1)} %bitcast.39, bf16[2,512,1536]{2,1,0:T(8,128)(2,1)} %bitcast.44, ...), custom_call_target="tpu_custom_call" | custom-call | tf_op jit(solution)/shard_map/pallas_call | solution.py:155
  150.5 2.8 %copy.35 = bf16[2,2,2,32,1536]{4,2,1,0,3:T(2,128)(2,1)} copy(bf16[2,2,2,32,1536]{4,3,2,1,0:T(8,128)(2,1)} %bitcast.54) | data formatting | bytes 1572864 | tf_op jit(solution)/shard_map/reshape | solution.py:171
  153.3 7.3 %all-to-all-start.1 = ((bf16[2,2,2,32,1536]{4,2,1,0,3:T(2,128)(2,1)}), bf16[2,2,2,32,1536]{4,2,1,0,3:T(2,128)(2,1)S(1)}, u32[]{:S(2)}, u32[]{:S(2)}) async-start(bf16[2,2,2,32,1536]{4,2,1,0,3:T(2,128)(2,1)} %copy.35), calls=%async_computation.1 | async-start | bytes 1572864 | tf_op jit(solution)/shard_map/all_to_all | solution.py:172
  160.7 3.2 %collective-permute-start.4 = (bf16[2,1,2,32,1536]{4,3,2,1,0:T(8,128)(2,1)S(1)}, bf16[2,1,2,32,1536]{4,3,2,1,0:T(8,128)(2,1)S(1)}, u32[]{:S(2)}, u32[]{:S(2)}) collective-permute-start(bf16[2,1,2,32,1536]{4,3,2,1,0:T(8,128)(2,1)S(1)} %get-tuple-element.24), channel_id=1, source_target_pairs={{0,32},{32,64},{64,96},{96,128},{128,160},{160,192},{192,224},{224... | collective-permute-start | bytes 1179656 | tf_op jit(solution)/shard_map/ppermute | solution.py:23
  163.9 1.3 collective-permute-start.5
  165.2 6.9 %collective-permute-done.4 = bf16[2,1,2,32,1536]{4,3,2,1,0:T(8,128)(2,1)S(1)} collective-permute-done((bf16[2,1,2,32,1536]{4,3,2,1,0:T(8,128)(2,1)S(1)}, bf16[2,1,2,32,1536]{4,3,2,1,0:T(8,128)(2,1)S(1)}, u32[]{:S(2)}, u32[]{:S(2)}) %collective-permute-start.4) | collective-permute-done | bytes 393248 | tf_op jit(solution)/shard_map/ppermute | solution.py:23
  172.1 5.0 %collective-permute-done.5 = bf16[2,1,2,32,1536]{4,3,2,1,0:T(8,128)(2,1)S(1)} collective-permute-done((bf16[2,1,2,32,1536]{4,3,2,1,0:T(8,128)(2,1)S(1)}, bf16[2,1,2,32,1536]{4,3,2,1,0:T(8,128)(2,1)S(1)}, u32[]{:S(2)}, u32[]{:S(2)}) %collective-permute-start.5) | collective-permute-done | bytes 393248 | tf_op jit(solution)/shard_map/ppermute | solution.py:24
  177.1 0.2 pad_maximum_fusion.4
  177.3 1.3 fusion.16
  178.6 4.2 %collective-permute-start.6 = (bf16[2,4,1,32,1536]{4,3,2,1,0:T(8,128)(2,1)}, bf16[2,4,1,32,1536]{4,3,2,1,0:T(8,128)(2,1)S(1)}, u32[]{:S(2)}, u32[]{:S(2)}) collective-permute-start(bf16[2,4,1,32,1536]{4,3,2,1,0:T(8,128)(2,1)} %get-tuple-element.14), channel_id=1, source_target_pairs={{0,1},{1,2},{2,3},{3,4},{4,5},{5,6},{6,7},{7,8},{8,9},{9,10},{10,1... | collective-permute-start | bytes 2359304 | tf_op jit(solution)/shard_map/ppermute | solution.py:23
  182.8 1.9 collective-permute-start.7
  184.8 1.4 reduce
  186.2 0.1 stack.52
  186.3 1.4 reduce.1
  187.7 0.1 stack.53
  187.8 4.6 %collective-permute-start.8 = (f32[2,12,1,2,32]{4,3,2,0,1:T(2,128)S(1)}, f32[2,12,1,2,32]{4,3,2,0,1:T(2,128)S(1)}, u32[]{:S(2)}, u32[]{:S(2)}) collective-permute-start(f32[2,12,1,2,32]{4,3,2,0,1:T(2,128)S(1)} %get-tuple-element.32), channel_id=1, source_target_pairs={{0,32},{32,64},{64,96},{96,128},{128,160},{160,192},{192,224},{224... | collective-permute-start | bytes 18440 | tf_op jit(solution)/shard_map/ppermute | solution.py:23
  192.4 1.3 collective-permute-start.9
  193.7 3.3 %collective-permute-done.9 = f32[2,12,1,2,32]{4,3,2,0,1:T(2,128)S(1)} collective-permute-done((f32[2,12,1,2,32]{4,3,2,0,1:T(2,128)S(1)}, f32[2,12,1,2,32]{4,3,2,0,1:T(2,128)S(1)}, u32[]{:S(2)}, u32[]{:S(2)}) %collective-permute-start.9) | collective-permute-done | bytes 6176 | tf_op jit(solution)/shard_map/ppermute | solution.py:24
  197.1 0.1 fusion.22
  197.1 5.1 %collective-permute-start.10 = (f32[2,12,4,1,32]{4,3,2,0,1:T(1,128)S(1)}, f32[2,12,4,1,32]{4,3,2,0,1:T(1,128)S(1)}, u32[]{:S(2)}, u32[]{:S(2)}) collective-permute-start(f32[2,12,4,1,32]{4,3,2,0,1:T(1,128)S(1)} %get-tuple-element.30), channel_id=1, source_target_pairs={{0,1},{1,2},{2,3},{3,4},{4,5},{5,6},{6,7},{7,8},{8,9},{9,10},{10,1... | collective-permute-start | bytes 36872 | tf_op jit(solution)/shard_map/ppermute | solution.py:23
  202.2 1.9 collective-permute-start.11
  204.2 1.3 collective-permute-done.7
  205.5 2.9 %pad_maximum_fusion.1 = bf16[2,4,4,32,1536]{4,3,2,1,0:T(8,128)(2,1)} fusion(bf16[2,4,1,32,1536]{4,3,2,1,0:T(8,128)(2,1)} %collective-permute-done.7, bf16[2,1,2,32,1536]{4,3,2,1,0:T(8,128)(2,1)S(1)} %collective-permute-done.5, bf16[2,2,2,32,1536]{4,3,2,1,0:T(8,128)(2,1)S(1)} %get-tuple-element.16, bf16[2,1,2,32,1536]{4,3,2,1,0:T(8,128)(2,1)S(1)} %collective-permute-done.4, ...), kind=kLoop, calls=%fused_computation.1 | loop fusion | flops 6291456 | bytes 6291456 | tf_op jit(solution)/shard_map/concatenate | solution.py:25
  208.4 0.2 pad_maximum_fusion.5
  208.5 0.2 reshape.496
  208.7 0.7 copy.46.lse_ref.dot_ref
  209.4 8.3 %shard_map.103 = bf16[2,128,1536]{2,1,0:T(8,128)(2,1)} custom-call(s32[3,12]{1,0:T(4,128)} %pad_add_fusion.1.reach_ref, bf16[4,128,1536]{2,1,0:T(8,128)(2,1)} %bitcast.40, bf16[4,128,1536]{2,1,0:T(8,128)(2,1)} %bitcast.41, bf16[2,512,1536]{2,1,0:T(8,128)(2,1)} %bitcast.42, bf16[2,512,1536]{2,1,0:T(8,128)(2,1)} %bitcast.43, ...), custom_call_target="tpu_custom_call" | custom-call | tf_op jit(solution)/shard_map/pallas_call | solution.py:181
  217.7 2.8 %copy.39 = bf16[2,2,2,32,1536]{4,2,1,0,3:T(2,128)(2,1)} copy(bf16[2,2,2,32,1536]{4,3,2,1,0:T(8,128)(2,1)} %bitcast.47) | data formatting | bytes 1572864 | tf_op jit(solution)/shard_map/reshape | solution.py:171
  220.5 13.4 %all-to-all-start.2 = ((bf16[2,2,2,32,1536]{4,2,1,0,3:T(2,128)(2,1)}), bf16[2,2,2,32,1536]{4,2,1,0,3:T(2,128)(2,1)S(1)}, u32[]{:S(2)}, u32[]{:S(2)}) async-start(bf16[2,2,2,32,1536]{4,2,1,0,3:T(2,128)(2,1)} %copy.39), calls=%async_computation.2 | async-start | bytes 1572864 | tf_op jit(solution)/shard_map/all_to_all | solution.py:172
  233.9 0.5 fusion.20
  234.5 0.3 copy.36
  234.8 0.8 copy.42
  235.6 0.3 copy.37
  235.9 0.8 copy.43
  236.7 41.9 %all-to-all-done.2 = bf16[2,2,2,32,1536]{4,2,1,0,3:T(2,128)(2,1)S(1)} async-done(((bf16[2,2,2,32,1536]{4,2,1,0,3:T(2,128)(2,1)}), bf16[2,2,2,32,1536]{4,2,1,0,3:T(2,128)(2,1)S(1)}, u32[]{:S(2)}, u32[]{:S(2)}) %all-to-all-start.2) | async-done | bytes 786464 | tf_op jit(solution)/shard_map/all_to_all | solution.py:172
  278.6 0.5 fusion.18
  279.1 0.3 copy.40
  279.5 0.8 copy.44
  280.2 0.3 copy.41
  280.6 0.8 copy.45
  (28 shorter events, 0.2 us)
Async XLA Ops:
  0.6 2.0 copy-start.2
  0.6 2.0 copy-start.1
  6.7 98.3 %all-to-all-start = ((bf16[4,2,64,1,1536]{4,1,3,0,2:T(2,128)(2,1)}), bf16[4,2,64,1,1536]{4,1,3,0,2:T(2,128)(2,1)S(1)}, u32[]{:S(2)}, u32[]{:S(2)}) async-start(bf16[4,2,64,1,1536]{4,1,3,0,2:T(2,128)(2,1)} %pad_maximum_fusion.2), calls=%async_computation | async-start | bytes 3145728 | tf_op jit(solution)/shard_map/all_to_all | solution.py:123
  105.9 1.2 copy-start
  107.1 11.1 %collective-permute-start = (bf16[2,1,2,32,1536]{4,3,2,1,0:T(8,128)(2,1)S(1)}, bf16[2,1,2,32,1536]{4,3,2,1,0:T(8,128)(2,1)S(1)}, u32[]{:S(2)}, u32[]{:S(2)}) collective-permute-start(bf16[2,1,2,32,1536]{4,3,2,1,0:T(8,128)(2,1)S(1)} %get-tuple-element.28), channel_id=1, source_target_pairs={{0,32},{32,64},{64,96},{96,128},{128,160},{160,192},{192,224},{224... | collective-permute-start | bytes 1179656 | tf_op jit(solution)/shard_map/ppermute | solution.py:23
  110.4 11.6 %collective-permute-start.1 = (bf16[2,1,2,32,1536]{4,3,2,1,0:T(8,128)(2,1)S(1)}, bf16[2,1,2,32,1536]{4,3,2,1,0:T(8,128)(2,1)S(1)}, u32[]{:S(2)}, u32[]{:S(2)}) collective-permute-start(bf16[2,1,2,32,1536]{4,3,2,1,0:T(8,128)(2,1)S(1)} %get-tuple-element.29), channel_id=1, source_target_pairs={{32,0},{64,32},{96,64},{128,96},{160,128},{192,160},{224,192},{256... | collective-permute-start | bytes 1179656 | tf_op jit(solution)/shard_map/ppermute | solution.py:24
  122.2 5.2 %copy-start.3 = (s32[12]{0:T(128)S(1)}, s32[12]{0:T(128)}, u32[]{:S(2)}) copy-start(s32[12]{0:T(128)} %param.13) | copy-start | bytes 148
  122.2 5.2 %copy-start.4 = (s32[12]{0:T(128)S(1)}, s32[12]{0:T(128)}, u32[]{:S(2)}) copy-start(s32[12]{0:T(128)} %param.12) | copy-start | bytes 148
  122.2 5.2 %copy-start.5 = (s32[12]{0:T(128)S(1)}, s32[12]{0:T(128)}, u32[]{:S(2)}) copy-start(s32[12]{0:T(128)} %param.11) | copy-start | bytes 148
  122.3 11.0 %collective-permute-start.2 = (bf16[2,4,1,32,1536]{4,3,2,1,0:T(8,128)(2,1)S(1)}, bf16[2,4,1,32,1536]{4,3,2,1,0:T(8,128)(2,1)S(1)}, u32[]{:S(2)}, u32[]{:S(2)}) collective-permute-start(bf16[2,4,1,32,1536]{4,3,2,1,0:T(8,128)(2,1)S(1)} %get-tuple-element.18), channel_id=1, source_target_pairs={{0,1},{1,2},{2,3},{3,4},{4,5},{5,6},{6,7},{7,8},{8,9},{9,10},{10,1... | collective-permute-start | bytes 2359304 | tf_op jit(solution)/shard_map/ppermute | solution.py:23
  124.4 13.3 %collective-permute-start.3 = (bf16[2,4,1,32,1536]{4,3,2,1,0:T(8,128)(2,1)S(1)}, bf16[2,4,1,32,1536]{4,3,2,1,0:T(8,128)(2,1)S(1)}, u32[]{:S(2)}, u32[]{:S(2)}) collective-permute-start(bf16[2,4,1,32,1536]{4,3,2,1,0:T(8,128)(2,1)S(1)} %get-tuple-element.19), channel_id=1, source_target_pairs={{1,0},{2,1},{3,2},{4,3},{5,4},{6,5},{7,6},{8,7},{9,8},{10,9},{11,1... | collective-permute-start | bytes 2359304 | tf_op jit(solution)/shard_map/ppermute | solution.py:24
  153.3 67.2 %all-to-all-start.1 = ((bf16[2,2,2,32,1536]{4,2,1,0,3:T(2,128)(2,1)}), bf16[2,2,2,32,1536]{4,2,1,0,3:T(2,128)(2,1)S(1)}, u32[]{:S(2)}, u32[]{:S(2)}) async-start(bf16[2,2,2,32,1536]{4,2,1,0,3:T(2,128)(2,1)} %copy.35), calls=%async_computation.1 | async-start | bytes 1572864 | tf_op jit(solution)/shard_map/all_to_all | solution.py:172
  160.7 11.4 %collective-permute-start.4 = (bf16[2,1,2,32,1536]{4,3,2,1,0:T(8,128)(2,1)S(1)}, bf16[2,1,2,32,1536]{4,3,2,1,0:T(8,128)(2,1)S(1)}, u32[]{:S(2)}, u32[]{:S(2)}) collective-permute-start(bf16[2,1,2,32,1536]{4,3,2,1,0:T(8,128)(2,1)S(1)} %get-tuple-element.24), channel_id=1, source_target_pairs={{0,32},{32,64},{64,96},{96,128},{128,160},{160,192},{192,224},{224... | collective-permute-start | bytes 1179656 | tf_op jit(solution)/shard_map/ppermute | solution.py:23
  163.9 13.3 %collective-permute-start.5 = (bf16[2,1,2,32,1536]{4,3,2,1,0:T(8,128)(2,1)S(1)}, bf16[2,1,2,32,1536]{4,3,2,1,0:T(8,128)(2,1)S(1)}, u32[]{:S(2)}, u32[]{:S(2)}) collective-permute-start(bf16[2,1,2,32,1536]{4,3,2,1,0:T(8,128)(2,1)S(1)} %get-tuple-element.25), channel_id=1, source_target_pairs={{32,0},{64,32},{96,64},{128,96},{160,128},{192,160},{224,192},{256... | collective-permute-start | bytes 1179656 | tf_op jit(solution)/shard_map/ppermute | solution.py:24
  178.6 25.5 %collective-permute-start.6 = (bf16[2,4,1,32,1536]{4,3,2,1,0:T(8,128)(2,1)}, bf16[2,4,1,32,1536]{4,3,2,1,0:T(8,128)(2,1)S(1)}, u32[]{:S(2)}, u32[]{:S(2)}) collective-permute-start(bf16[2,4,1,32,1536]{4,3,2,1,0:T(8,128)(2,1)} %get-tuple-element.14), channel_id=1, source_target_pairs={{0,1},{1,2},{2,3},{3,4},{4,5},{5,6},{6,7},{7,8},{8,9},{9,10},{10,1... | collective-permute-start | bytes 2359304 | tf_op jit(solution)/shard_map/ppermute | solution.py:23
  182.8 22.6 %collective-permute-start.7 = (bf16[2,4,1,32,1536]{4,3,2,1,0:T(8,128)(2,1)}, bf16[2,4,1,32,1536]{4,3,2,1,0:T(8,128)(2,1)}, u32[]{:S(2)}, u32[]{:S(2)}) collective-permute-start(bf16[2,4,1,32,1536]{4,3,2,1,0:T(8,128)(2,1)} %get-tuple-element.15), channel_id=1, source_target_pairs={{1,0},{2,1},{3,2},{4,3},{5,4},{6,5},{7,6},{8,7},{9,8},{10,9},{11,1... | collective-permute-start | bytes 2359304 | tf_op jit(solution)/shard_map/ppermute | solution.py:24
  187.8 5.9 %collective-permute-start.8 = (f32[2,12,1,2,32]{4,3,2,0,1:T(2,128)S(1)}, f32[2,12,1,2,32]{4,3,2,0,1:T(2,128)S(1)}, u32[]{:S(2)}, u32[]{:S(2)}) collective-permute-start(f32[2,12,1,2,32]{4,3,2,0,1:T(2,128)S(1)} %get-tuple-element.32), channel_id=1, source_target_pairs={{0,32},{32,64},{64,96},{96,128},{128,160},{160,192},{192,224},{224... | collective-permute-start | bytes 18440 | tf_op jit(solution)/shard_map/ppermute | solution.py:23
  192.4 4.6 %collective-permute-start.9 = (f32[2,12,1,2,32]{4,3,2,0,1:T(2,128)S(1)}, f32[2,12,1,2,32]{4,3,2,0,1:T(2,128)S(1)}, u32[]{:S(2)}, u32[]{:S(2)}) collective-permute-start(f32[2,12,1,2,32]{4,3,2,0,1:T(2,128)S(1)} %get-tuple-element.33), channel_id=1, source_target_pairs={{32,0},{64,32},{96,64},{128,96},{160,128},{192,160},{224,192},{256... | collective-permute-start | bytes 18440 | tf_op jit(solution)/shard_map/ppermute | solution.py:24
  197.1 11.2 %collective-permute-start.10 = (f32[2,12,4,1,32]{4,3,2,0,1:T(1,128)S(1)}, f32[2,12,4,1,32]{4,3,2,0,1:T(1,128)S(1)}, u32[]{:S(2)}, u32[]{:S(2)}) collective-permute-start(f32[2,12,4,1,32]{4,3,2,0,1:T(1,128)S(1)} %get-tuple-element.30), channel_id=1, source_target_pairs={{0,1},{1,2},{2,3},{3,4},{4,5},{5,6},{6,7},{7,8},{8,9},{9,10},{10,1... | collective-permute-start | bytes 36872 | tf_op jit(solution)/shard_map/ppermute | solution.py:23
  202.2 6.1 %collective-permute-start.11 = (f32[2,12,4,1,32]{4,3,2,0,1:T(1,128)S(1)}, f32[2,12,4,1,32]{4,3,2,0,1:T(1,128)S(1)}, u32[]{:S(2)}, u32[]{:S(2)}) collective-permute-start(f32[2,12,4,1,32]{4,3,2,0,1:T(1,128)S(1)} %get-tuple-element.31), channel_id=1, source_target_pairs={{1,0},{2,1},{3,2},{4,3},{5,4},{6,5},{7,6},{8,7},{9,8},{10,9},{11,1... | collective-permute-start | bytes 36872 | tf_op jit(solution)/shard_map/ppermute | solution.py:24
  220.5 58.1 %all-to-all-start.2 = ((bf16[2,2,2,32,1536]{4,2,1,0,3:T(2,128)(2,1)}), bf16[2,2,2,32,1536]{4,2,1,0,3:T(2,128)(2,1)S(1)}, u32[]{:S(2)}, u32[]{:S(2)}) async-start(bf16[2,2,2,32,1536]{4,2,1,0,3:T(2,128)(2,1)} %copy.39), calls=%async_computation.2 | async-start | bytes 1572864 | tf_op jit(solution)/shard_map/all_to_all | solution.py:172

commit v7 on v6

--- a/solution.py
+++ b/solution.py
@@ -10,7 +10,7 @@
 DH = 128
 HEADS = 12
 TW = 8
-PER_STEP = 2
+PER_STEP = 4
 
 
 def with_halo(array, sides, width):

time: 282 us -> 282 us (level)
  no operation moved by 1% of the time
where the time goes in v7:
time: 282 us; the launch traced here: 281 us
  waiting for transfers between devices  155 us (55%)
  starting transfers between devices  74.5 us (26%)
  local copies, waits for them, and re-layouts  18.7 us (7%)
  Pallas kernels  18.3 us (6%)
  other arithmetic  13.2 us (5%)
    all_to_all x1, waiting for transfers between devices, body(): lax.all_to_all(stacked, 'ulysses', split_axis=2, concat_axis=3, tiled=True)  77.8 us
    all_to_all x2, waiting for transfers between devices, back_to_columns(): lax.all_to_all(shaped, 'ulysses', split_axis=3, concat_axis=2, tiled=True)  41.9 us
    ppermute x6, starting transfers between devices, with_halo(): before = lax.ppermute(last, axis, up)  22.3 us
    all_to_all x2, starting transfers between devices, back_to_columns(): lax.all_to_all(shaped, 'ulysses', split_axis=3, concat_axis=2, tiled=True)  20.9 us
    all_to_all x1, starting transfers between devices, body(): lax.all_to_all(stacked, 'ulysses', split_axis=2, concat_axis=3, tiled=True)  20.4 us
    ppermute x6, waiting for transfers between devices, with_halo(): after = lax.ppermute(initial, axis, down)  17.6 us
    ppermute x6, waiting for transfers between devices, with_halo(): before = lax.ppermute(last, axis, up)  17.5 us
    pallas_call x1, Pallas kernels, body(): pl.pallas_call(make_query_kernel(), grid_spec=pltpu.PrefetchScalarGridSpe...  10.9 us
  transfers between devices with their start and end apart: 15, of which 10 were waited for; matrix products, arithmetic and copies ran while one was open for 6% of the time, Pallas kernels for 3%

profile of v7, /device:TPU:1, one launch (start us, length us, event | category | flops | bytes accessed | tf_op | source)
XLA Modules:
  0.0 280.6 jit_solution(11467425359439111176)
XLA Ops:
  0.7 2.0 copy_bitcast_fusion
  2.7 0.8 copy_bitcast_fusion.2
  3.5 3.3 %pad_maximum_fusion.2 = bf16[4,2,64,1,1536]{4,1,3,0,2:T(2,128)(2,1)} fusion(bf16[1,2,64,1,1536]{4,1,3,0,2:T(2,128)(2,1)S(1)} %get-tuple-element.34, bf16[1,2,64,1,1536]{4,1,3,0,2:T(2,128)(2,1)S(1)} %get-tuple-element.35, bf16[1,2,64,1,1536]{4,1,3,0,2:T(2,128)(2,1)S(1)} %get-tuple-element.36, bf16[1,2,64,1,1536]{4,1,3,0,2:T(2,128)(2,1)S(1)} %get-tuple-element.37), kind=kLoop, calls=%fused_computation.2 | loop fusion | flops 2359296 | bytes 3145728 | tf_op jit(solution)/shard_map/stack | solution.py:122
  6.7 20.4 %all-to-all-start = ((bf16[4,2,64,1,1536]{4,1,3,0,2:T(2,128)(2,1)}), bf16[4,2,64,1,1536]{4,1,3,0,2:T(2,128)(2,1)S(1)}, u32[]{:S(2)}, u32[]{:S(2)}) async-start(bf16[4,2,64,1,1536]{4,1,3,0,2:T(2,128)(2,1)} %pad_maximum_fusion.2), calls=%async_computation | async-start | bytes 3145728 | tf_op jit(solution)/shard_map/all_to_all | solution.py:123
  27.2 77.8 %all-to-all-done = bf16[4,2,64,1,1536]{4,1,3,0,2:T(2,128)(2,1)S(1)} async-done(((bf16[4,2,64,1,1536]{4,1,3,0,2:T(2,128)(2,1)}), bf16[4,2,64,1,1536]{4,1,3,0,2:T(2,128)(2,1)S(1)}, u32[]{:S(2)}, u32[]{:S(2)}) %all-to-all-start) | async-done | bytes 1572896 | tf_op jit(solution)/shard_map/all_to_all | solution.py:123
  105.0 0.9 copy.53
  105.9 0.1 slice_bitcast_fusion
  106.0 1.1 copy-done
  107.0 0.1 fusion.21
  107.1 3.2 %collective-permute-start = (bf16[2,1,2,32,1536]{4,3,2,1,0:T(8,128)(2,1)S(1)}, bf16[2,1,2,32,1536]{4,3,2,1,0:T(8,128)(2,1)S(1)}, u32[]{:S(2)}, u32[]{:S(2)}) collective-permute-start(bf16[2,1,2,32,1536]{4,3,2,1,0:T(8,128)(2,1)S(1)} %get-tuple-element.28), channel_id=1, source_target_pairs={{0,32},{32,64},{64,96},{96,128},{128,160},{160,192},{192,224},{224... | collective-permute-start | bytes 1179656 | tf_op jit(solution)/shard_map/ppermute | solution.py:23
  110.4 1.3 collective-permute-start.1
  111.7 6.5 %collective-permute-done = bf16[2,1,2,32,1536]{4,3,2,1,0:T(8,128)(2,1)S(1)} collective-permute-done((bf16[2,1,2,32,1536]{4,3,2,1,0:T(8,128)(2,1)S(1)}, bf16[2,1,2,32,1536]{4,3,2,1,0:T(8,128)(2,1)S(1)}, u32[]{:S(2)}, u32[]{:S(2)}) %collective-permute-start) | collective-permute-done | bytes 393248 | tf_op jit(solution)/shard_map/ppermute | solution.py:23
  118.2 3.8 %collective-permute-done.1 = bf16[2,1,2,32,1536]{4,3,2,1,0:T(8,128)(2,1)S(1)} collective-permute-done((bf16[2,1,2,32,1536]{4,3,2,1,0:T(8,128)(2,1)S(1)}, bf16[2,1,2,32,1536]{4,3,2,1,0:T(8,128)(2,1)S(1)}, u32[]{:S(2)}, u32[]{:S(2)}) %collective-permute-start.1) | collective-permute-done | bytes 393248 | tf_op jit(solution)/shard_map/ppermute | solution.py:24
  122.0 0.2 pad_maximum_fusion.3
  122.2 0.1 fusion.17
  122.3 2.1 collective-permute-start.2
  124.4 3.0 %collective-permute-start.3 = (bf16[2,4,1,32,1536]{4,3,2,1,0:T(8,128)(2,1)S(1)}, bf16[2,4,1,32,1536]{4,3,2,1,0:T(8,128)(2,1)S(1)}, u32[]{:S(2)}, u32[]{:S(2)}) collective-permute-start(bf16[2,4,1,32,1536]{4,3,2,1,0:T(8,128)(2,1)S(1)} %get-tuple-element.19), channel_id=1, source_target_pairs={{1,0},{2,1},{3,2},{4,3},{5,4},{6,5},{7,6},{8,7},{9,8},{10,9},{11,1... | collective-permute-start | bytes 2359304 | tf_op jit(solution)/shard_map/ppermute | solution.py:24
  127.4 0.6 pad_add_fusion.1.reach_ref
  128.0 0.1 abs_select_fusion
  128.1 0.1 subtract_abs_fusion
  128.3 1.0 pad_add_fusion.gap_ref
  129.2 4.1 %collective-permute-done.2 = bf16[2,4,1,32,1536]{4,3,2,1,0:T(8,128)(2,1)S(1)} collective-permute-done((bf16[2,4,1,32,1536]{4,3,2,1,0:T(8,128)(2,1)S(1)}, bf16[2,4,1,32,1536]{4,3,2,1,0:T(8,128)(2,1)S(1)}, u32[]{:S(2)}, u32[]{:S(2)}) %collective-permute-start.2) | collective-permute-done | bytes 786464 | tf_op jit(solution)/shard_map/ppermute | solution.py:23
  133.3 4.4 %collective-permute-done.3 = bf16[2,4,1,32,1536]{4,3,2,1,0:T(8,128)(2,1)S(1)} collective-permute-done((bf16[2,4,1,32,1536]{4,3,2,1,0:T(8,128)(2,1)S(1)}, bf16[2,4,1,32,1536]{4,3,2,1,0:T(8,128)(2,1)S(1)}, u32[]{:S(2)}, u32[]{:S(2)}) %collective-permute-start.3) | collective-permute-done | bytes 786464 | tf_op jit(solution)/shard_map/ppermute | solution.py:24
  137.7 1.9 pad_maximum_fusion
  139.6 10.9 %shard_map.102 = (bf16[2,128,1536]{2,1,0:T(8,128)(2,1)}, f32[12,128,1]{2,1,0:T(8,128)}, f32[12,128,1]{2,1,0:T(8,128)}) custom-call(s32[3,12]{1,0:T(4,128)} %pad_add_fusion.1.reach_ref, bf16[4,128,1536]{2,1,0:T(8,128)(2,1)} %bitcast.38, bf16[4,128,1536]{2,1,0:T(8,128)(2,1)} %bitcast.39, bf16[2,512,1536]{2,1,0:T(8,128)(2,1)} %bitcast.44, ...), custom_call_target="tpu_custom_call" | custom-call | tf_op jit(solution)/shard_map/pallas_call | solution.py:155
  150.5 2.8 %copy.35 = bf16[2,2,2,32,1536]{4,2,1,0,3:T(2,128)(2,1)} copy(bf16[2,2,2,32,1536]{4,3,2,1,0:T(8,128)(2,1)} %bitcast.54) | data formatting | bytes 1572864 | tf_op jit(solution)/shard_map/reshape | solution.py:171
  153.3 7.3 %all-to-all-start.1 = ((bf16[2,2,2,32,1536]{4,2,1,0,3:T(2,128)(2,1)}), bf16[2,2,2,32,1536]{4,2,1,0,3:T(2,128)(2,1)S(1)}, u32[]{:S(2)}, u32[]{:S(2)}) async-start(bf16[2,2,2,32,1536]{4,2,1,0,3:T(2,128)(2,1)} %copy.35), calls=%async_computation.1 | async-start | bytes 1572864 | tf_op jit(solution)/shard_map/all_to_all | solution.py:172
  160.7 3.2 %collective-permute-start.4 = (bf16[2,1,2,32,1536]{4,3,2,1,0:T(8,128)(2,1)S(1)}, bf16[2,1,2,32,1536]{4,3,2,1,0:T(8,128)(2,1)S(1)}, u32[]{:S(2)}, u32[]{:S(2)}) collective-permute-start(bf16[2,1,2,32,1536]{4,3,2,1,0:T(8,128)(2,1)S(1)} %get-tuple-element.24), channel_id=1, source_target_pairs={{0,32},{32,64},{64,96},{96,128},{128,160},{160,192},{192,224},{224... | collective-permute-start | bytes 1179656 | tf_op jit(solution)/shard_map/ppermute | solution.py:23
  163.9 1.3 collective-permute-start.5
  165.2 6.9 %collective-permute-done.4 = bf16[2,1,2,32,1536]{4,3,2,1,0:T(8,128)(2,1)S(1)} collective-permute-done((bf16[2,1,2,32,1536]{4,3,2,1,0:T(8,128)(2,1)S(1)}, bf16[2,1,2,32,1536]{4,3,2,1,0:T(8,128)(2,1)S(1)}, u32[]{:S(2)}, u32[]{:S(2)}) %collective-permute-start.4) | collective-permute-done | bytes 393248 | tf_op jit(solution)/shard_map/ppermute | solution.py:23
  172.1 5.0 %collective-permute-done.5 = bf16[2,1,2,32,1536]{4,3,2,1,0:T(8,128)(2,1)S(1)} collective-permute-done((bf16[2,1,2,32,1536]{4,3,2,1,0:T(8,128)(2,1)S(1)}, bf16[2,1,2,32,1536]{4,3,2,1,0:T(8,128)(2,1)S(1)}, u32[]{:S(2)}, u32[]{:S(2)}) %collective-permute-start.5) | collective-permute-done | bytes 393248 | tf_op jit(solution)/shard_map/ppermute | solution.py:24
  177.1 0.2 pad_maximum_fusion.4
  177.3 1.3 fusion.16
  178.6 4.2 %collective-permute-start.6 = (bf16[2,4,1,32,1536]{4,3,2,1,0:T(8,128)(2,1)}, bf16[2,4,1,32,1536]{4,3,2,1,0:T(8,128)(2,1)S(1)}, u32[]{:S(2)}, u32[]{:S(2)}) collective-permute-start(bf16[2,4,1,32,1536]{4,3,2,1,0:T(8,128)(2,1)} %get-tuple-element.14), channel_id=1, source_target_pairs={{0,1},{1,2},{2,3},{3,4},{4,5},{5,6},{6,7},{7,8},{8,9},{9,10},{10,1... | collective-permute-start | bytes 2359304 | tf_op jit(solution)/shard_map/ppermute | solution.py:23
  182.9 1.9 collective-permute-start.7
  184.8 1.4 reduce
  186.2 0.1 stack.52
  186.3 1.4 reduce.1
  187.7 0.1 stack.53
  187.9 4.6 %collective-permute-start.8 = (f32[2,12,1,2,32]{4,3,2,0,1:T(2,128)S(1)}, f32[2,12,1,2,32]{4,3,2,0,1:T(2,128)S(1)}, u32[]{:S(2)}, u32[]{:S(2)}) collective-permute-start(f32[2,12,1,2,32]{4,3,2,0,1:T(2,128)S(1)} %get-tuple-element.32), channel_id=1, source_target_pairs={{0,32},{32,64},{64,96},{96,128},{128,160},{160,192},{192,224},{224... | collective-permute-start | bytes 18440 | tf_op jit(solution)/shard_map/ppermute | solution.py:23
  192.4 1.3 collective-permute-start.9
  193.8 3.3 %collective-permute-done.9 = f32[2,12,1,2,32]{4,3,2,0,1:T(2,128)S(1)} collective-permute-done((f32[2,12,1,2,32]{4,3,2,0,1:T(2,128)S(1)}, f32[2,12,1,2,32]{4,3,2,0,1:T(2,128)S(1)}, u32[]{:S(2)}, u32[]{:S(2)}) %collective-permute-start.9) | collective-permute-done | bytes 6176 | tf_op jit(solution)/shard_map/ppermute | solution.py:24
  197.1 0.1 fusion.22
  197.2 5.1 %collective-permute-start.10 = (f32[2,12,4,1,32]{4,3,2,0,1:T(1,128)S(1)}, f32[2,12,4,1,32]{4,3,2,0,1:T(1,128)S(1)}, u32[]{:S(2)}, u32[]{:S(2)}) collective-permute-start(f32[2,12,4,1,32]{4,3,2,0,1:T(1,128)S(1)} %get-tuple-element.30), channel_id=1, source_target_pairs={{0,1},{1,2},{2,3},{3,4},{4,5},{5,6},{6,7},{7,8},{8,9},{9,10},{10,1... | collective-permute-start | bytes 36872 | tf_op jit(solution)/shard_map/ppermute | solution.py:23
  202.2 2.1 collective-permute-start.11
  204.4 1.1 collective-permute-done.7
  205.5 2.9 %pad_maximum_fusion.1 = bf16[2,4,4,32,1536]{4,3,2,1,0:T(8,128)(2,1)} fusion(bf16[2,4,1,32,1536]{4,3,2,1,0:T(8,128)(2,1)} %collective-permute-done.7, bf16[2,1,2,32,1536]{4,3,2,1,0:T(8,128)(2,1)S(1)} %collective-permute-done.5, bf16[2,2,2,32,1536]{4,3,2,1,0:T(8,128)(2,1)S(1)} %get-tuple-element.16, bf16[2,1,2,32,1536]{4,3,2,1,0:T(8,128)(2,1)S(1)} %collective-permute-done.4, ...), kind=kLoop, calls=%fused_computation.1 | loop fusion | flops 6291456 | bytes 6291456 | tf_op jit(solution)/shard_map/concatenate | solution.py:25
  208.4 0.2 pad_maximum_fusion.5
  208.5 0.2 reshape.496
  208.7 0.7 copy.46.lse_ref.dot_ref
  209.4 7.4 %shard_map.103 = bf16[2,128,1536]{2,1,0:T(8,128)(2,1)} custom-call(s32[3,12]{1,0:T(4,128)} %pad_add_fusion.1.reach_ref, bf16[4,128,1536]{2,1,0:T(8,128)(2,1)} %bitcast.40, bf16[4,128,1536]{2,1,0:T(8,128)(2,1)} %bitcast.41, bf16[2,512,1536]{2,1,0:T(8,128)(2,1)} %bitcast.42, bf16[2,512,1536]{2,1,0:T(8,128)(2,1)} %bitcast.43, ...), custom_call_target="tpu_custom_call" | custom-call | tf_op jit(solution)/shard_map/pallas_call | solution.py:181
  216.8 2.8 %copy.39 = bf16[2,2,2,32,1536]{4,2,1,0,3:T(2,128)(2,1)} copy(bf16[2,2,2,32,1536]{4,3,2,1,0:T(8,128)(2,1)} %bitcast.47) | data formatting | bytes 1572864 | tf_op jit(solution)/shard_map/reshape | solution.py:171
  219.6 13.6 %all-to-all-start.2 = ((bf16[2,2,2,32,1536]{4,2,1,0,3:T(2,128)(2,1)}), bf16[2,2,2,32,1536]{4,2,1,0,3:T(2,128)(2,1)S(1)}, u32[]{:S(2)}, u32[]{:S(2)}) async-start(bf16[2,2,2,32,1536]{4,2,1,0,3:T(2,128)(2,1)} %copy.39), calls=%async_computation.2 | async-start | bytes 1572864 | tf_op jit(solution)/shard_map/all_to_all | solution.py:172
  233.2 0.5 fusion.20
  233.8 0.3 copy.36
  234.1 0.8 copy.42
  234.9 0.3 copy.37
  235.2 0.8 copy.43
  236.0 41.9 %all-to-all-done.2 = bf16[2,2,2,32,1536]{4,2,1,0,3:T(2,128)(2,1)S(1)} async-done(((bf16[2,2,2,32,1536]{4,2,1,0,3:T(2,128)(2,1)}), bf16[2,2,2,32,1536]{4,2,1,0,3:T(2,128)(2,1)S(1)}, u32[]{:S(2)}, u32[]{:S(2)}) %all-to-all-start.2) | async-done | bytes 786464 | tf_op jit(solution)/shard_map/all_to_all | solution.py:172
  277.9 0.5 fusion.18
  278.4 0.3 copy.40
  278.7 0.8 copy.44
  279.5 0.3 copy.41
  279.8 0.8 copy.45
  (28 shorter events, 0.2 us)
Async XLA Ops:
  0.6 2.0 copy-start.2
  0.6 2.0 copy-start.1
  6.7 98.3 %all-to-all-start = ((bf16[4,2,64,1,1536]{4,1,3,0,2:T(2,128)(2,1)}), bf16[4,2,64,1,1536]{4,1,3,0,2:T(2,128)(2,1)S(1)}, u32[]{:S(2)}, u32[]{:S(2)}) async-start(bf16[4,2,64,1,1536]{4,1,3,0,2:T(2,128)(2,1)} %pad_maximum_fusion.2), calls=%async_computation | async-start | bytes 3145728 | tf_op jit(solution)/shard_map/all_to_all | solution.py:123
  105.9 1.2 copy-start
  107.1 11.1 %collective-permute-start = (bf16[2,1,2,32,1536]{4,3,2,1,0:T(8,128)(2,1)S(1)}, bf16[2,1,2,32,1536]{4,3,2,1,0:T(8,128)(2,1)S(1)}, u32[]{:S(2)}, u32[]{:S(2)}) collective-permute-start(bf16[2,1,2,32,1536]{4,3,2,1,0:T(8,128)(2,1)S(1)} %get-tuple-element.28), channel_id=1, source_target_pairs={{0,32},{32,64},{64,96},{96,128},{128,160},{160,192},{192,224},{224... | collective-permute-start | bytes 1179656 | tf_op jit(solution)/shard_map/ppermute | solution.py:23
  110.4 11.6 %collective-permute-start.1 = (bf16[2,1,2,32,1536]{4,3,2,1,0:T(8,128)(2,1)S(1)}, bf16[2,1,2,32,1536]{4,3,2,1,0:T(8,128)(2,1)S(1)}, u32[]{:S(2)}, u32[]{:S(2)}) collective-permute-start(bf16[2,1,2,32,1536]{4,3,2,1,0:T(8,128)(2,1)S(1)} %get-tuple-element.29), channel_id=1, source_target_pairs={{32,0},{64,32},{96,64},{128,96},{160,128},{192,160},{224,192},{256... | collective-permute-start | bytes 1179656 | tf_op jit(solution)/shard_map/ppermute | solution.py:24
  122.2 5.2 %copy-start.3 = (s32[12]{0:T(128)S(1)}, s32[12]{0:T(128)}, u32[]{:S(2)}) copy-start(s32[12]{0:T(128)} %param.13) | copy-start | bytes 148
  122.2 5.2 %copy-start.4 = (s32[12]{0:T(128)S(1)}, s32[12]{0:T(128)}, u32[]{:S(2)}) copy-start(s32[12]{0:T(128)} %param.12) | copy-start | bytes 148
  122.2 5.2 %copy-start.5 = (s32[12]{0:T(128)S(1)}, s32[12]{0:T(128)}, u32[]{:S(2)}) copy-start(s32[12]{0:T(128)} %param.11) | copy-start | bytes 148
  122.3 11.0 %collective-permute-start.2 = (bf16[2,4,1,32,1536]{4,3,2,1,0:T(8,128)(2,1)S(1)}, bf16[2,4,1,32,1536]{4,3,2,1,0:T(8,128)(2,1)S(1)}, u32[]{:S(2)}, u32[]{:S(2)}) collective-permute-start(bf16[2,4,1,32,1536]{4,3,2,1,0:T(8,128)(2,1)S(1)} %get-tuple-element.18), channel_id=1, source_target_pairs={{0,1},{1,2},{2,3},{3,4},{4,5},{5,6},{6,7},{7,8},{8,9},{9,10},{10,1... | collective-permute-start | bytes 2359304 | tf_op jit(solution)/shard_map/ppermute | solution.py:23
  124.4 13.3 %collective-permute-start.3 = (bf16[2,4,1,32,1536]{4,3,2,1,0:T(8,128)(2,1)S(1)}, bf16[2,4,1,32,1536]{4,3,2,1,0:T(8,128)(2,1)S(1)}, u32[]{:S(2)}, u32[]{:S(2)}) collective-permute-start(bf16[2,4,1,32,1536]{4,3,2,1,0:T(8,128)(2,1)S(1)} %get-tuple-element.19), channel_id=1, source_target_pairs={{1,0},{2,1},{3,2},{4,3},{5,4},{6,5},{7,6},{8,7},{9,8},{10,9},{11,1... | collective-permute-start | bytes 2359304 | tf_op jit(solution)/shard_map/ppermute | solution.py:24
  153.3 66.3 %all-to-all-start.1 = ((bf16[2,2,2,32,1536]{4,2,1,0,3:T(2,128)(2,1)}), bf16[2,2,2,32,1536]{4,2,1,0,3:T(2,128)(2,1)S(1)}, u32[]{:S(2)}, u32[]{:S(2)}) async-start(bf16[2,2,2,32,1536]{4,2,1,0,3:T(2,128)(2,1)} %copy.35), calls=%async_computation.1 | async-start | bytes 1572864 | tf_op jit(solution)/shard_map/all_to_all | solution.py:172
  160.7 11.5 %collective-permute-start.4 = (bf16[2,1,2,32,1536]{4,3,2,1,0:T(8,128)(2,1)S(1)}, bf16[2,1,2,32,1536]{4,3,2,1,0:T(8,128)(2,1)S(1)}, u32[]{:S(2)}, u32[]{:S(2)}) collective-permute-start(bf16[2,1,2,32,1536]{4,3,2,1,0:T(8,128)(2,1)S(1)} %get-tuple-element.24), channel_id=1, source_target_pairs={{0,32},{32,64},{64,96},{96,128},{128,160},{160,192},{192,224},{224... | collective-permute-start | bytes 1179656 | tf_op jit(solution)/shard_map/ppermute | solution.py:23
  163.9 13.3 %collective-permute-start.5 = (bf16[2,1,2,32,1536]{4,3,2,1,0:T(8,128)(2,1)S(1)}, bf16[2,1,2,32,1536]{4,3,2,1,0:T(8,128)(2,1)S(1)}, u32[]{:S(2)}, u32[]{:S(2)}) collective-permute-start(bf16[2,1,2,32,1536]{4,3,2,1,0:T(8,128)(2,1)S(1)} %get-tuple-element.25), channel_id=1, source_target_pairs={{32,0},{64,32},{96,64},{128,96},{160,128},{192,160},{224,192},{256... | collective-permute-start | bytes 1179656 | tf_op jit(solution)/shard_map/ppermute | solution.py:24
  178.6 25.7 %collective-permute-start.6 = (bf16[2,4,1,32,1536]{4,3,2,1,0:T(8,128)(2,1)}, bf16[2,4,1,32,1536]{4,3,2,1,0:T(8,128)(2,1)S(1)}, u32[]{:S(2)}, u32[]{:S(2)}) collective-permute-start(bf16[2,4,1,32,1536]{4,3,2,1,0:T(8,128)(2,1)} %get-tuple-element.14), channel_id=1, source_target_pairs={{0,1},{1,2},{2,3},{3,4},{4,5},{5,6},{6,7},{7,8},{8,9},{9,10},{10,1... | collective-permute-start | bytes 2359304 | tf_op jit(solution)/shard_map/ppermute | solution.py:23
  182.9 22.6 %collective-permute-start.7 = (bf16[2,4,1,32,1536]{4,3,2,1,0:T(8,128)(2,1)}, bf16[2,4,1,32,1536]{4,3,2,1,0:T(8,128)(2,1)}, u32[]{:S(2)}, u32[]{:S(2)}) collective-permute-start(bf16[2,4,1,32,1536]{4,3,2,1,0:T(8,128)(2,1)} %get-tuple-element.15), channel_id=1, source_target_pairs={{1,0},{2,1},{3,2},{4,3},{5,4},{6,5},{7,6},{8,7},{9,8},{10,9},{11,1... | collective-permute-start | bytes 2359304 | tf_op jit(solution)/shard_map/ppermute | solution.py:24
  187.9 5.9 %collective-permute-start.8 = (f32[2,12,1,2,32]{4,3,2,0,1:T(2,128)S(1)}, f32[2,12,1,2,32]{4,3,2,0,1:T(2,128)S(1)}, u32[]{:S(2)}, u32[]{:S(2)}) collective-permute-start(f32[2,12,1,2,32]{4,3,2,0,1:T(2,128)S(1)} %get-tuple-element.32), channel_id=1, source_target_pairs={{0,32},{32,64},{64,96},{96,128},{128,160},{160,192},{192,224},{224... | collective-permute-start | bytes 18440 | tf_op jit(solution)/shard_map/ppermute | solution.py:23
  192.4 4.6 %collective-permute-start.9 = (f32[2,12,1,2,32]{4,3,2,0,1:T(2,128)S(1)}, f32[2,12,1,2,32]{4,3,2,0,1:T(2,128)S(1)}, u32[]{:S(2)}, u32[]{:S(2)}) collective-permute-start(f32[2,12,1,2,32]{4,3,2,0,1:T(2,128)S(1)} %get-tuple-element.33), channel_id=1, source_target_pairs={{32,0},{64,32},{96,64},{128,96},{160,128},{192,160},{224,192},{256... | collective-permute-start | bytes 18440 | tf_op jit(solution)/shard_map/ppermute | solution.py:24
  197.2 11.2 %collective-permute-start.10 = (f32[2,12,4,1,32]{4,3,2,0,1:T(1,128)S(1)}, f32[2,12,4,1,32]{4,3,2,0,1:T(1,128)S(1)}, u32[]{:S(2)}, u32[]{:S(2)}) collective-permute-start(f32[2,12,4,1,32]{4,3,2,0,1:T(1,128)S(1)} %get-tuple-element.30), channel_id=1, source_target_pairs={{0,1},{1,2},{2,3},{3,4},{4,5},{5,6},{6,7},{7,8},{8,9},{9,10},{10,1... | collective-permute-start | bytes 36872 | tf_op jit(solution)/shard_map/ppermute | solution.py:23
  202.2 6.1 %collective-permute-start.11 = (f32[2,12,4,1,32]{4,3,2,0,1:T(1,128)S(1)}, f32[2,12,4,1,32]{4,3,2,0,1:T(1,128)S(1)}, u32[]{:S(2)}, u32[]{:S(2)}) collective-permute-start(f32[2,12,4,1,32]{4,3,2,0,1:T(1,128)S(1)} %get-tuple-element.31), channel_id=1, source_target_pairs={{1,0},{2,1},{3,2},{4,3},{5,4},{6,5},{7,6},{8,7},{9,8},{10,9},{11,1... | collective-permute-start | bytes 36872 | tf_op jit(solution)/shard_map/ppermute | solution.py:24
  219.6 58.2 %all-to-all-start.2 = ((bf16[2,2,2,32,1536]{4,2,1,0,3:T(2,128)(2,1)}), bf16[2,2,2,32,1536]{4,2,1,0,3:T(2,128)(2,1)S(1)}, u32[]{:S(2)}, u32[]{:S(2)}) async-start(bf16[2,2,2,32,1536]{4,2,1,0,3:T(2,128)(2,1)} %copy.39), calls=%async_computation.2 | async-start | bytes 1572864 | tf_op jit(solution)/shard_map/all_to_all | solution.py:172
